TPU v7x, 32 devices: a whole 2x2x4 slice. The times are simulated.
32 devices in a mesh: grp: 4 (over y, x), feat: 8 (over z, core).
Axes of the slice: x: 2, y: 2, z: 4, core: 2. Of those that a mesh axis runs over, the one named last changes fastest.
Arguments:
- inputs: bfloat16 [32, 32, 2048], P(None, 'feat'), may hold values from -8 to 8
- labels: int32 [32], replicated, may hold values from 0 to 32767
- phases: float32 [32, 32, 1024], P('feat'), may hold values from -3.140625 to 3.140625
- sign_bits: int32 [8, 32, 32, 1024], P('grp', 'feat'), may hold values from 0 to 1
- moment_first: float32 [32, 32, 1024], P('feat', 'grp'), may hold values from -1.2 to 1.2
- moment_second: float32 [32, 32, 1024], P('feat', 'grp'), may hold values from 0.001 to 0.03
Outputs:
- estimate: float32 [32, 32, 1024], P('feat', 'grp')
- moment_first_new: float32 [32, 32, 1024], P('feat', 'grp')
- moment_second_new: float32 [32, 32, 1024], P('feat', 'grp')
- phases_next: float32 [32, 32, 1024], P('feat')
All inputs are finite; a program needn't handle non-finite values.
Results may differ from a plain program's by a relative error of at most 0.00135.
The roundings to bfloat16 on the way count: a program that leaves them out, or rounds other values in their place, can miss the bound.
Values may be sent and summed in bfloat16 or wider, within the bound.
No kernel may reach another device: no remote copies, remote signals or barrier semaphores. Data moves between devices by JAX's collectives and lax.ppermute only.
A program may use at most 128 MiB of HBM per device.

v0:
```python
import math

import jax
import jax.numpy as jnp
from jax import lax
from jax.sharding import PartitionSpec as P

ADAM_STEP = 10


logit_scale = 3.0
perturb_size = 0.2
learn_rate = 0.1
beta_first = 0.9
beta_second = 0.999
adam_eps = 1e-08


def tables(block_len):
    counter = jnp.arange(block_len, dtype=jnp.int32)
    product = counter[:, None] * counter[None, :] % block_len
    angles = product.astype(jnp.float32) * (2.0 * math.pi / block_len)
    factor = 1.0 / math.sqrt(block_len)
    cosine = (jnp.cos(angles) * factor).astype(jnp.bfloat16)
    sine_part = (jnp.sin(angles) * factor).astype(jnp.bfloat16)
    forward = jnp.concatenate(
        [jnp.concatenate([cosine, -sine_part], 1), jnp.concatenate([sine_part, cosine], 1)], 0
    )
    inverse = jnp.concatenate(
        [jnp.concatenate([cosine, sine_part], 1), jnp.concatenate([-sine_part, cosine], 1)], 0
    )
    return (forward, inverse)


def transmit(phase_part, shift_part):
    senses = jnp.array([1.0, -1.0], jnp.float32)
    angles = (
        phase_part[None, None]
        + senses[None, :, None, None, None] * perturb_size * shift_part[:, None]
    )
    shape_now = angles.shape
    angles = angles.reshape(shape_now[0] * 2, shape_now[2], shape_now[3], shape_now[4])
    return (jnp.cos(angles).astype(jnp.bfloat16), jnp.sin(angles).astype(jnp.bfloat16))


def complex_matrix(real_part, imag_part):
    upper = jnp.stack([real_part, -imag_part], 1)
    lower = jnp.stack([imag_part, real_part], 1)
    return jnp.stack([upper, lower], 1)


def complex_mix(matrix, piece):
    return jnp.einsum("nocijk,rjck->nriok", matrix, piece, preferred_element_type=jnp.float32)


def body(inputs, labels, phases, sign_bits, moment_first, moment_second):
    row_count, owned_blocks, doubled = inputs.shape
    block_len = doubled // 2
    blocks = phases.shape[1]
    pairs_here = sign_bits.shape[0]
    total_pairs = pairs_here * lax.axis_size("grp")
    net_count = 2 * pairs_here
    mix_factor = 1.0 / math.sqrt(blocks)
    forward, inverse = tables(block_len)
    spectra = jnp.dot(
        inputs.reshape(row_count * owned_blocks, doubled),
        forward,
        preferred_element_type=jnp.float32,
    )
    spectra = spectra.astype(jnp.bfloat16).reshape(row_count, owned_blocks, doubled)
    shifts = 2.0 * sign_bits.astype(jnp.float32) - 1.0
    trans_real, trans_imag = transmit(phases, shifts)
    trans_matrix = complex_matrix(trans_real, trans_imag)
    shard_piece = lax.all_gather(spectra, "feat", axis=1, tiled=True)
    piece_count = shard_piece.shape[1]
    split_piece = shard_piece.reshape(row_count, piece_count, 2, block_len)
    summed = complex_mix(trans_matrix, split_piece)
    mixed = (
        (summed * mix_factor)
        .astype(jnp.bfloat16)
        .reshape(net_count, row_count, owned_blocks, doubled)
    )
    output_field = jnp.dot(
        mixed.reshape(net_count * row_count * owned_blocks, doubled),
        inverse,
        preferred_element_type=jnp.float32,
    )
    output_field = output_field.reshape(net_count, row_count, owned_blocks, doubled)
    intensity = output_field[..., :block_len] ** 2 + output_field[..., block_len:] ** 2
    logits = logit_scale * intensity.reshape(net_count, row_count, owned_blocks * block_len)
    first_class = lax.axis_index("feat") * (owned_blocks * block_len)
    classes = first_class + jnp.arange(owned_blocks * block_len, dtype=jnp.int32)
    matches = classes[None, None, :] == labels[None, :, None]
    local_top = jnp.max(logits, axis=2)
    local_label = jnp.sum(jnp.where(matches, logits, 0.0), axis=2)
    row_top = lax.pmax(local_top, "feat")
    local_total = jnp.sum(jnp.exp(logits - row_top[..., None]), axis=2)
    row_total, row_label = lax.psum((local_total, local_label), "feat")
    losses = jnp.mean(row_top + jnp.log(row_total) - row_label, axis=1).reshape(pairs_here, 2)
    differences = (losses[:, 0] - losses[:, 1]) / (2.0 * perturb_size)
    group_term = (
        jnp.tensordot(differences, shifts, 1, precision=lax.Precision.HIGHEST) / total_pairs
    )
    estimate = lax.psum_scatter(group_term, "grp", scatter_dimension=1, tiled=True)
    own_columns = estimate.shape[1]
    first_column = lax.axis_index("grp") * own_columns
    own_phases = lax.dynamic_slice_in_dim(phases, first_column, own_columns, 1)
    first_new = beta_first * moment_first + (1.0 - beta_first) * estimate
    second_new = beta_second * moment_second + (1.0 - beta_second) * estimate * estimate
    first_bias = 1.0 - beta_first**ADAM_STEP
    second_bias = 1.0 - beta_second**ADAM_STEP
    own_next = own_phases - learn_rate * (first_new / first_bias) / (
        jnp.sqrt(second_new / second_bias) + adam_eps
    )
    phases_next = lax.all_gather(own_next, "grp", axis=1, tiled=True)
    return (estimate, first_new, second_new, phases_next)


def solution(mesh):
    return jax.shard_map(
        body,
        mesh=mesh,
        in_specs=(
            P(None, "feat", None),
            P(),
            P("feat", None, None),
            P("grp", "feat", None, None),
            P("feat", "grp", None),
            P("feat", "grp", None),
        ),
        out_specs=(
            P("feat", "grp", None),
            P("feat", "grp", None),
            P("feat", "grp", None),
            P("feat", None, None),
        ),
        check_vma=False,
    )
```

profile of v0, /device:TPU:0, one launch (start us, length us, event | category | flops | bytes accessed | tf_op | source)
XLA Modules:
  0.0 269.0 jit_solution(7880083783832270591)
XLA Ops:
  7.2 0.0 copy-start.3
  7.2 0.0 all-gather.2.cloned.1.call-start
  7.2 17.9 %multiply_convert_fusion = (bf16[1024,1024]{1,0:T(8,128)(2,1)S(1)}, bf16[1024,1024]{1,0:T(8,128)(2,1)}) fusion(), kind=kLoop, calls=%fused_computation.24 | loop fusion | flops 18874368 | bytes 4194304 | tf_op jit(solution)/shard_map/convert_element_type | solution.py:25
  25.1 16.5 %fusion.33 = bf16[1024,1024]{1,0:T(8,128)(2,1)} fusion(), kind=kLoop, calls=%fused_computation.45 | loop fusion | flops 19922944 | bytes 2097152 | tf_op jit(solution)/shard_map/neg | solution.py:27
  41.6 0.0 copy-done.3
  41.6 0.1 reshape.112
  41.7 0.0 copy-done.2
  41.8 0.0 copy-start.7
  41.8 12.8 %fusion.26 = bf16[128,2048]{1,0:T(8,128)(2,1)S(1)} fusion(bf16[128,2048]{1,0:T(8,128)(2,1)S(1)} %reshape.112, bf16[1024,1024]{1,0:T(8,128)(2,1)} %get-tuple-element.16, bf16[1024,1024]{1,0:T(8,128)(2,1)S(1)} %get-tuple-element.15, bf16[1024,1024]{1,0:T(8,128)(2,1)} %fusion.33), kind=kOutput, calls=%fused_computation.30 | convolution fusion | flops 1107558400 | bytes 7340032 | tf_op jit(solution)/shard_map/dot_general | solution.py:65
  54.6 0.0 copy-start.1
  54.6 0.2 reshape.113
  54.8 1.1 copy.26
  55.9 0.0 all-gather.2.cloned.1.call-update
  55.9 0.2 reduce-scatter.2.cloned.1.call-start
  56.1 0.1 mul.198
  56.2 1.4 multiply_add_fusion.1
  57.6 0.2 mul.202
  57.8 0.0 copy-done.1
  57.8 7.1 %cosine_convert_fusion = bf16[4,1,4,32,1024]{4,3,2,1,0:T(8,128)(2,1)S(1)} fusion(f32[4,1,4,32,1024]{4,3,2,1,0:T(8,128)S(1)} %bitcast.34, f32[4]{0:T(128)S(1)} %mul.198, f32[4,32,1024]{2,1,0:T(8,128)S(1)} %copy-done.1), kind=kLoop, calls=%fused_computation.40 | loop fusion | flops 1572864 | bytes 3670032 | tf_op jit(solution)/shard_map/convert_element_type | solution.py:43
  65.0 7.3 %fusion.41 = (bf16[4,1,4,32,1024]{4,3,2,1,0:T(8,128)(2,1)S(1)}, bf16[4,1,4,32,1024]{4,3,2,1,0:T(8,128)(2,1)S(1)}) fusion(f32[4,1,4,32,1024]{4,3,2,1,0:T(8,128)S(1)} %bitcast.35, f32[4]{0:T(128)S(1)} %mul.198, f32[4,32,1024]{2,1,0:T(8,128)S(1)} %copy-done.1), kind=kLoop, calls=%fused_computation.61 | loop fusion | flops 3145728 | bytes 4718608 | tf_op jit(solution)/shard_map/neg | solution.py:47
  72.2 1.7 pad_maximum_fusion.5
  73.9 13.4 %copy.28 = bf16[4,2,4,32,1024]{3,2,1,0,4:T(4,128)(2,1)} copy(bf16[4,2,4,32,1024]{4,3,2,1,0:T(8,128)(2,1)} %get-tuple-element.13) | data formatting | bytes 4194304 | tf_op jit(solution)/shard_map/stack | solution.py:47
  87.3 10.7 %copy.29 = bf16[4,2,4,32,1024]{3,2,1,0,4:T(4,128)(2,1)} copy(bf16[4,2,4,32,1024]{4,3,2,1,0:T(8,128)(2,1)S(1)} %get-tuple-element.14) | data formatting | bytes 4194304 | tf_op jit(solution)/shard_map/stack | solution.py:48
  98.0 0.1 broadcast_compare_fusion
  98.1 7.6 %all-gather.2.cloned.1.call-done = bf16[32,32,2048]{2,0,1:T(8,128)(2,1)} async-done(((bf16[32,4,2048]{2,0,1:T(8,128)(2,1)}), bf16[32,32,2048]{2,0,1:T(8,128)(2,1)}) %all-gather.2.cloned.1.call-update) | async-done | bytes 4194320 | tf_op jit(solution)/shard_map/all_gather | solution.py:74
  105.8 7.8 %reshape.120 = bf16[32,32,2,1024]{3,2,0,1:T(2,128)(2,1)} reshape(bf16[32,32,2048]{2,0,1:T(8,128)(2,1)} %all-gather.2.cloned.1.call-done) | data formatting | bytes 8388608 | tf_op jit(solution)/shard_map/reshape | solution.py:76
  113.6 27.0 %copy.32 = bf16[32,32,2,1024,1,1]{1,0,2,5,4,3:T(8,128)(2,1)} copy(bf16[32,32,2,1024,1,1]{3,2,0,1,5,4:T(2,128)(2,1)} %bitcast.36) | data formatting | bytes 8388608 | tf_op jit(solution)/shard_map/reshape | solution.py:76
  140.6 20.7 %fusion.10 = bf16[4,32,4,2,1024]{1,2,3,0,4:T(4,128)(2,1)} fusion(bf16[32,32,2,1024,1,1]{1,0,2,5,4,3:T(8,128)(2,1)} %copy.32, bf16[4,1,2,4,32,1024]{4,3,2,1,0,5:T(4,128)(2,1)} %bitcast.38, bf16[4,1,2,4,32,1024]{4,3,2,1,0,5:T(4,128)(2,1)} %bitcast.37), kind=kOutput, calls=%fused_computation.14 | convolution fusion | flops 144703488 | bytes 10485760 | tf_op jit(solution)/shard_map/nocijk,rjck->nriok/dot_general | solution.py:53
  161.3 12.5 %copy.31 = bf16[4,32,4,2,1024]{4,3,1,2,0:T(2,128)(2,1)S(1)} copy(bf16[4,32,4,2,1024]{1,2,3,0,4:T(4,128)(2,1)} %fusion.10) | data formatting | bytes 4194304 | tf_op jit(solution)/shard_map/convert_element_type | solution.py:80
  173.8 2.8 %dot_general.16 = bf16[4,32,4,2048]{3,1,2,0:T(8,128)(2,1)} reshape(bf16[4,32,4,2,1024]{4,3,1,2,0:T(2,128)(2,1)S(1)} %copy.31) | data formatting | bytes 4194304 | tf_op jit(solution)/shard_map/dot_general | solution.py:83
  176.6 11.0 %fusion.8 = f32[4,32,4,2048]{3,1,2,0:T(8,128)S(1)} fusion(bf16[4,32,4,2048]{3,1,2,0:T(8,128)(2,1)} %dot_general.16, bf16[1024,1024]{1,0:T(8,128)(2,1)} %get-tuple-element.16, bf16[1024,1024]{1,0:T(8,128)(2,1)} %fusion.33, bf16[1024,1024]{1,0:T(8,128)(2,1)} %copy-done.2), kind=kOutput, calls=%fused_computation.13 | convolution fusion | flops 4328521728 | bytes 12582912 | tf_op jit(solution)/shard_map/dot_general | solution.py:83
  187.6 0.0 copy-start
  187.6 1.9 copy-done
  189.5 0.4 fusion.39
  190.0 14.8 %pmax.7 = f32[4,32]{1,0:T(4,128)S(1)} all-reduce(f32[4,32]{1,0:T(4,128)S(1)} %fusion.39), channel_id=1, replica_groups=mesh['grp'=4,'feat'=8] {'feat'}, use_global_device_ids=true, to_apply=%region_1.2 | all-reduce | flops 128 | bytes 1024 | tf_op jit(solution)/shard_map/pmax | solution.py:96
  204.7 3.2 %exponential_reduce_fusion = (f32[4,32]{1,0:T(4,128)S(1)}, f32[4,32]{1,0:T(4,128)S(1)}) fusion(f32[4,32]{1,0:T(4,128)S(1)} %pmax.7, f32[4,32,4,2048]{3,1,2,0:T(8,128)} %copy-done, pred[32,4,1024]{2,0,1:T(8,128)(4,1)S(1)} %broadcast_compare_fusion), kind=kLoop, calls=%fused_computation.38 | loop fusion | flops 4194048 | bytes 4326912 | tf_op jit(solution)/shard_map/reduce_sum | solution.py:97
  208.0 13.6 %all-reduce = (f32[4,32]{1,0:T(4,128)S(1)}, f32[4,32]{1,0:T(4,128)S(1)}) all-reduce(f32[4,32]{1,0:T(4,128)S(1)} %get-tuple-element.5, f32[4,32]{1,0:T(4,128)S(1)} %get-tuple-element.4), channel_id=1, replica_groups=mesh['grp'=4,'feat'=8] {'feat'}, use_global_device_ids=true, to_apply=%region_5.6 | all-reduce | flops 256 | bytes 2048 | tf_op jit(solution)/shard_map/psum | solution.py:98
  221.5 0.1 subtract_reduce_fusion
  221.7 0.1 div.28
  221.8 0.2 multiply_reduce_fusion
  221.9 3.8 %fusion.31 = f32[1,4,32,1024]{3,0,2,1:T(1,128)S(1)} fusion(f32[2,4,32,1024]{3,2,1,0:T(8,128)S(1)} %multiply_add_fusion.1, f32[2]{0:T(128)S(1)} %multiply_reduce_fusion), kind=kOutput, calls=%fused_computation.43 | convolution fusion | flops 3145728 | bytes 1572872 | tf_op jit(solution)/shard_map/dot_general | solution.py:102
  225.7 0.9 bitcast_multiply_fusion.1
  226.6 0.0 reduce-scatter.2.cloned.1.call-update
  226.7 23.0 %reduce-scatter.2.cloned.1.call-done = f32[4,8,1024]{2,1,0:T(8,128)} async-done(((f32[4,32,1024]{2,1,0:T(8,128)}), f32[4,8,1024]{2,1,0:T(8,128)}) %reduce-scatter.2.cloned.1.call-update) | async-done | bytes 131088 | tf_op jit(solution)/shard_map/reduce_scatter | solution.py:104
  249.6 0.0 copy-done.4
  249.6 1.7 divide_subtract_fusion
  251.4 10.0 %all_gather.7 = f32[4,32,1024]{2,1,0:T(8,128)S(1)} all-gather(f32[4,8,1024]{2,1,0:T(8,128)S(1)} %get-tuple-element.8), channel_id=1, replica_groups=mesh['grp'=4,'feat'=8] {'grp'}, dimensions={1}, use_global_device_ids=true | all-gather | bytes 655360 | tf_op jit(solution)/shard_map/all_gather | solution.py:115
  261.4 0.8 copy.46
  (10 shorter events, 0.0 us)
Async XLA Ops:
  7.2 34.5 %copy-start.3 = (bf16[32,4,2048]{2,1,0:T(4,128)(2,1)S(1)}, bf16[32,4,2048]{2,1,0:T(4,128)(2,1)}, u32[]{:S(2)}) copy-start(bf16[32,4,2048]{2,1,0:T(4,128)(2,1)} %param.7) | copy-start | bytes 1572868
  7.2 98.6 %all-gather.2.cloned.1.call-start = ((), (), s32[]{:S(2)}) async-start(), calls=%async_computation.1 | async-start | bytes 4718592 | tf_op jit(solution)/shard_map/all_gather | solution.py:74
  25.1 16.7 %copy-start.2 = (bf16[1024,1024]{1,0:T(8,128)(2,1)}, bf16[1024,1024]{1,0:T(8,128)(2,1)S(1)}, u32[]{:S(2)}) copy-start(bf16[1024,1024]{1,0:T(8,128)(2,1)S(1)} %get-tuple-element.15) | copy-start | bytes 6291460
  41.8 14.4 %copy-start.7 = (f32[2]{0:T(128)S(1)}, f32[2]{0:T(128)}, u32[]{:S(2)}) copy-start(f32[2]{0:T(128)} %constant.83) | copy-start | bytes 28
  54.6 3.3 %copy-start.1 = (f32[4,32,1024]{2,1,0:T(8,128)S(1)}, f32[4,32,1024]{2,1,0:T(8,128)}, u32[]{:S(2)}) copy-start(f32[4,32,1024]{2,1,0:T(8,128)} %param.9) | copy-start | bytes 1572868
  55.9 193.8 %reduce-scatter.2.cloned.1.call-start = ((), (), s32[]{:S(2)}) async-start(), calls=%async_computation.2 | async-start | bytes 655360 | tf_op jit(solution)/shard_map/reduce_scatter | solution.py:104
  87.3 10.7 %copy-start.6 = (s32[32]{0:T(128)S(1)}, s32[32]{0:T(128)}, u32[]{:S(2)}) copy-start(s32[32]{0:T(128)} %param.8) | copy-start | bytes 388
  187.6 1.9 copy-start
  189.9 59.7 %copy-start.4 = (f32[4,8,1024]{2,1,0:T(8,128)S(1)}, f32[4,8,1024]{2,1,0:T(8,128)}, u32[]{:S(2)}) copy-start(f32[4,8,1024]{2,1,0:T(8,128)} %param.12) | copy-start | bytes 393220
  190.0 59.7 %copy-start.5 = (f32[4,8,1024]{2,1,0:T(8,128)S(1)}, f32[4,8,1024]{2,1,0:T(8,128)}, u32[]{:S(2)}) copy-start(f32[4,8,1024]{2,1,0:T(8,128)} %param.11) | copy-start | bytes 393220
Sparse Core Ops, SparseCore 0:
  56.0 49.7 all-gather.1
  226.8 22.8 reduce-scatter.1
where the time goes:
time: 271 us; the launch traced here: 269 us
  local copies, waits for them, and re-layouts  78.7 us (29%)
  other arithmetic  58.6 us (22%)
  matrix products  48.2 us (18%)
  blocking collectives  38.3 us (14%)
  waiting for transfers between devices  30.7 us (11%)
  between operations  14.2 us (5%)
    reshape x2, local copies, waits for them, and re-layouts, body(): split_piece = shard_piece.reshape(row_count, piece_count, 2, block_len)  34.8 us
    reduce_scatter x1, waiting for transfers between devices, body(): lax.psum_scatter(group_term, 'grp', scatter_dimension=1, tiled=True)  23 us
    dot_general x1, matrix products, complex_mix(): jnp.einsum('nocijk,rjck->nriok', matrix, piece, preferred_element_type=jn...  20.7 us
    convert_element_type x1, other arithmetic, tables(): sine_part = (jnp.sin(angles) * factor).astype(jnp.bfloat16)  17.9 us
    neg x1, other arithmetic, tables(): -sine_part  16.5 us
    pmax x1, blocking collectives, body(): row_top = lax.pmax(local_top, 'feat')  14.8 us
    psum x1, blocking collectives, body(): row_total, row_label = lax.psum((local_total, local_label), 'feat')  13.6 us
    another operation x1, local copies, waits for them, and re-layouts, complex_matrix(): upper = jnp.stack([real_part, -imag_part], 1)  13.4 us
  transfers between devices with their start and end apart: 2, of which 2 were waited for; matrix products, arithmetic and copies ran while one was open for 16% of the time, Pallas kernels for 0%

commit v1 on v0

v1 whole, which is shorter than its diff:
```python
import functools
import math

import jax
import jax.numpy as jnp
from jax import lax
from jax.experimental import pallas as pl
from jax.experimental.pallas import tpu as pltpu
from jax.sharding import PartitionSpec as P

ADAM_STEP = 10


logit_scale = 3.0
perturb_size = 0.2
learn_rate = 0.1
beta_first = 0.9
beta_second = 0.999
adam_eps = 1e-08


def tables(block_len):
    low_len = 1 << (int(math.log2(block_len)) // 2)
    high_len = block_len // low_len
    counter = jnp.arange(block_len, dtype=jnp.int32)
    high = jnp.arange(high_len, dtype=jnp.int32) * low_len
    low = jnp.arange(low_len, dtype=jnp.int32)
    step = 2.0 * math.pi / block_len
    high_angle = (high[:, None] * counter[None, :] % block_len).astype(jnp.float32) * step
    low_angle = (low[:, None] * counter[None, :] % block_len).astype(jnp.float32) * step
    high_cos, high_sin = jnp.cos(high_angle), jnp.sin(high_angle)
    low_cos, low_sin = jnp.cos(low_angle), jnp.sin(low_angle)
    factor = 1.0 / math.sqrt(block_len)
    cosine = high_cos[:, None] * low_cos[None] - high_sin[:, None] * low_sin[None]
    sine_part = high_sin[:, None] * low_cos[None] + high_cos[:, None] * low_sin[None]
    cosine = (cosine * factor).astype(jnp.bfloat16).reshape(block_len, block_len)
    sine_part = (sine_part * factor).astype(jnp.bfloat16).reshape(block_len, block_len)
    return cosine, sine_part


def to_bf16(values):
    return lax.reduce_precision(values, exponent_bits=8, mantissa_bits=7)


def mix_kernel(s_ref, tr_ref, ti_ref, o_ref, s32_ref, *, blocks, block_len, rows, chunk, factor):
    @pl.when((pl.program_id(0) == 0) & (pl.program_id(1) == 0))
    def _():
        def convert(j, carry):
            s32_ref[j] = s_ref[j].astype(jnp.float32)
            return carry

        lax.fori_loop(0, blocks, convert, 0)

    for start in range(0, block_len, chunk):
        def step(j, carry):
            acc_real, acc_imag = carry
            t_real = tr_ref[0, 0, pl.ds(j, 1), pl.ds(start, chunk)]
            t_imag = ti_ref[0, 0, pl.ds(j, 1), pl.ds(start, chunk)]
            s_real = s32_ref[j, :, pl.ds(start, chunk)]
            s_imag = s32_ref[j, :, pl.ds(block_len + start, chunk)]
            acc_real = acc_real + (t_real * s_real - t_imag * s_imag)
            acc_imag = acc_imag + (t_real * s_imag + t_imag * s_real)
            return acc_real, acc_imag

        zero = jnp.zeros((rows, chunk), jnp.float32)
        acc_real, acc_imag = lax.fori_loop(0, blocks, step, (zero, zero), unroll=4)
        o_ref[0, 0, :, pl.ds(start, chunk)] = (acc_real * factor).astype(o_ref.dtype)
        o_ref[0, 0, :, pl.ds(block_len + start, chunk)] = (acc_imag * factor).astype(o_ref.dtype)


def mix(spectra_all, t_real, t_imag):
    blocks, rows, doubled = spectra_all.shape
    block_len = doubled // 2
    nets, owned = t_real.shape[:2]
    kernel = functools.partial(
        mix_kernel,
        blocks=blocks,
        block_len=block_len,
        rows=rows,
        chunk=256,
        factor=1.0 / math.sqrt(blocks),
    )
    t_spec = pl.BlockSpec((1, 1, blocks, block_len), lambda n, i: (n, i, 0, 0))
    return pl.pallas_call(
        kernel,
        grid=(nets, owned),
        in_specs=[pl.BlockSpec((blocks, rows, doubled), lambda n, i: (0, 0, 0)), t_spec, t_spec],
        out_specs=pl.BlockSpec((1, 1, rows, doubled), lambda n, i: (n, i, 0, 0)),
        out_shape=jax.ShapeDtypeStruct((nets, owned, rows, doubled), jnp.bfloat16),
        scratch_shapes=[pltpu.VMEM((blocks, rows, doubled), jnp.float32)],
        compiler_params=pltpu.CompilerParams(
            dimension_semantics=("arbitrary", "arbitrary"), vmem_limit_bytes=48 * 1024 * 1024
        ),
    )(spectra_all, t_real, t_imag)


def body(inputs, labels, phases, sign_bits, moment_first, moment_second):
    row_count, owned_blocks, doubled = inputs.shape
    block_len = doubled // 2
    blocks = phases.shape[1]
    pairs_here = sign_bits.shape[0]
    group_count = lax.axis_size("grp")
    feat_count = lax.axis_size("feat")
    total_pairs = pairs_here * group_count
    net_count = 2 * pairs_here
    own_columns = blocks // group_count
    group_index = lax.axis_index("grp")
    feat_index = lax.axis_index("feat")

    directions = (2 * sign_bits - 1).astype(jnp.bfloat16)
    all_directions = lax.all_gather(directions, "grp", axis=0, tiled=True)
    all_first = lax.all_gather(moment_first, "grp", axis=1, tiled=True)
    all_second = lax.all_gather(moment_second, "grp", axis=1, tiled=True)

    cosine, sine_part = tables(block_len)
    local_in = jnp.transpose(inputs, (1, 0, 2)).reshape(owned_blocks * row_count, doubled)
    in_real = local_in[:, :block_len]
    in_imag = local_in[:, block_len:]
    f32 = jnp.float32
    spec_real = jnp.dot(in_real, cosine, preferred_element_type=f32) + jnp.dot(
        in_imag, sine_part, preferred_element_type=f32
    )
    spec_imag = jnp.dot(in_imag, cosine, preferred_element_type=f32) - jnp.dot(
        in_real, sine_part, preferred_element_type=f32
    )
    spectra = jnp.concatenate([spec_real, spec_imag], 1).astype(jnp.bfloat16)
    spectra = spectra.reshape(owned_blocks, row_count, doubled)
    spectra_all = lax.all_gather(spectra, "feat", axis=0, tiled=True)

    angle_plus = phases + jnp.float32(perturb_size)
    angle_minus = phases - jnp.float32(perturb_size)
    cos_plus = to_bf16(jnp.cos(angle_plus))
    sin_plus = to_bf16(jnp.sin(angle_plus))
    cos_minus = to_bf16(jnp.cos(angle_minus))
    sin_minus = to_bf16(jnp.sin(angle_minus))
    up = sign_bits == 1
    t_real = jnp.stack(
        [jnp.where(up, cos_plus, cos_minus), jnp.where(up, cos_minus, cos_plus)], 1
    ).reshape(net_count, owned_blocks, blocks, block_len)
    t_imag = jnp.stack(
        [jnp.where(up, sin_plus, sin_minus), jnp.where(up, sin_minus, sin_plus)], 1
    ).reshape(net_count, owned_blocks, blocks, block_len)

    mixed = mix(spectra_all, t_real, t_imag)
    mixed = mixed.reshape(net_count * owned_blocks * row_count, doubled)
    mix_real = mixed[:, :block_len]
    mix_imag = mixed[:, block_len:]
    field_real = jnp.dot(mix_real, cosine, preferred_element_type=f32) - jnp.dot(
        mix_imag, sine_part, preferred_element_type=f32
    )
    field_imag = jnp.dot(mix_real, sine_part, preferred_element_type=f32) + jnp.dot(
        mix_imag, cosine, preferred_element_type=f32
    )
    intensity = field_real**2 + field_imag**2
    logits = logit_scale * intensity.reshape(net_count, owned_blocks, row_count, block_len)
    first_class = feat_index * (owned_blocks * block_len)
    classes = first_class + jnp.arange(owned_blocks * block_len, dtype=jnp.int32).reshape(
        owned_blocks, 1, block_len
    )
    matches = classes == labels[None, :, None]
    local_top = jnp.max(logits, axis=(1, 3))
    local_total = jnp.sum(jnp.exp(logits - local_top[:, None, :, None]), axis=(1, 3))
    local_label = jnp.sum(jnp.where(matches[None], logits, 0.0), axis=(1, 3))
    stats = jnp.stack([local_top, local_total, local_label], 0)
    all_stats = lax.all_gather(stats, ("grp", "feat"), axis=0, tiled=False)
    all_stats = all_stats.reshape(group_count, feat_count, 3, net_count, row_count)
    part_top = all_stats[:, :, 0]
    row_top = jnp.max(part_top, axis=1)
    row_total = jnp.sum(all_stats[:, :, 1] * jnp.exp(part_top - row_top[:, None]), axis=1)
    row_label = jnp.sum(all_stats[:, :, 2], axis=1)
    losses = jnp.mean(row_top + jnp.log(row_total) - row_label, axis=2)
    losses = losses.reshape(total_pairs, 2)
    differences = (losses[:, 0] - losses[:, 1]) / (2.0 * perturb_size)

    estimate_all = (
        jnp.tensordot(
            differences, all_directions.astype(f32), 1, precision=lax.Precision.HIGHEST
        )
        / total_pairs
    )
    first_bias = 1.0 - beta_first**ADAM_STEP
    second_bias = 1.0 - beta_second**ADAM_STEP
    first_all = beta_first * all_first + (1.0 - beta_first) * estimate_all
    second_all = beta_second * all_second + (1.0 - beta_second) * estimate_all * estimate_all
    phases_next = phases - learn_rate * (first_all / first_bias) / (
        jnp.sqrt(second_all / second_bias) + adam_eps
    )
    first_column = group_index * own_columns
    estimate = lax.dynamic_slice_in_dim(estimate_all, first_column, own_columns, 1)
    first_new = beta_first * moment_first + (1.0 - beta_first) * estimate
    second_new = beta_second * moment_second + (1.0 - beta_second) * estimate * estimate
    return (estimate, first_new, second_new, phases_next)


def solution(mesh):
    return jax.shard_map(
        body,
        mesh=mesh,
        in_specs=(
            P(None, "feat", None),
            P(),
            P("feat", None, None),
            P("grp", "feat", None, None),
            P("feat", "grp", None),
            P("feat", "grp", None),
        ),
        out_specs=(
            P("feat", "grp", None),
            P("feat", "grp", None),
            P("feat", "grp", None),
            P("feat", None, None),
        ),
        check_vma=False,
    )
```

time: 271 us -> 151 us (0.56)
  local copies, waits for them, and re-layouts: 78.7 us -> 4.4 us
  other arithmetic: 58.6 us -> 13.4 us
  matrix products: 48.2 us -> 11.2 us
  Pallas kernels: 0 us -> 25.7 us
  blocking collectives: 38.3 us -> 62.7 us
  waiting for transfers between devices: 30.7 us -> 19.5 us
    all_gather x1 -> x3, blocking collectives: 9.97 us -> 62.7 us  [the longest x1 40.1 us: body(): all_stats = lax.all_gather(stats, ('grp', 'feat'), axis=0, tiled=False)]
    dot_general x4 -> x9, matrix products: 48.2 us -> 11.2 us  [the longest x1 4.13 us: body(): jnp.tensordot(differences, all_directions.astype(f32), 1, precision=lax.P...]
    reshape x5 -> x0, local copies, waits for them, and re-layouts: 36.2 us -> none  [the longest x2 34.8 us: body(): split_piece = shard_piece.reshape(row_count, piece_count, 2, block_len)]
    pallas_call x0 -> x1, Pallas kernels: none -> 25.7 us  [mix(): pl.pallas_call(kernel, grid=(nets, owned), in_specs=[pl.BlockSpec((blocks...]
    neg x2 -> x0, other arithmetic: 23.8 us -> none  [the longest x1 16.5 us: tables(): -sine_part]
    reduce_scatter x1 -> x0, waiting for transfers between devices: 23 us -> none  [body(): lax.psum_scatter(group_term, 'grp', scatter_dimension=1, tiled=True)]
    convert_element_type x2, other arithmetic: 25 us -> 2.48 us  [the longest x1 1.54 us: tables(): (cosine * factor).astype(jnp.bfloat16).reshape(block_len, block_len)]
    another operation x2, local copies, waits for them, and re-layouts: 24 us -> 1.67 us  [the longest x1 1.43 us: body(): jnp.stack([jnp.where(up, sin_plus, sin_minus), jnp.where(up, sin_minus, s...]
  transfers between devices with their start and end apart: 2 -> 2, of which waited for: 2 -> 1; matrix products, arithmetic and copies ran while one was open for 16% -> 10% of each run, Pallas kernels for 0% -> 17%
where the time goes in v1:
time: 151 us
  blocking collectives  62.7 us (42%)
  Pallas kernels  25.7 us (17%)
  waiting for transfers between devices  19.5 us (13%)
  between operations  14.3 us (9%)
  other arithmetic  13.4 us (9%)
  matrix products  11.2 us (7%)
  local copies, waits for them, and re-layouts  4.4 us (3%)
    all_gather x1, blocking collectives, body(): all_stats = lax.all_gather(stats, ('grp', 'feat'), axis=0, tiled=False)  40.1 us
    pallas_call x1, Pallas kernels, mix(): pl.pallas_call(kernel, grid=(nets, owned), in_specs=[pl.BlockSpec((blocks...  25.7 us
    all_gather x1, waiting for transfers between devices, body(): spectra_all = lax.all_gather(spectra, 'feat', axis=0, tiled=True)  19.4 us
    all_gather x1, blocking collectives, body(): all_first = lax.all_gather(moment_first, 'grp', axis=1, tiled=True)  11.5 us
    all_gather x1, blocking collectives, body(): all_second = lax.all_gather(moment_second, 'grp', axis=1, tiled=True)  11.1 us
    dot_general x1, matrix products, body(): jnp.tensordot(differences, all_directions.astype(f32), 1, precision=lax.P...  4.13 us
    reduce_precision x1, other arithmetic, to_bf16(): return lax.reduce_precision(values, exponent_bits=8, mantissa_bits=7)  3.75 us
  transfers between devices with their start and end apart: 2, of which 1 were waited for; matrix products, arithmetic and copies ran while one was open for 10% of the time, Pallas kernels for 17%

profile of v1, /device:TPU:0, one launch (start us, length us, event | category | flops | bytes accessed | tf_op | source)
XLA Modules:
  0.0 151.2 jit_solution(14416144480955646146)
XLA Ops:
  7.2 0.0 all-gather.4.cloned.1.call-start
  7.2 0.5 fusion.42
  7.8 0.6 fusion.45
  8.3 1.3 copy.21
  9.7 1.5 %multiply_convert_fusion.1 = (bf16[32,32,1024]{2,1,0:T(8,128)(2,1)S(1)}, bf16[32,32,1024]{2,1,0:T(8,128)(2,1)S(1)}) fusion(f32[32,1024]{1,0:T(8,128)S(1)} %get-tuple-element.25, f32[32,1024]{1,0:T(8,128)S(1)} %get-tuple-element.22, f32[32,1024]{1,0:T(8,128)S(1)} %get-tuple-element.26, f32[32,1024]{1,0:T(8,128)S(1)} %get-tuple-element.21), kind=kLoop, calls=%fused_computation.1 | loop fusion | flops 10485760 | bytes 4718592 | tf_op jit(solution)/shard_map/convert_element_type | solution.py:36
  11.3 0.4 fusion.23
  11.7 0.4 fusion.21
  12.2 0.4 copy-done
  12.6 0.4 fusion.2
  13.0 0.2 copy-done.2
  13.2 0.4 fusion.3
  13.7 0.9 pad_maximum_fusion.2
  14.6 0.0 all-gather.4.cloned.1.call-update
  14.6 0.0 all-gather.6.cloned.1.call-start
  14.6 0.9 add_convert_fusion
  15.6 0.0 all-gather.6.cloned.1.call-update
  15.6 3.7 %cosine_reduce-precision_fusion.1 = (f32[4,32,1024]{2,1,0:T(8,128)S(1)}, f32[4,32,1024]{2,1,0:T(8,128)S(1)}, f32[4,32,1024]{2,1,0:T(8,128)S(1)}, f32[4,32,1024]{2,1,0:T(8,128)S(1)}) fusion(f32[4,32,1024]{2,1,0:T(8,128)S(1)} %copy-done.5), kind=kLoop, calls=%fused_computation.41 | loop fusion | flops 786432 | bytes 2621440 | tf_op jit(solution)/shard_map/reduce_precision | solution.py:42
  19.4 0.2 select_bitcast_fusion.1
  19.6 0.5 select_bitcast_fusion.3
  20.1 0.6 pad_maximum_fusion
  20.7 0.2 copy.22
  20.9 0.0 copy-start.8
  21.0 0.0 copy-start.7
  21.0 1.4 copy.23
  22.4 11.5 %all_gather.22 = f32[4,32,1024]{2,1,0:T(8,128)S(1)} all-gather(f32[4,8,1024]{2,1,0:T(8,128)S(1)} %copy-done.8), channel_id=1, replica_groups=mesh['grp'=4,'feat'=8] {'grp'}, dimensions={1}, use_global_device_ids=true | all-gather | bytes 655360 | tf_op jit(solution)/shard_map/all_gather | solution.py:112
  33.9 11.1 %all_gather.23 = f32[4,32,1024]{2,1,0:T(8,128)} all-gather(f32[4,8,1024]{2,1,0:T(8,128)S(1)} %copy-done.7), channel_id=1, replica_groups=mesh['grp'=4,'feat'=8] {'grp'}, dimensions={1}, use_global_device_ids=true | all-gather | bytes 655360 | tf_op jit(solution)/shard_map/all_gather | solution.py:113
  45.0 0.1 broadcast_compare_fusion.1
  45.2 19.4 %all-gather.4.cloned.1.call-done.s_ref = bf16[32,32,2048]{2,1,0:T(8,128)(2,1)} async-done(((bf16[4,32,2048]{2,1,0:T(8,128)(2,1)}), bf16[32,32,2048]{2,1,0:T(8,128)(2,1)}) %all-gather.4.cloned.1.call-update) | async-done | bytes 4194320 | tf_op jit(solution)/shard_map/all_gather | solution.py:128
  64.6 25.7 %shard_map.93 = bf16[4,4,32,2048]{3,2,1,0:T(8,128)(2,1)S(1)} custom-call(bf16[32,32,2048]{2,1,0:T(8,128)(2,1)} %all-gather.4.cloned.1.call-done.s_ref, f32[4,4,32,1024]{3,2,1,0:T(8,128)S(1)} %bitcast.82, f32[4,4,32,1024]{3,2,1,0:T(8,128)} %bitcast.95), custom_call_target="tpu_custom_call" | custom-call | tf_op jit(solution)/shard_map/pallas_call | solution.py:84
  90.3 1.2 fusion.5
  91.6 0.3 copy-done.1
  91.9 1.2 fusion.9
  93.2 1.3 fusion.7
  94.4 1.5 %fusion.47 = (f32[512]{0:T(512)S(1)}, f32[512,1024]{1,0:T(8,128)S(1)}) fusion(f32[512,1024]{1,0:T(8,128)S(1)} %fusion.7, bf16[1024,1024]{1,0:T(8,128)(2,1)S(1)} %bitcast.90, bf16[512,2048]{1,0:T(8,128)(2,1)S(1)} %bitcast.86, f32[512,1024]{1,0:T(8,128)S(1)} %fusion.9, f32[512,1024]{1,0:T(8,128)S(1)} %fusion.5), kind=kOutput, calls=%fused_computation.90 | convolution fusion | flops 1077411328 | bytes 11536384 | tf_op jit(solution)/shard_map/dot_general | solution.py:151
  95.9 0.1 reduce_max.26
  96.1 0.1 sub.63
  96.1 0.7 exponential_reduce_fusion
  96.9 0.1 reduce_sum.60
  97.0 0.1 reduce_sum.63
  97.1 40.1 %all-gather = f32[96,4,32]{2,1,0:T(4,128)S(1)} all-gather(f32[3,4,32]{2,1,0:T(4,128)S(1)} %pad_maximum_fusion.3), channel_id=2, replica_groups=mesh['grp'=4,'feat'=8] {'grp','feat'}, dimensions={0}, use_global_device_ids=true | all-gather | bytes 50688 | tf_op jit(solution)/shard_map/all_gather | solution.py:165
  137.3 0.1 subtract_reduce_fusion
  137.4 0.1 div.28
  137.5 0.2 multiply_reduce_fusion
  137.6 0.0 all-gather.6.cloned.1.call-done
  137.7 4.1 %fusion = f32[1,4,32,1024]{3,0,2,1:T(1,128)S(1)} fusion(bf16[8,4,32,1024]{3,2,1,0:T(8,128)(2,1)} %all-gather.6.cloned.1.call-done, f32[8]{0:T(128)S(1)} %multiply_reduce_fusion), kind=kOutput, calls=%fused_computation.4 | convolution fusion | flops 12582912 | bytes 2621472 | tf_op jit(solution)/shard_map/dot_general | solution.py:176
  141.8 1.2 fusion.14
  143.0 0.7 fusion.32
  143.7 0.7 multiply_add_fusion
  (28 shorter events, 0.2 us)
Async XLA Ops:
  7.2 57.4 %all-gather.4.cloned.1.call-start = ((), (), s32[]{:S(2)}) async-start(), calls=%async_computation | async-start | bytes 4718592 | tf_op jit(solution)/shard_map/all_gather | solution.py:128
  11.2 1.3 copy-start
  11.2 2.0 %copy-start.2 = (bf16[32,32,1024]{2,1,0:T(8,128)(2,1)}, bf16[32,32,1024]{2,1,0:T(8,128)(2,1)S(1)}, u32[]{:S(2)}) copy-start(bf16[32,32,1024]{2,1,0:T(8,128)(2,1)S(1)} %get-tuple-element.19) | copy-start | bytes 6291460
  13.2 1.4 copy-start.4
  13.7 1.9 %copy-start.5 = (f32[4,32,1024]{2,1,0:T(8,128)S(1)}, f32[4,32,1024]{2,1,0:T(8,128)}, u32[]{:S(2)}) copy-start(f32[4,32,1024]{2,1,0:T(8,128)} %param.8) | copy-start | bytes 1572868
  14.6 123.1 %all-gather.6.cloned.1.call-start = ((), (), s32[]{:S(2)}) async-start(), calls=%async_computation.1 | async-start | bytes 2621440 | tf_op jit(solution)/shard_map/all_gather | solution.py:111
  20.9 1.5 copy-start.8
  21.0 12.9 %copy-start.7 = (f32[4,8,1024]{2,1,0:T(8,128)S(1)}, f32[4,8,1024]{2,1,0:T(8,128)}, u32[]{:S(2)}) copy-start(f32[4,8,1024]{2,1,0:T(8,128)} %param.11) | copy-start | bytes 393220
  21.0 24.0 %copy-start.10 = (s32[32]{0:T(128)S(1)}, s32[32]{0:T(128)}, u32[]{:S(2)}) copy-start(s32[32]{0:T(128)} %param.7) | copy-start | bytes 388
  64.6 25.7 %copy-start.3 = (bf16[32,32,1024]{2,1,0:T(8,128)(2,1)S(1)}, bf16[32,32,1024]{2,1,0:T(8,128)(2,1)}, u32[]{:S(2)}) copy-start(bf16[32,32,1024]{2,1,0:T(8,128)(2,1)} %copy-done.2) | copy-start | bytes 6291460
  90.3 1.6 %copy-start.1 = (bf16[32,32,1024]{2,1,0:T(8,128)(2,1)S(1)}, bf16[32,32,1024]{2,1,0:T(8,128)(2,1)}, u32[]{:S(2)}) copy-start(bf16[32,32,1024]{2,1,0:T(8,128)(2,1)} %copy-done) | copy-start | bytes 6291460
  96.9 44.9 %copy-start.6 = (f32[4,32,1024]{2,1,0:T(8,128)S(1)}, f32[4,32,1024]{2,1,0:T(8,128)}, u32[]{:S(2)}) copy-start(f32[4,32,1024]{2,1,0:T(8,128)} %all_gather.23) | copy-start | bytes 1572868
  143.7 0.7 copy-start.9
Sparse Core Ops, SparseCore 0:
  14.7 49.8 all-gather.3
  67.0 34.0 all-gather.5

commit v2 on v1

--- a/solution.py
+++ b/solution.py
@@ -109,8 +109,11 @@
 
     directions = (2 * sign_bits - 1).astype(jnp.bfloat16)
     all_directions = lax.all_gather(directions, "grp", axis=0, tiled=True)
-    all_first = lax.all_gather(moment_first, "grp", axis=1, tiled=True)
-    all_second = lax.all_gather(moment_second, "grp", axis=1, tiled=True)
+    moments = jnp.transpose(jnp.stack([moment_first, moment_second], 0), (2, 0, 1, 3))
+    all_moments = lax.all_gather(moments, "grp", axis=0, tiled=True)
+    all_moments = jnp.transpose(all_moments, (1, 2, 0, 3))
+    all_first = all_moments[0]
+    all_second = all_moments[1]
 
     cosine, sine_part = tables(block_len)
     local_in = jnp.transpose(inputs, (1, 0, 2)).reshape(owned_blocks * row_count, doubled)
@@ -162,15 +165,15 @@
     local_total = jnp.sum(jnp.exp(logits - local_top[:, None, :, None]), axis=(1, 3))
     local_label = jnp.sum(jnp.where(matches[None], logits, 0.0), axis=(1, 3))
     stats = jnp.stack([local_top, local_total, local_label], 0)
-    all_stats = lax.all_gather(stats, ("grp", "feat"), axis=0, tiled=False)
-    all_stats = all_stats.reshape(group_count, feat_count, 3, net_count, row_count)
-    part_top = all_stats[:, :, 0]
-    row_top = jnp.max(part_top, axis=1)
-    row_total = jnp.sum(all_stats[:, :, 1] * jnp.exp(part_top - row_top[:, None]), axis=1)
-    row_label = jnp.sum(all_stats[:, :, 2], axis=1)
-    losses = jnp.mean(row_top + jnp.log(row_total) - row_label, axis=2)
-    losses = losses.reshape(total_pairs, 2)
-    differences = (losses[:, 0] - losses[:, 1]) / (2.0 * perturb_size)
+    all_stats = lax.all_gather(stats, "feat", axis=0, tiled=False)
+    part_top = all_stats[:, 0]
+    row_top = jnp.max(part_top, axis=0)
+    row_total = jnp.sum(all_stats[:, 1] * jnp.exp(part_top - row_top[None]), axis=0)
+    row_label = jnp.sum(all_stats[:, 2], axis=0)
+    losses = jnp.mean(row_top + jnp.log(row_total) - row_label, axis=1)
+    losses = losses.reshape(pairs_here, 2)
+    own_differences = (losses[:, 0] - losses[:, 1]) / (2.0 * perturb_size)
+    differences = lax.all_gather(own_differences, "grp", axis=0, tiled=True)
 
     estimate_all = (
         jnp.tensordot(

time: 151 us -> 140 us (0.927)
  blocking collectives: 62.7 us -> 24.2 us
  waiting for transfers between devices: 19.5 us -> 43.3 us
  other arithmetic: 13.4 us -> 15.3 us
    all_gather x3 -> x2, blocking collectives: 62.7 us -> 24.2 us  [the longest x1 14 us: body(): all_stats = lax.all_gather(stats, 'feat', axis=0, tiled=False)]
    all_gather x1, waiting for transfers between devices: 19.4 us -> 39.6 us  [body(): spectra_all = lax.all_gather(spectra, 'feat', axis=0, tiled=True)]
    all_gather x0 -> x1, waiting for transfers between devices: none -> 3.71 us  [body(): all_moments = lax.all_gather(moments, 'grp', axis=0, tiled=True)]
    unnamed x23 -> x26, local copies, waits for them, and re-layouts: 2.31 us -> 3.14 us
  transfers between devices with their start and end apart: 2 -> 3, of which waited for: 1 -> 2; matrix products, arithmetic and copies ran while one was open for 10% -> 15% of each run, Pallas kernels for 17% -> 18%
where the time goes in v2:
time: 140 us
  waiting for transfers between devices  43.3 us (31%)
  Pallas kernels  25.7 us (18%)
  blocking collectives  24.2 us (17%)
  other arithmetic  15.3 us (11%)
  between operations  14.7 us (10%)
  matrix products  11.2 us (8%)
  local copies, waits for them, and re-layouts  5.24 us (4%)
    all_gather x1, waiting for transfers between devices, body(): spectra_all = lax.all_gather(spectra, 'feat', axis=0, tiled=True)  39.6 us
    pallas_call x1, Pallas kernels, mix(): pl.pallas_call(kernel, grid=(nets, owned), in_specs=[pl.BlockSpec((blocks...  25.7 us
    all_gather x1, blocking collectives, body(): all_stats = lax.all_gather(stats, 'feat', axis=0, tiled=False)  14 us
    all_gather x1, blocking collectives, body(): differences = lax.all_gather(own_differences, 'grp', axis=0, tiled=True)  10.3 us
    dot_general x1, matrix products, body(): jnp.tensordot(differences, all_directions.astype(f32), 1, precision=lax.P...  4.13 us
    reduce_precision x1, other arithmetic, to_bf16(): return lax.reduce_precision(values, exponent_bits=8, mantissa_bits=7)  3.75 us
    all_gather x1, waiting for transfers between devices, body(): all_moments = lax.all_gather(moments, 'grp', axis=0, tiled=True)  3.71 us
    unnamed x26, local copies, waits for them, and re-layouts  3.14 us
  transfers between devices with their start and end apart: 3, of which 2 were waited for; matrix products, arithmetic and copies ran while one was open for 15% of the time, Pallas kernels for 18%

profile of v2, /device:TPU:0, one launch (start us, length us, event | category | flops | bytes accessed | tf_op | source)
XLA Modules:
  0.0 139.9 jit_solution(11787500597440508737)
XLA Ops:
  7.2 0.0 all-gather.6.cloned.1.call-start
  7.2 0.5 fusion.41
  7.8 0.6 fusion.44
  8.3 1.3 copy.21
  9.7 1.5 %multiply_convert_fusion.1 = (bf16[32,32,1024]{2,1,0:T(8,128)(2,1)S(1)}, bf16[32,32,1024]{2,1,0:T(8,128)(2,1)S(1)}) fusion(f32[32,1024]{1,0:T(8,128)S(1)} %get-tuple-element.25, f32[32,1024]{1,0:T(8,128)S(1)} %get-tuple-element.22, f32[32,1024]{1,0:T(8,128)S(1)} %get-tuple-element.26, f32[32,1024]{1,0:T(8,128)S(1)} %get-tuple-element.21), kind=kLoop, calls=%fused_computation.1 | loop fusion | flops 10485760 | bytes 4718592 | tf_op jit(solution)/shard_map/convert_element_type | solution.py:36
  11.3 0.4 fusion.25
  11.7 0.4 fusion.23
  12.2 0.4 copy-done
  12.6 0.4 fusion.2
  13.0 0.2 copy-done.2
  13.2 0.4 fusion.3
  13.7 0.8 pad_maximum_fusion.2
  14.5 0.0 all-gather.6.cloned.1.call-update
  14.5 0.0 all-gather.8.cloned.1.call-start
  14.6 0.9 add_convert_fusion
  15.6 0.2 all-gather.10.cloned.1.call-start
  15.8 0.7 maximum_bitcast_fusion
  16.6 3.7 %cosine_reduce-precision_fusion.1 = (f32[4,32,1024]{2,1,0:T(8,128)S(1)}, f32[4,32,1024]{2,1,0:T(8,128)S(1)}, f32[4,32,1024]{2,1,0:T(8,128)S(1)}, f32[4,32,1024]{2,1,0:T(8,128)S(1)}) fusion(f32[4,32,1024]{2,1,0:T(8,128)S(1)} %copy-done.5), kind=kLoop, calls=%fused_computation.45 | loop fusion | flops 786432 | bytes 2621440 | tf_op jit(solution)/shard_map/reduce_precision | solution.py:42
  20.3 0.2 select_bitcast_fusion.1
  20.6 0.5 select_bitcast_fusion.3
  21.1 0.6 pad_maximum_fusion
  21.6 0.2 copy.22
  21.9 1.4 %copy.23 = f32[2,2,4,32,1024]{4,3,2,1,0:T(8,128)} copy(f32[2,2,4,32,1024]{4,3,2,0,1:T(8,128)S(1)} %get-tuple-element.28) | data formatting | bytes 4194304 | tf_op jit(solution)/shard_map/stack | solution.py:143
  23.4 0.1 broadcast_compare_fusion.1
  23.5 0.6 dynamic-slice
  24.8 39.6 %all-gather.6.cloned.1.call-done.s_ref = bf16[32,32,2048]{2,1,0:T(8,128)(2,1)} async-done(((bf16[4,32,2048]{2,1,0:T(8,128)(2,1)}), bf16[32,32,2048]{2,1,0:T(8,128)(2,1)}) %all-gather.6.cloned.1.call-update) | async-done | bytes 4194320 | tf_op jit(solution)/shard_map/all_gather | solution.py:131
  64.3 25.7 %shard_map.93 = bf16[4,4,32,2048]{3,2,1,0:T(8,128)(2,1)S(1)} custom-call(bf16[32,32,2048]{2,1,0:T(8,128)(2,1)} %all-gather.6.cloned.1.call-done.s_ref, f32[4,4,32,1024]{3,2,1,0:T(8,128)S(1)} %bitcast.96, f32[4,4,32,1024]{3,2,1,0:T(8,128)} %bitcast.109), custom_call_target="tpu_custom_call" | custom-call | tf_op jit(solution)/shard_map/pallas_call | solution.py:84
  90.1 1.3 fusion.5
  91.3 0.3 copy-done.1
  91.6 1.2 fusion.9
  92.9 1.2 fusion.7
  94.1 1.5 %fusion.49 = (f32[512]{0:T(512)S(1)}, f32[512,1024]{1,0:T(8,128)S(1)}) fusion(f32[512,1024]{1,0:T(8,128)S(1)} %fusion.7, bf16[1024,1024]{1,0:T(8,128)(2,1)S(1)} %bitcast.104, bf16[512,2048]{1,0:T(8,128)(2,1)S(1)} %bitcast.100, f32[512,1024]{1,0:T(8,128)S(1)} %fusion.9, f32[512,1024]{1,0:T(8,128)S(1)} %fusion.5), kind=kOutput, calls=%fused_computation.95 | convolution fusion | flops 1077411328 | bytes 11536384 | tf_op jit(solution)/shard_map/dot_general | solution.py:154
  95.7 0.1 reduce_max.26
  95.8 0.1 sub.63
  95.9 0.7 exponential_reduce_fusion
  96.6 0.1 reduce_sum.60
  96.7 0.1 reduce_sum.63
  96.8 14.0 %all-gather = f32[24,4,32]{2,1,0:T(4,128)S(1)} all-gather(f32[3,4,32]{2,1,0:T(4,128)S(1)} %pad_maximum_fusion.3), channel_id=2, replica_groups=mesh['grp'=4,'feat'=8] {'feat'}, dimensions={0}, use_global_device_ids=true | all-gather | bytes 13824 | tf_op jit(solution)/shard_map/all_gather | solution.py:168
  110.9 0.1 subtract_reduce_fusion
  111.0 0.1 div.28
  111.1 0.2 multiply_reduce_fusion
  111.3 0.2 dynamic-update-slice
  111.5 10.3 %all-reduce = f32[8]{0:T(128)S(1)} all-reduce(f32[8]{0:T(128)S(1)} %dynamic-update-slice), channel_id=3, replica_groups=mesh['grp'=4,'feat'=8] {'grp'}, use_global_device_ids=true, to_apply=%add | all-reduce | flops 8 | bytes 64 | tf_op jit(solution)/shard_map/all_gather | solution.py:176
  121.8 4.1 %fusion = f32[1,4,32,1024]{3,0,2,1:T(1,128)S(1)} fusion(bf16[8,4,32,1024]{3,2,1,0:T(8,128)(2,1)} %all-gather.8.cloned.1.call-done, f32[8]{0:T(128)S(1)} %all-reduce), kind=kOutput, calls=%fused_computation.4 | convolution fusion | flops 12582912 | bytes 2621472 | tf_op jit(solution)/shard_map/dot_general | solution.py:179
  125.9 3.7 %all-gather.10.cloned.1.call-done = f32[32,2,4,1024]{3,0,2,1:T(8,128)} async-done(((f32[8,2,4,1024]{3,0,2,1:T(8,128)}), f32[32,2,4,1024]{3,0,2,1:T(8,128)}) %all-gather.10.cloned.1.call-update) | async-done | bytes 1048592 | tf_op jit(solution)/shard_map/all_gather | solution.py:113
  129.6 2.4 %fusion.17 = (f32[4,32,1024]{2,1,0:T(8,128)}, f32[4,32,1024]{2,1,0:T(8,128)S(1)}) fusion(f32[4,32,1024]{2,1,0:T(8,128)S(1)} %copy-done.5, f32[2,4,32,1024]{3,2,1,0:T(8,128)} %bitcast.114, f32[1,4,32,1024]{3,0,2,1:T(1,128)S(1)} %fusion), kind=kLoop, calls=%fused_computation.32 | loop fusion | flops 1703936 | bytes 3145728 | tf_op jit(solution)/shard_map/sub | solution.py:188
  132.0 0.7 fusion.34
  132.7 0.7 multiply_add_fusion
  (34 shorter events, 0.2 us)
Async XLA Ops:
  7.2 57.2 %all-gather.6.cloned.1.call-start = ((), (), s32[]{:S(2)}) async-start(), calls=%async_computation | async-start | bytes 4718592 | tf_op jit(solution)/shard_map/all_gather | solution.py:131
  11.2 1.3 copy-start
  11.2 2.0 %copy-start.2 = (bf16[32,32,1024]{2,1,0:T(8,128)(2,1)}, bf16[32,32,1024]{2,1,0:T(8,128)(2,1)S(1)}, u32[]{:S(2)}) copy-start(bf16[32,32,1024]{2,1,0:T(8,128)(2,1)S(1)} %get-tuple-element.19) | copy-start | bytes 6291460
  13.2 1.4 copy-start.4
  13.7 2.1 %copy-start.7 = (f32[4,8,1024]{2,1,0:T(8,128)S(1)}, f32[4,8,1024]{2,1,0:T(8,128)}, u32[]{:S(2)}) copy-start(f32[4,8,1024]{2,1,0:T(8,128)} %param.11) | copy-start | bytes 393220
  13.7 2.1 %copy-start.8 = (f32[4,8,1024]{2,1,0:T(8,128)S(1)}, f32[4,8,1024]{2,1,0:T(8,128)}, u32[]{:S(2)}) copy-start(f32[4,8,1024]{2,1,0:T(8,128)} %param.10) | copy-start | bytes 393220
  13.7 2.9 %copy-start.5 = (f32[4,32,1024]{2,1,0:T(8,128)S(1)}, f32[4,32,1024]{2,1,0:T(8,128)}, u32[]{:S(2)}) copy-start(f32[4,32,1024]{2,1,0:T(8,128)} %param.8) | copy-start | bytes 1572868
  14.5 107.2 %all-gather.8.cloned.1.call-start = ((), (), s32[]{:S(2)}) async-start(), calls=%async_computation.1 | async-start | bytes 2621440 | tf_op jit(solution)/shard_map/all_gather | solution.py:111
  15.6 114.1 %all-gather.10.cloned.1.call-start = ((), (), s32[]{:S(2)}) async-start(), calls=%async_computation.2 | async-start | bytes 1310720 | tf_op jit(solution)/shard_map/all_gather | solution.py:113
  21.9 1.5 %copy-start.9 = (s32[32]{0:T(128)S(1)}, s32[32]{0:T(128)}, u32[]{:S(2)}) copy-start(s32[32]{0:T(128)} %param.7) | copy-start | bytes 388
  21.9 1.6 %copy-start.10 = (u32[32]{0:T(128)S(1)}, u32[32]{0:T(128)}, u32[]{:S(2)}) copy-start(u32[32]{0:T(128)} %constant.99) | copy-start | bytes 388
  64.3 25.7 %copy-start.3 = (bf16[32,32,1024]{2,1,0:T(8,128)(2,1)S(1)}, bf16[32,32,1024]{2,1,0:T(8,128)(2,1)}, u32[]{:S(2)}) copy-start(bf16[32,32,1024]{2,1,0:T(8,128)(2,1)} %copy-done.2) | copy-start | bytes 6291460
  90.0 1.6 %copy-start.1 = (bf16[32,32,1024]{2,1,0:T(8,128)(2,1)S(1)}, bf16[32,32,1024]{2,1,0:T(8,128)(2,1)}, u32[]{:S(2)}) copy-start(bf16[32,32,1024]{2,1,0:T(8,128)(2,1)} %copy-done) | copy-start | bytes 6291460
  132.7 0.7 copy-start.6
Sparse Core Ops, SparseCore 0:
  14.7 49.6 all-gather.5
  66.7 34.2 all-gather.7
  102.9 26.6 all-gather.9

commit v3 on v2

--- a/solution.py
+++ b/solution.py
@@ -100,12 +100,13 @@
     blocks = phases.shape[1]
     pairs_here = sign_bits.shape[0]
     group_count = lax.axis_size("grp")
-    feat_count = lax.axis_size("feat")
+    outer_count = lax.axis_size("fz")
+    core_count = lax.axis_size("fc")
     total_pairs = pairs_here * group_count
     net_count = 2 * pairs_here
     own_columns = blocks // group_count
     group_index = lax.axis_index("grp")
-    feat_index = lax.axis_index("feat")
+    feat_index = lax.axis_index("fz") * core_count + lax.axis_index("fc")
 
     directions = (2 * sign_bits - 1).astype(jnp.bfloat16)
     all_directions = lax.all_gather(directions, "grp", axis=0, tiled=True)
@@ -128,15 +129,23 @@
     )
     spectra = jnp.concatenate([spec_real, spec_imag], 1).astype(jnp.bfloat16)
     spectra = spectra.reshape(owned_blocks, row_count, doubled)
-    spectra_all = lax.all_gather(spectra, "feat", axis=0, tiled=True)
-
-    angle_plus = phases + jnp.float32(perturb_size)
-    angle_minus = phases - jnp.float32(perturb_size)
+    spectra_all = lax.all_gather(spectra, "fz", axis=0, tiled=True)
+    spectra_all = lax.all_gather(spectra_all, "fc", axis=0, tiled=True)
+
+    def core_major(values):
+        lead = values.shape[:-2]
+        values = values.reshape(lead + (outer_count, core_count, owned_blocks, block_len))
+        values = jnp.swapaxes(values, -3, -4)
+        return values.reshape(lead + (blocks, block_len))
+
+    phases_order = core_major(phases)
+    angle_plus = phases_order + jnp.float32(perturb_size)
+    angle_minus = phases_order - jnp.float32(perturb_size)
     cos_plus = to_bf16(jnp.cos(angle_plus))
     sin_plus = to_bf16(jnp.sin(angle_plus))
     cos_minus = to_bf16(jnp.cos(angle_minus))
     sin_minus = to_bf16(jnp.sin(angle_minus))
-    up = sign_bits == 1
+    up = core_major(sign_bits) == 1
     t_real = jnp.stack(
         [jnp.where(up, cos_plus, cos_minus), jnp.where(up, cos_minus, cos_plus)], 1
     ).reshape(net_count, owned_blocks, blocks, block_len)
@@ -165,7 +174,7 @@
     local_total = jnp.sum(jnp.exp(logits - local_top[:, None, :, None]), axis=(1, 3))
     local_label = jnp.sum(jnp.where(matches[None], logits, 0.0), axis=(1, 3))
     stats = jnp.stack([local_top, local_total, local_label], 0)
-    all_stats = lax.all_gather(stats, "feat", axis=0, tiled=False)
+    all_stats = lax.all_gather(stats, ("fz", "fc"), axis=0, tiled=False)
     part_top = all_stats[:, 0]
     row_top = jnp.max(part_top, axis=0)
     row_total = jnp.sum(all_stats[:, 1] * jnp.exp(part_top - row_top[None]), axis=0)
@@ -196,22 +205,28 @@
 
 
 def solution(mesh):
+    group_count = mesh.shape["grp"]
+    feat_count = mesh.shape["feat"]
+    core_count = 2 if feat_count % 2 == 0 else 1
+    devices = mesh.devices.reshape(group_count, feat_count // core_count, core_count)
+    split_mesh = jax.sharding.Mesh(devices, ("grp", "fz", "fc"))
+    feat = ("fz", "fc")
     return jax.shard_map(
         body,
-        mesh=mesh,
+        mesh=split_mesh,
         in_specs=(
-            P(None, "feat", None),
+            P(None, feat, None),
             P(),
-            P("feat", None, None),
-            P("grp", "feat", None, None),
-            P("feat", "grp", None),
-            P("feat", "grp", None),
+            P(feat, None, None),
+            P("grp", feat, None, None),
+            P(feat, "grp", None),
+            P(feat, "grp", None),
         ),
         out_specs=(
-            P("feat", "grp", None),
-            P("feat", "grp", None),
-            P("feat", "grp", None),
-            P("feat", None, None),
+            P(feat, "grp", None),
+            P(feat, "grp", None),
+            P(feat, "grp", None),
+            P(feat, None, None),
         ),
         check_vma=False,
     )

time: 140 us -> 155 us (1.11)
  waiting for transfers between devices: 43.3 us -> 54.5 us
  local copies, waits for them, and re-layouts: 5.24 us -> 7.42 us
    all_gather x1 -> x2, waiting for transfers between devices: 39.6 us -> 48.8 us  [the longest x1 48.7 us: body(): spectra_all = lax.all_gather(spectra, 'fz', axis=0, tiled=True)]
    reduce_precision x0 -> x12, local copies, waits for them, and re-layouts: none -> 3.2 us  [to_bf16(): return lax.reduce_precision(values, exponent_bits=8, mantissa_bits=7)]
    all_gather x1, waiting for transfers between devices: 3.71 us -> 5.69 us  [body(): all_moments = lax.all_gather(moments, 'grp', axis=0, tiled=True)]
    another operation x2 -> x0, local copies, waits for them, and re-layouts: 1.67 us -> none  [the longest x1 1.43 us: body(): jnp.stack([jnp.where(up, sin_plus, sin_minus), jnp.where(up, sin_minus, s...]
    unnamed x26 -> x28, local copies, waits for them, and re-layouts: 3.14 us -> 3.14 us
  transfers between devices with their start and end apart: 3 -> 4, of which waited for: 2 -> 2; matrix products, arithmetic and copies ran while one was open for 15% -> 16% of each run, Pallas kernels for 18% -> 17%
where the time goes in v3:
time: 155 us
  waiting for transfers between devices  54.5 us (35%)
  Pallas kernels  25.7 us (17%)
  blocking collectives  24.3 us (16%)
  other arithmetic  16.8 us (11%)
  between operations  14.8 us (10%)
  matrix products  11.2 us (7%)
  local copies, waits for them, and re-layouts  7.42 us (5%)
    all_gather x1, waiting for transfers between devices, body(): spectra_all = lax.all_gather(spectra, 'fz', axis=0, tiled=True)  48.7 us
    pallas_call x1, Pallas kernels, mix(): pl.pallas_call(kernel, grid=(nets, owned), in_specs=[pl.BlockSpec((blocks...  25.7 us
    all_gather x1, blocking collectives, body(): all_stats = lax.all_gather(stats, ('fz', 'fc'), axis=0, tiled=False)  14.5 us
    all_gather x1, blocking collectives, body(): differences = lax.all_gather(own_differences, 'grp', axis=0, tiled=True)  9.81 us
    all_gather x1, waiting for transfers between devices, body(): all_moments = lax.all_gather(moments, 'grp', axis=0, tiled=True)  5.69 us
    dot_general x1, matrix products, body(): jnp.tensordot(differences, all_directions.astype(f32), 1, precision=lax.P...  4.13 us
    reduce_precision x1, other arithmetic, to_bf16(): return lax.reduce_precision(values, exponent_bits=8, mantissa_bits=7)  3.93 us
    reduce_precision x12, local copies, waits for them, and re-layouts, to_bf16(): return lax.reduce_precision(values, exponent_bits=8, mantissa_bits=7)  3.2 us
  transfers between devices with their start and end apart: 4, of which 2 were waited for; matrix products, arithmetic and copies ran while one was open for 16% of the time, Pallas kernels for 17%

profile of v3, /device:TPU:0, one launch (start us, length us, event | category | flops | bytes accessed | tf_op | source)
XLA Modules:
  0.0 155.0 jit_solution(5513973933891021538)
XLA Ops:
  7.2 0.5 fusion.41
  7.8 0.6 fusion.44
  8.3 1.3 copy.34
  9.7 1.5 multiply_convert_fusion.1
  11.3 0.4 fusion.25
  11.7 0.4 fusion.23
  12.2 0.4 copy-done
  12.6 0.4 fusion.2
  13.0 0.2 copy-done.2
  13.2 0.4 fusion.3
  13.7 0.8 pad_maximum_fusion.2
  14.6 48.7 %all-gather.7.cloned.1.call-done = bf16[16,32,2048]{2,1,0:T(8,128)(2,1)} async-done(((bf16[4,32,2048]{2,1,0:T(8,128)(2,1)}), bf16[16,32,2048]{2,1,0:T(8,128)(2,1)}) %all-gather.7.cloned.1.call-update) | async-done | bytes 2097168 | tf_op jit(solution)/shard_map/all_gather | solution.py:132
  63.4 0.9 add_convert_fusion
  64.4 0.7 maximum_bitcast_fusion
  65.4 3.9 %sine_reduce-precision_fusion.1 = (f32[4,32,1024]{2,1,0:T(8,128)S(1)}, f32[4,32,1024]{2,1,0:T(8,128)S(1)}, f32[4,32,1024]{2,1,0:T(8,128)S(1)}, f32[4,32,1024]{2,1,0:T(8,128)S(1)}) fusion(f32[4,32,1024]{2,1,0:T(8,128)S(1)} %copy-done.5), kind=kLoop, calls=%fused_computation.41 | loop fusion | flops 786432 | bytes 2621440 | tf_op jit(solution)/shard_map/reduce_precision | solution.py:42
  69.3 0.1 reshape.246
  69.5 0.3 copy.36
  69.8 0.3 copy.37
  70.1 0.1 reshape.247
  70.3 0.3 copy.38
  70.6 0.3 copy.39
  70.9 0.1 reshape.248
  71.1 0.3 copy.40
  71.5 0.3 copy.41
  71.9 0.3 copy.42
  72.3 0.3 copy.43
  72.6 0.2 eq.52
  72.8 0.3 copy.35
  73.1 0.2 eq.54
  73.5 0.6 dynamic-slice
  74.7 0.7 broadcast_select_fusion.1
  75.4 1.8 %pad_maximum_fusion = (f32[2,2,4,32,1024]{4,3,2,1,0:T(8,128)S(1)}, f32[2,2,4,32,1024]{4,3,2,1,0:T(8,128)}) fusion(f32[2,1,4,32,1024]{4,3,2,1,0:T(8,128)S(1)} %get-tuple-element.20, f32[2,1,4,32,1024]{4,3,2,1,0:T(8,128)S(1)} %get-tuple-element.21, f32[2,1,4,32,1024]{4,3,2,1,0:T(8,128)S(1)} %get-tuple-element.9, f32[2,1,4,32,1024]{4,3,2,1,0:T(8,128)S(1)} %get-tuple-element.8), kind=kLoop, calls=%fused_computation.2 | loop fusion | flops 1048576 | bytes 8388608 | tf_op jit(solution)/shard_map/stack | solution.py:149
  77.3 25.7 %shard_map.93 = bf16[4,4,32,2048]{3,2,1,0:T(8,128)(2,1)S(1)} custom-call(bf16[32,32,2048]{2,1,0:T(8,128)(2,1)} %all-gather.9.cloned.1.call-done.s_ref, f32[4,4,32,1024]{3,2,1,0:T(8,128)S(1)} %bitcast.103, f32[4,4,32,1024]{3,2,1,0:T(8,128)} %bitcast.116), custom_call_target="tpu_custom_call" | custom-call | tf_op jit(solution)/shard_map/pallas_call | solution.py:84
  103.0 1.3 fusion.5
  104.3 0.3 copy-done.1
  104.6 1.2 fusion.9
  105.9 1.3 fusion.7
  107.1 1.5 fusion.49
  108.9 0.7 exponential_reduce_fusion
  109.8 14.5 %all-gather = f32[24,4,32]{2,1,0:T(4,128)S(1)} all-gather(f32[3,4,32]{2,1,0:T(4,128)S(1)} %pad_maximum_fusion.3), channel_id=2, replica_groups=mesh['grp'=4,'fz'=4,'fc'=2] {'fz','fc'}, dimensions={0}, use_global_device_ids=true | all-gather | bytes 13824 | tf_op jit(solution)/shard_map/all_gather | solution.py:177
  124.6 0.2 multiply_reduce_fusion
  124.8 0.2 dynamic-update-slice
  125.0 9.8 %all-reduce = f32[8]{0:T(128)S(1)} all-reduce(f32[8]{0:T(128)S(1)} %dynamic-update-slice), channel_id=3, replica_groups=mesh['grp'=4,'fz'=4,'fc'=2] {'grp'}, use_global_device_ids=true, to_apply=%add | all-reduce | flops 8 | bytes 64 | tf_op jit(solution)/shard_map/all_gather | solution.py:185
  134.8 4.1 %fusion = f32[1,4,32,1024]{3,0,2,1:T(1,128)S(1)} fusion(bf16[8,4,32,1024]{3,2,1,0:T(8,128)(2,1)} %all-gather.11.cloned.1.call-done, f32[8]{0:T(128)S(1)} %all-reduce), kind=kOutput, calls=%fused_computation.4 | convolution fusion | flops 12582912 | bytes 2621472 | tf_op jit(solution)/shard_map/dot_general | solution.py:188
  139.0 5.7 %all-gather.13.cloned.1.call-done = f32[32,2,4,1024]{3,0,2,1:T(8,128)} async-done(((f32[8,2,4,1024]{3,0,2,1:T(8,128)}), f32[32,2,4,1024]{3,0,2,1:T(8,128)}) %all-gather.13.cloned.1.call-update) | async-done | bytes 1048592 | tf_op jit(solution)/shard_map/all_gather | solution.py:114
  144.7 2.4 %fusion.17 = (f32[4,32,1024]{2,1,0:T(8,128)}, f32[4,32,1024]{2,1,0:T(8,128)S(1)}) fusion(f32[4,32,1024]{2,1,0:T(8,128)S(1)} %copy-done.5, f32[2,4,32,1024]{3,2,1,0:T(8,128)} %bitcast.125, f32[1,4,32,1024]{3,0,2,1:T(1,128)S(1)} %fusion), kind=kLoop, calls=%fused_computation.28 | loop fusion | flops 1703936 | bytes 3145728 | tf_op jit(solution)/shard_map/sub | solution.py:197
  147.1 0.7 fusion.34
  147.7 0.7 multiply_add_fusion
  (52 shorter events, 1.5 us)
Async XLA Ops:
  7.2 56.2 %all-gather.7.cloned.1.call-start = ((), (), s32[]{:S(2)}) async-start(), calls=%async_computation | async-start | bytes 2621440 | tf_op jit(solution)/shard_map/all_gather | solution.py:132
  11.2 1.3 copy-start
  11.2 2.0 %copy-start.2 = (bf16[32,32,1024]{2,1,0:T(8,128)(2,1)}, bf16[32,32,1024]{2,1,0:T(8,128)(2,1)S(1)}, u32[]{:S(2)}) copy-start(bf16[32,32,1024]{2,1,0:T(8,128)(2,1)S(1)} %get-tuple-element.19) | copy-start | bytes 6291460
  13.7 49.8 %copy-start.4 = (s32[2,4,32,1024]{3,2,1,0:T(8,128)S(1)}, s32[2,4,32,1024]{3,2,1,0:T(8,128)}, u32[]{:S(2)}) copy-start(s32[2,4,32,1024]{3,2,1,0:T(8,128)} %param.9) | copy-start | bytes 3145732
  14.5 62.8 %all-gather.9.cloned.1.call-start = ((), (), s32[]{:S(2)}) async-start(), calls=%async_computation.1 | async-start | bytes 6291456 | tf_op jit(solution)/shard_map/all_gather | solution.py:133
  63.3 1.1 copy-start.7
  63.3 1.1 copy-start.8
  63.3 2.0 %copy-start.5 = (f32[4,32,1024]{2,1,0:T(8,128)S(1)}, f32[4,32,1024]{2,1,0:T(8,128)}, u32[]{:S(2)}) copy-start(f32[4,32,1024]{2,1,0:T(8,128)} %param.8) | copy-start | bytes 1572868
  63.4 71.5 %all-gather.11.cloned.1.call-start = ((), (), s32[]{:S(2)}) async-start(), calls=%async_computation.2 | async-start | bytes 2621440 | tf_op jit(solution)/shard_map/all_gather | solution.py:112
  64.4 80.3 %all-gather.13.cloned.1.call-start = ((), (), s32[]{:S(2)}) async-start(), calls=%async_computation.3 | async-start | bytes 1310720 | tf_op jit(solution)/shard_map/all_gather | solution.py:114
  71.9 1.4 copy-start.10
  71.9 1.5 copy-start.11
  77.3 25.7 %copy-start.3 = (bf16[32,32,1024]{2,1,0:T(8,128)(2,1)S(1)}, bf16[32,32,1024]{2,1,0:T(8,128)(2,1)}, u32[]{:S(2)}) copy-start(bf16[32,32,1024]{2,1,0:T(8,128)(2,1)} %copy-done.2) | copy-start | bytes 6291460
  103.0 1.6 %copy-start.1 = (bf16[32,32,1024]{2,1,0:T(8,128)(2,1)S(1)}, bf16[32,32,1024]{2,1,0:T(8,128)(2,1)}, u32[]{:S(2)}) copy-start(bf16[32,32,1024]{2,1,0:T(8,128)(2,1)} %copy-done) | copy-start | bytes 6291460
  139.0 8.8 %copy-start.9 = (f32[4,8,1024]{2,1,0:T(8,128)S(1)}, f32[4,8,1024]{2,1,0:T(8,128)}, u32[]{:S(2)}) copy-start(f32[4,8,1024]{2,1,0:T(8,128)} %param.10) | copy-start | bytes 393220
  147.7 0.7 copy-start.6
Sparse Core Ops, SparseCore 0:
  14.6 48.6 all-gather.6
  64.9 12.3 all-gather.8
  79.7 36.4 all-gather.10
  117.9 26.7 all-gather.12

commit v4 on v2

--- a/solution.py
+++ b/solution.py
@@ -94,6 +94,48 @@
     )(spectra_all, t_real, t_imag)
 
 
+def gather_by_permutes(values, axis_name, size, index):
+    parts = [values] + [
+        lax.ppermute(values, axis_name, [(i, (i + s) % size) for i in range(size)])
+        for s in range(1, size)
+    ]
+    order = (index - jnp.arange(size)) % size
+    return jnp.take(jnp.stack(parts, 0), order, axis=0)
+
+
+def merge_stats(top, total, label, axis_name, size):
+    if size & (size - 1):
+        tops, totals, labels = lax.all_gather((top, total, label), axis_name)
+        merged = jnp.max(tops, axis=0)
+        merged_total = jnp.sum(totals * jnp.exp(tops - merged[None]), axis=0)
+        return merged, merged_total, jnp.sum(labels, axis=0)
+    step = 1
+    while step < size:
+        perm = [(i, i ^ step) for i in range(size)]
+        packed = lax.ppermute(jnp.stack([top, total, label], 0), axis_name, perm)
+        other_top, other_total, other_label = packed[0], packed[1], packed[2]
+        merged = jnp.maximum(top, other_top)
+        total = total * jnp.exp(top - merged) + other_total * jnp.exp(other_top - merged)
+        label = label + other_label
+        top = merged
+        step *= 2
+    return top, total, label
+
+
+def gather_small(values, axis_name, size, index):
+    if size & (size - 1):
+        return lax.all_gather(values, axis_name, axis=0, tiled=True)
+    count = values.shape[0]
+    slots = jnp.zeros((size * count,), values.dtype)
+    slots = lax.dynamic_update_slice_in_dim(slots, values, index * count, 0)
+    step = 1
+    while step < size:
+        perm = [(i, i ^ step) for i in range(size)]
+        slots = slots + lax.ppermute(slots, axis_name, perm)
+        step *= 2
+    return slots
+
+
 def body(inputs, labels, phases, sign_bits, moment_first, moment_second):
     row_count, owned_blocks, doubled = inputs.shape
     block_len = doubled // 2
@@ -108,10 +150,13 @@
     feat_index = lax.axis_index("feat")
 
     directions = (2 * sign_bits - 1).astype(jnp.bfloat16)
-    all_directions = lax.all_gather(directions, "grp", axis=0, tiled=True)
-    moments = jnp.transpose(jnp.stack([moment_first, moment_second], 0), (2, 0, 1, 3))
-    all_moments = lax.all_gather(moments, "grp", axis=0, tiled=True)
-    all_moments = jnp.transpose(all_moments, (1, 2, 0, 3))
+    all_directions = gather_by_permutes(directions, "grp", group_count, group_index)
+    all_directions = all_directions.reshape((total_pairs,) + directions.shape[1:])
+    moments = jnp.stack([moment_first, moment_second], 0)
+    all_moments = gather_by_permutes(moments, "grp", group_count, group_index)
+    all_moments = jnp.transpose(all_moments, (1, 2, 0, 3, 4)).reshape(
+        (2, owned_blocks, blocks, block_len)
+    )
     all_first = all_moments[0]
     all_second = all_moments[1]
 
@@ -164,21 +209,16 @@
     local_top = jnp.max(logits, axis=(1, 3))
     local_total = jnp.sum(jnp.exp(logits - local_top[:, None, :, None]), axis=(1, 3))
     local_label = jnp.sum(jnp.where(matches[None], logits, 0.0), axis=(1, 3))
-    stats = jnp.stack([local_top, local_total, local_label], 0)
-    all_stats = lax.all_gather(stats, "feat", axis=0, tiled=False)
-    part_top = all_stats[:, 0]
-    row_top = jnp.max(part_top, axis=0)
-    row_total = jnp.sum(all_stats[:, 1] * jnp.exp(part_top - row_top[None]), axis=0)
-    row_label = jnp.sum(all_stats[:, 2], axis=0)
+    row_top, row_total, row_label = merge_stats(
+        local_top, local_total, local_label, "feat", feat_count
+    )
     losses = jnp.mean(row_top + jnp.log(row_total) - row_label, axis=1)
     losses = losses.reshape(pairs_here, 2)
     own_differences = (losses[:, 0] - losses[:, 1]) / (2.0 * perturb_size)
-    differences = lax.all_gather(own_differences, "grp", axis=0, tiled=True)
+    differences = gather_small(own_differences, "grp", group_count, group_index)
 
     estimate_all = (
-        jnp.tensordot(
-            differences, all_directions.astype(f32), 1, precision=lax.Precision.HIGHEST
-        )
+        jnp.sum(differences[:, None, None, None] * all_directions.astype(f32), axis=0)
         / total_pairs
     )
     first_bias = 1.0 - beta_first**ADAM_STEP

time: 140 us -> 127 us (0.907)
  blocking collectives: 24.2 us -> 0 us
  starting transfers between devices: 0.3 us -> 14.4 us
  waiting for transfers between devices: 43.3 us -> 35.2 us
  other arithmetic: 15.3 us -> 21 us
  matrix products: 11.2 us -> 7.06 us
  local copies, waits for them, and re-layouts: 5.24 us -> 9.11 us
    all_gather x1, waiting for transfers between devices: 39.6 us -> 7.64 us  [body(): spectra_all = lax.all_gather(spectra, 'feat', axis=0, tiled=True)]
    ppermute x0 -> x11, waiting for transfers between devices: none -> 27.5 us  [the longest x6 20 us: gather_by_permutes(): lax.ppermute(values, axis_name, [(i, (i + s) % size) for i in range(size)])]
    all_gather x2 -> x0, blocking collectives: 24.2 us -> none  [the longest x1 14 us: body(): all_stats = lax.all_gather(stats, 'feat', axis=0, tiled=False)]
    ppermute x0 -> x11, starting transfers between devices: none -> 14.4 us  [the longest x6 9.91 us: gather_by_permutes(): lax.ppermute(values, axis_name, [(i, (i + s) % size) for i in range(size)])]
    another operation x1 -> x7, other arithmetic: 0.01 us -> 5.88 us  [the longest x4 5.86 us: gather_by_permutes(): return jnp.take(jnp.stack(parts, 0), order, axis=0)]
    dot_general x1 -> x0, matrix products: 4.13 us -> none  [body(): jnp.tensordot(differences, all_directions.astype(f32), 1, precision=lax.P...]
    gather x0 -> x2, local copies, waits for them, and re-layouts: none -> 3.86 us  [gather_by_permutes(): return jnp.take(jnp.stack(parts, 0), order, axis=0)]
    all_gather x2 -> x0, waiting for transfers between devices: 3.71 us -> none  [the longest x1 3.71 us: body(): all_moments = lax.all_gather(moments, 'grp', axis=0, tiled=True)]
  transfers between devices with their start and end apart: 3 -> 12, of which waited for: 2 -> 7; matrix products, arithmetic and copies ran while one was open for 15% -> 20% of each run, Pallas kernels for 18% -> 20%
where the time goes in v4:
time: 127 us
  waiting for transfers between devices  35.2 us (28%)
  Pallas kernels  25.7 us (20%)
  other arithmetic  21 us (17%)
  starting transfers between devices  14.4 us (11%)
  between operations  14.4 us (11%)
  local copies, waits for them, and re-layouts  9.11 us (7%)
  matrix products  7.06 us (6%)
    pallas_call x1, Pallas kernels, mix(): pl.pallas_call(kernel, grid=(nets, owned), in_specs=[pl.BlockSpec((blocks...  25.7 us
    ppermute x6, waiting for transfers between devices, gather_by_permutes(): lax.ppermute(values, axis_name, [(i, (i + s) % size) for i in range(size)])  20 us
    ppermute x6, starting transfers between devices, gather_by_permutes(): lax.ppermute(values, axis_name, [(i, (i + s) % size) for i in range(size)])  9.91 us
    all_gather x1, waiting for transfers between devices, body(): spectra_all = lax.all_gather(spectra, 'feat', axis=0, tiled=True)  7.64 us
    another operation x4, other arithmetic, gather_by_permutes(): return jnp.take(jnp.stack(parts, 0), order, axis=0)  5.86 us
    ppermute x2, waiting for transfers between devices, gather_small(): slots = slots + lax.ppermute(slots, axis_name, perm)  4.12 us
    gather x2, local copies, waits for them, and re-layouts, gather_by_permutes(): return jnp.take(jnp.stack(parts, 0), order, axis=0)  3.86 us
    reduce_precision x1, other arithmetic, to_bf16(): return lax.reduce_precision(values, exponent_bits=8, mantissa_bits=7)  3.73 us
  transfers between devices with their start and end apart: 12, of which 7 were waited for; matrix products, arithmetic and copies ran while one was open for 20% of the time, Pallas kernels for 20%

profile of v4, /device:TPU:0, one launch (start us, length us, event | category | flops | bytes accessed | tf_op | source)
XLA Modules:
  0.0 126.9 jit_solution(5433492662965805166)
XLA Ops:
  7.2 0.5 fusion.34
  7.8 0.6 fusion.37
  8.3 1.3 %copy.24 = bf16[32,4,2048]{2,0,1:T(8,128)(2,1)S(1)} copy(bf16[32,4,2048]{2,1,0:T(4,128)(2,1)} %param.6) | data formatting | bytes 1048576 | tf_op args[0]
  9.7 1.5 %multiply_convert_fusion.1 = (bf16[32,32,1024]{2,1,0:T(8,128)(2,1)S(1)}, bf16[32,32,1024]{2,1,0:T(8,128)(2,1)S(1)}) fusion(f32[32,1024]{1,0:T(8,128)S(1)} %get-tuple-element.35, f32[32,1024]{1,0:T(8,128)S(1)} %get-tuple-element.32, f32[32,1024]{1,0:T(8,128)S(1)} %get-tuple-element.36, f32[32,1024]{1,0:T(8,128)S(1)} %get-tuple-element.31), kind=kLoop, calls=%fused_computation.4 | loop fusion | flops 10485760 | bytes 4718592 | tf_op jit(solution)/shard_map/convert_element_type | solution.py:36
  11.3 0.4 fusion.18
  11.7 0.4 fusion.16
  12.2 0.4 copy-done
  12.6 0.4 fusion
  13.2 0.4 fusion.1
  13.7 0.8 pad_maximum_fusion.4
  14.6 1.0 add_convert_fusion
  15.5 2.9 %collective-permute-start.5 = (bf16[2,4,32,1024]{3,2,1,0:T(8,128)(2,1)}, bf16[2,4,32,1024]{3,2,1,0:T(8,128)(2,1)}, u32[]{:S(2)}, u32[]{:S(2)}) collective-permute-start(bf16[2,4,32,1024]{3,2,1,0:T(8,128)(2,1)} %add_convert_fusion), channel_id=1, source_target_pairs={{0,8},{8,16},{16,24},{24,0},{1,9},{9,17},{17,25},{25,1},{2,10},{10... | collective-permute-start | bytes 1572872 | tf_op jit(solution)/shard_map/ppermute | solution.py:99
  18.5 1.5 %collective-permute-start.6 = (bf16[2,4,32,1024]{3,2,1,0:T(8,128)(2,1)}, bf16[2,4,32,1024]{3,2,1,0:T(8,128)(2,1)}, u32[]{:S(2)}, u32[]{:S(2)}) collective-permute-start(bf16[2,4,32,1024]{3,2,1,0:T(8,128)(2,1)} %add_convert_fusion), channel_id=1, source_target_pairs={{0,16},{8,24},{16,0},{24,8},{1,17},{9,25},{17,1},{25,9},{2,18},{10... | collective-permute-start | bytes 1572872 | tf_op jit(solution)/shard_map/ppermute | solution.py:99
  20.0 0.8 fusion.60
  20.8 2.0 %collective-permute-start.9 = (f32[2,4,8,1024]{3,2,1,0:T(8,128)}, f32[2,4,8,1024]{3,2,1,0:T(8,128)}, u32[]{:S(2)}, u32[]{:S(2)}) collective-permute-start(f32[2,4,8,1024]{3,2,1,0:T(8,128)} %get-tuple-element.25), channel_id=1, source_target_pairs={{0,16},{8,24},{16,0},{24,8},{1,17},{9,25},{17,1},{25,9},{2,18},{10... | collective-permute-start | bytes 786440 | tf_op jit(solution)/shard_map/ppermute | solution.py:99
  22.8 1.4 %collective-permute-start.10 = (f32[2,4,8,1024]{3,2,1,0:T(8,128)}, f32[2,4,8,1024]{3,2,1,0:T(8,128)}, u32[]{:S(2)}, u32[]{:S(2)}) collective-permute-start(f32[2,4,8,1024]{3,2,1,0:T(8,128)} %get-tuple-element.25), channel_id=1, source_target_pairs={{0,24},{8,0},{16,8},{24,16},{1,25},{9,1},{17,9},{25,17},{2,26},{10... | collective-permute-start | bytes 786440 | tf_op jit(solution)/shard_map/ppermute | solution.py:99
  24.2 3.7 %cosine_reduce-precision_fusion.1 = (f32[4,32,1024]{2,1,0:T(8,128)S(1)}, f32[4,32,1024]{2,1,0:T(8,128)S(1)}, f32[4,32,1024]{2,1,0:T(8,128)S(1)}, f32[4,32,1024]{2,1,0:T(8,128)S(1)}) fusion(f32[4,32,1024]{2,1,0:T(8,128)S(1)} %copy-done.6), kind=kLoop, calls=%fused_computation.43 | loop fusion | flops 786432 | bytes 2621440 | tf_op jit(solution)/shard_map/reduce_precision | solution.py:42
  28.2 0.4 select_bitcast_fusion.4
  28.6 0.6 pad_maximum_fusion
  29.5 1.5 %copy.26 = f32[2,2,4,32,1024]{4,3,2,1,0:T(8,128)} copy(f32[2,2,4,32,1024]{4,3,2,0,1:T(8,128)S(1)} %get-tuple-element.38) | data formatting | bytes 4194304 | tf_op jit(solution)/shard_map/stack | solution.py:188
  31.2 1.0 fusion.70
  32.2 6.0 %collective-permute-done.8 = f32[2,4,8,1024]{3,2,1,0:T(8,128)} collective-permute-done((f32[2,4,8,1024]{3,2,1,0:T(8,128)}, f32[2,4,8,1024]{3,2,1,0:T(8,128)}, u32[]{:S(2)}, u32[]{:S(2)}) %collective-permute-start.8) | collective-permute-done | bytes 262176 | tf_op jit(solution)/shard_map/ppermute | solution.py:99
  38.2 2.0 %collective-permute-start.7 = (bf16[2,4,32,1024]{3,2,1,0:T(8,128)(2,1)}, bf16[2,4,32,1024]{3,2,1,0:T(8,128)(2,1)}, u32[]{:S(2)}, u32[]{:S(2)}) collective-permute-start(bf16[2,4,32,1024]{3,2,1,0:T(8,128)(2,1)} %add_convert_fusion), channel_id=1, source_target_pairs={{0,24},{8,0},{16,8},{24,16},{1,25},{9,1},{17,9},{25,17},{2,26},{10... | collective-permute-start | bytes 1572872 | tf_op jit(solution)/shard_map/ppermute | solution.py:99
  40.2 14.0 %collective-permute-done.9 = f32[2,4,8,1024]{3,2,1,0:T(8,128)} collective-permute-done((f32[2,4,8,1024]{3,2,1,0:T(8,128)}, f32[2,4,8,1024]{3,2,1,0:T(8,128)}, u32[]{:S(2)}, u32[]{:S(2)}) %collective-permute-start.9) | collective-permute-done | bytes 262176 | tf_op jit(solution)/shard_map/ppermute | solution.py:99
  54.2 1.2 pad_maximum_fusion.3
  55.3 1.6 %gather_fusion.1 = f32[4,2,4,8,1024]{4,3,2,1,0:T(8,128)} fusion(f32[4,2,4,8,1024]{4,3,2,1,0:T(8,128)S(1)} %pad_maximum_fusion.3, s32[1024]{0:T(1024)S(1)} %pad_clamp_fusion), kind=kCustom, calls=%fused_computation.1 | custom fusion | bytes 2097168 | tf_op jit(solution)/shard_map/jit(_take)/gather | solution.py:103
  56.9 7.6 %all-gather.2.cloned.1.call-done.s_ref = bf16[32,32,2048]{2,1,0:T(8,128)(2,1)} async-done(((bf16[4,32,2048]{2,1,0:T(8,128)(2,1)}), bf16[32,32,2048]{2,1,0:T(8,128)(2,1)}) %all-gather.2.cloned.1.call-update) | async-done | bytes 4194320 | tf_op jit(solution)/shard_map/all_gather | solution.py:176
  64.6 25.7 %shard_map.93 = bf16[4,4,32,2048]{3,2,1,0:T(8,128)(2,1)S(1)} custom-call(bf16[32,32,2048]{2,1,0:T(8,128)(2,1)} %all-gather.2.cloned.1.call-done.s_ref, f32[4,4,32,1024]{3,2,1,0:T(8,128)S(1)} %bitcast.160, f32[4,4,32,1024]{3,2,1,0:T(8,128)} %bitcast.173), custom_call_target="tpu_custom_call" | custom-call | tf_op jit(solution)/shard_map/pallas_call | solution.py:84
  90.3 1.2 fusion.3
  91.9 1.2 fusion.7
  93.1 1.3 fusion.5
  94.4 1.5 %fusion.61 = (f32[512]{0:T(512)S(1)}, f32[512,1024]{1,0:T(8,128)S(1)}) fusion(f32[512,1024]{1,0:T(8,128)S(1)} %fusion.5, bf16[1024,1024]{1,0:T(8,128)(2,1)S(1)} %bitcast.168, bf16[512,2048]{1,0:T(8,128)(2,1)S(1)} %bitcast.164, f32[512,1024]{1,0:T(8,128)S(1)} %fusion.7, f32[512,1024]{1,0:T(8,128)S(1)} %fusion.3), kind=kOutput, calls=%fused_computation.139 | convolution fusion | flops 1077411328 | bytes 11536384 | tf_op jit(solution)/shard_map/dot_general | solution.py:199
  96.1 0.7 exponential_reduce_fusion
  97.6 0.7 collective-permute-done
  98.4 0.9 slice_multiply_fusion.1
  99.3 2.7 %collective-permute-done.1 = f32[3,4,32]{2,1,0:T(4,128)S(1)} collective-permute-done((f32[3,4,32]{2,1,0:T(4,128)S(1)}, f32[3,4,32]{2,1,0:T(4,128)S(1)}, u32[]{:S(2)}, u32[]{:S(2)}) %collective-permute-start.1) | collective-permute-done | bytes 1568 | tf_op jit(solution)/shard_map/ppermute | solution.py:115
  102.1 1.1 collective-permute-start.2
  103.2 3.0 %pad_maximum_fusion.2 = bf16[4,2,4,32,1024]{4,3,2,1,0:T(8,128)(2,1)} fusion(bf16[1,2,4,32,1024]{4,3,2,1,0:T(8,128)(2,1)} %bitcast.32, bf16[1,2,4,32,1024]{4,3,2,1,0:T(8,128)(2,1)} %bitcast.31, bf16[1,2,4,32,1024]{4,3,2,1,0:T(8,128)(2,1)} %bitcast.30, bf16[1,2,4,32,1024]{4,3,2,1,0:T(8,128)(2,1)S(1)} %copy-done.8), kind=kLoop, calls=%fused_computation.7 | loop fusion | flops 3145728 | bytes 4194304 | tf_op jit(solution)/shard_map/stack | solution.py:103
  106.2 2.3 %gather_fusion = bf16[4,2,4,32,1024]{4,3,2,1,0:T(8,128)(2,1)S(1)} fusion(bf16[4,2,4,32,1024]{4,3,2,1,0:T(8,128)(2,1)} %pad_maximum_fusion.2, s32[1024]{0:T(1024)S(1)} %pad_clamp_fusion), kind=kCustom, calls=%fused_computation | custom fusion | bytes 4194320 | tf_op jit(solution)/shard_map/jit(_take)/gather | solution.py:103
  109.1 1.5 %collective-permute-start.3 = (f32[8]{0:T(128)S(1)}, f32[8]{0:T(128)S(1)}, u32[]{:S(2)}, u32[]{:S(2)}) collective-permute-start(f32[8]{0:T(128)S(1)} %dynamic_update_slice.5), channel_id=1, source_target_pairs={{0,8},{8,0},{16,24},{24,16},{1,9},{9,1},{17,25},{25,17},{2,10},{10... | collective-permute-start | bytes 104 | tf_op jit(solution)/shard_map/ppermute | solution.py:134
  110.6 2.1 %collective-permute-done.3 = f32[8]{0:T(128)S(1)} collective-permute-done((f32[8]{0:T(128)S(1)}, f32[8]{0:T(128)S(1)}, u32[]{:S(2)}, u32[]{:S(2)}) %collective-permute-start.3) | collective-permute-done | bytes 64 | tf_op jit(solution)/shard_map/ppermute | solution.py:134
  112.8 1.5 %collective-permute-start.4 = (f32[8]{0:T(128)S(1)}, f32[8]{0:T(128)S(1)}, u32[]{:S(2)}, u32[]{:S(2)}) collective-permute-start(f32[8]{0:T(128)S(1)} %add_dynamic-update-slice_fusion), channel_id=1, source_target_pairs={{0,16},{8,24},{16,0},{24,8},{1,17},{9,25},{17,1},{25,9},{2,18},{10... | collective-permute-start | bytes 104 | tf_op jit(solution)/shard_map/ppermute | solution.py:134
  114.3 2.1 %collective-permute-done.4 = f32[8]{0:T(128)S(1)} collective-permute-done((f32[8]{0:T(128)S(1)}, f32[8]{0:T(128)S(1)}, u32[]{:S(2)}, u32[]{:S(2)}) %collective-permute-start.4) | collective-permute-done | bytes 64 | tf_op jit(solution)/shard_map/ppermute | solution.py:134
  116.5 0.6 multiply_reduce_fusion
  117.1 0.4 copy-done.9
  117.5 1.1 fusion.13
  118.7 0.7 fusion.27
  119.3 0.7 multiply_add_fusion
  (71 shorter events, 3.2 us)
Async XLA Ops:
  7.2 57.4 %all-gather.2.cloned.1.call-start = ((), (), s32[]{:S(2)}) async-start(), calls=%async_computation | async-start | bytes 4718592 | tf_op jit(solution)/shard_map/all_gather | solution.py:176
  11.2 1.4 %copy-start = (bf16[32,32,1024]{2,1,0:T(8,128)(2,1)}, bf16[32,32,1024]{2,1,0:T(8,128)(2,1)S(1)}, u32[]{:S(2)}) copy-start(bf16[32,32,1024]{2,1,0:T(8,128)(2,1)S(1)} %get-tuple-element.22) | copy-start | bytes 6291460
  11.2 2.0 %copy-start.2 = (bf16[32,32,1024]{2,1,0:T(8,128)(2,1)}, bf16[32,32,1024]{2,1,0:T(8,128)(2,1)S(1)}, u32[]{:S(2)}) copy-start(bf16[32,32,1024]{2,1,0:T(8,128)(2,1)S(1)} %get-tuple-element.23) | copy-start | bytes 6291460
  13.2 1.3 %copy-start.4 = (s32[2,4,32,1024]{3,2,1,0:T(8,128)S(1)}, s32[2,4,32,1024]{3,2,1,0:T(8,128)}, u32[]{:S(2)}) copy-start(s32[2,4,32,1024]{3,2,1,0:T(8,128)} %param.9) | copy-start | bytes 3145732
  13.7 6.3 %copy-start.11 = (f32[4,8,1024]{2,1,0:T(8,128)S(1)}, f32[4,8,1024]{2,1,0:T(8,128)}, u32[]{:S(2)}) copy-start(f32[4,8,1024]{2,1,0:T(8,128)} %param.11) | copy-start | bytes 393220
  13.7 6.3 %copy-start.13 = (f32[4,8,1024]{2,1,0:T(8,128)S(1)}, f32[4,8,1024]{2,1,0:T(8,128)}, u32[]{:S(2)}) copy-start(f32[4,8,1024]{2,1,0:T(8,128)} %param.10) | copy-start | bytes 393220
  13.7 10.5 %copy-start.6 = (f32[4,32,1024]{2,1,0:T(8,128)S(1)}, f32[4,32,1024]{2,1,0:T(8,128)}, u32[]{:S(2)}) copy-start(f32[4,32,1024]{2,1,0:T(8,128)} %param.8) | copy-start | bytes 1572868
  15.5 87.6 %collective-permute-start.5 = (bf16[2,4,32,1024]{3,2,1,0:T(8,128)(2,1)}, bf16[2,4,32,1024]{3,2,1,0:T(8,128)(2,1)}, u32[]{:S(2)}, u32[]{:S(2)}) collective-permute-start(bf16[2,4,32,1024]{3,2,1,0:T(8,128)(2,1)} %add_convert_fusion), channel_id=1, source_target_pairs={{0,8},{8,16},{16,24},{24,0},{1,9},{9,17},{17,25},{25,1},{2,10},{10... | collective-permute-start | bytes 1572872 | tf_op jit(solution)/shard_map/ppermute | solution.py:99
  18.5 84.7 %collective-permute-start.6 = (bf16[2,4,32,1024]{3,2,1,0:T(8,128)(2,1)}, bf16[2,4,32,1024]{3,2,1,0:T(8,128)(2,1)}, u32[]{:S(2)}, u32[]{:S(2)}) collective-permute-start(bf16[2,4,32,1024]{3,2,1,0:T(8,128)(2,1)} %add_convert_fusion), channel_id=1, source_target_pairs={{0,16},{8,24},{16,0},{24,8},{1,17},{9,25},{17,1},{25,9},{2,18},{10... | collective-permute-start | bytes 1572872 | tf_op jit(solution)/shard_map/ppermute | solution.py:99
  20.8 17.4 %collective-permute-start.8 = (f32[2,4,8,1024]{3,2,1,0:T(8,128)}, f32[2,4,8,1024]{3,2,1,0:T(8,128)}, u32[]{:S(2)}, u32[]{:S(2)}) collective-permute-start(f32[2,4,8,1024]{3,2,1,0:T(8,128)} %get-tuple-element.25), channel_id=1, source_target_pairs={{0,8},{8,16},{16,24},{24,0},{1,9},{9,17},{17,25},{25,1},{2,10},{10... | collective-permute-start | bytes 786440 | tf_op jit(solution)/shard_map/ppermute | solution.py:99
  20.8 33.4 %collective-permute-start.9 = (f32[2,4,8,1024]{3,2,1,0:T(8,128)}, f32[2,4,8,1024]{3,2,1,0:T(8,128)}, u32[]{:S(2)}, u32[]{:S(2)}) collective-permute-start(f32[2,4,8,1024]{3,2,1,0:T(8,128)} %get-tuple-element.25), channel_id=1, source_target_pairs={{0,16},{8,24},{16,0},{24,8},{1,17},{9,25},{17,1},{25,9},{2,18},{10... | collective-permute-start | bytes 786440 | tf_op jit(solution)/shard_map/ppermute | solution.py:99
  22.8 31.4 %collective-permute-start.10 = (f32[2,4,8,1024]{3,2,1,0:T(8,128)}, f32[2,4,8,1024]{3,2,1,0:T(8,128)}, u32[]{:S(2)}, u32[]{:S(2)}) collective-permute-start(f32[2,4,8,1024]{3,2,1,0:T(8,128)} %get-tuple-element.25), channel_id=1, source_target_pairs={{0,24},{8,0},{16,8},{24,16},{1,25},{9,1},{17,9},{25,17},{2,26},{10... | collective-permute-start | bytes 786440 | tf_op jit(solution)/shard_map/ppermute | solution.py:99
  29.4 1.6 %copy-start.15 = (s32[32]{0:T(128)S(1)}, s32[32]{0:T(128)}, u32[]{:S(2)}) copy-start(s32[32]{0:T(128)} %param.7) | copy-start | bytes 388
  38.2 65.0 %collective-permute-start.7 = (bf16[2,4,32,1024]{3,2,1,0:T(8,128)(2,1)}, bf16[2,4,32,1024]{3,2,1,0:T(8,128)(2,1)}, u32[]{:S(2)}, u32[]{:S(2)}) collective-permute-start(bf16[2,4,32,1024]{3,2,1,0:T(8,128)(2,1)} %add_convert_fusion), channel_id=1, source_target_pairs={{0,24},{8,0},{16,8},{24,16},{1,25},{9,1},{17,9},{25,17},{2,26},{10... | collective-permute-start | bytes 1572872 | tf_op jit(solution)/shard_map/ppermute | solution.py:99
  64.6 25.7 %copy-start.3 = (bf16[32,32,1024]{2,1,0:T(8,128)(2,1)S(1)}, bf16[32,32,1024]{2,1,0:T(8,128)(2,1)}, u32[]{:S(2)}) copy-start(bf16[32,32,1024]{2,1,0:T(8,128)(2,1)} %copy-done.2) | copy-start | bytes 6291460
  90.3 1.6 %copy-start.1 = (bf16[32,32,1024]{2,1,0:T(8,128)(2,1)S(1)}, bf16[32,32,1024]{2,1,0:T(8,128)(2,1)}, u32[]{:S(2)}) copy-start(bf16[32,32,1024]{2,1,0:T(8,128)(2,1)} %copy-done) | copy-start | bytes 6291460
  95.9 1.5 %copy-start.5 = (f32[4,2,4,8,1024]{4,3,2,1,0:T(8,128)S(1)}, f32[4,2,4,8,1024]{4,3,2,1,0:T(8,128)}, u32[]{:S(2)}) copy-start(f32[4,2,4,8,1024]{4,3,2,1,0:T(8,128)} %gather_fusion.1) | copy-start | bytes 3145732
  97.1 6.1 %copy-start.8 = (bf16[1,2,4,32,1024]{4,3,2,1,0:T(8,128)(2,1)S(1)}, bf16[1,2,4,32,1024]{4,3,2,1,0:T(8,128)(2,1)}, u32[]{:S(2)}) copy-start(bf16[1,2,4,32,1024]{4,3,2,1,0:T(8,128)(2,1)} %fusion.70) | copy-start | bytes 1572868
  97.1 1.2 collective-permute-start
  98.3 3.7 %collective-permute-start.1 = (f32[3,4,32]{2,1,0:T(4,128)S(1)}, f32[3,4,32]{2,1,0:T(4,128)S(1)}, u32[]{:S(2)}, u32[]{:S(2)}) collective-permute-start(f32[3,4,32]{2,1,0:T(4,128)S(1)} %pad_maximum_fusion.7), channel_id=1, source_target_pairs={{0,2},{1,3},{2,0},{3,1},{4,6},{5,7},{6,4},{7,5},{8,10},{9,11},{10,... | collective-permute-start | bytes 4616 | tf_op jit(solution)/shard_map/ppermute | solution.py:115
  102.1 6.4 %collective-permute-start.2 = (f32[3,4,32]{2,1,0:T(4,128)S(1)}, f32[3,4,32]{2,1,0:T(4,128)S(1)}, u32[]{:S(2)}, u32[]{:S(2)}) collective-permute-start(f32[3,4,32]{2,1,0:T(4,128)S(1)} %pad_maximum_fusion.8), channel_id=1, source_target_pairs={{0,4},{1,5},{2,6},{3,7},{4,0},{5,1},{6,2},{7,3},{8,12},{9,13},{10,... | collective-permute-start | bytes 4616 | tf_op jit(solution)/shard_map/ppermute | solution.py:115
  108.4 8.7 %copy-start.7 = (f32[4,32,1024]{2,1,0:T(8,128)S(1)}, f32[4,32,1024]{2,1,0:T(8,128)}, u32[]{:S(2)}) copy-start(f32[4,32,1024]{2,1,0:T(8,128)} %param.8) | copy-start | bytes 1572868
  109.1 3.6 %collective-permute-start.3 = (f32[8]{0:T(128)S(1)}, f32[8]{0:T(128)S(1)}, u32[]{:S(2)}, u32[]{:S(2)}) collective-permute-start(f32[8]{0:T(128)S(1)} %dynamic_update_slice.5), channel_id=1, source_target_pairs={{0,8},{8,0},{16,24},{24,16},{1,9},{9,1},{17,25},{25,17},{2,10},{10... | collective-permute-start | bytes 104 | tf_op jit(solution)/shard_map/ppermute | solution.py:134
  112.8 3.5 %collective-permute-start.4 = (f32[8]{0:T(128)S(1)}, f32[8]{0:T(128)S(1)}, u32[]{:S(2)}, u32[]{:S(2)}) collective-permute-start(f32[8]{0:T(128)S(1)} %add_dynamic-update-slice_fusion), channel_id=1, source_target_pairs={{0,16},{8,24},{16,0},{24,8},{1,17},{9,25},{17,1},{25,9},{2,18},{10... | collective-permute-start | bytes 104 | tf_op jit(solution)/shard_map/ppermute | solution.py:134
  116.5 1.0 copy-start.9
  117.1 1.6 %copy-start.12 = (f32[4,8,1024]{2,1,0:T(8,128)S(1)}, f32[4,8,1024]{2,1,0:T(8,128)}, u32[]{:S(2)}) copy-start(f32[4,8,1024]{2,1,0:T(8,128)} %param.11) | copy-start | bytes 393220
  117.1 2.2 %copy-start.14 = (f32[4,8,1024]{2,1,0:T(8,128)S(1)}, f32[4,8,1024]{2,1,0:T(8,128)}, u32[]{:S(2)}) copy-start(f32[4,8,1024]{2,1,0:T(8,128)} %param.10) | copy-start | bytes 393220
  119.3 0.7 copy-start.10
Sparse Core Ops, SparseCore 0:
  14.7 49.8 all-gather.1

commit v5 on v4

--- a/solution.py
+++ b/solution.py
@@ -42,8 +42,13 @@
     return lax.reduce_precision(values, exponent_bits=8, mantissa_bits=7)
 
 
-def mix_kernel(s_ref, tr_ref, ti_ref, o_ref, s32_ref, *, blocks, block_len, rows, chunk, factor):
-    @pl.when((pl.program_id(0) == 0) & (pl.program_id(1) == 0))
+def mix_kernel(s_ref, *refs, blocks, block_len, rows, chunk, factor, virtual):
+    tr_refs = refs[:virtual]
+    ti_refs = refs[virtual : 2 * virtual]
+    o_ref, s32_ref = refs[2 * virtual :]
+    half_factor = 0.5 * factor
+
+    @pl.when(pl.program_id(0) == 0)
     def _():
         def convert(j, carry):
             s32_ref[j] = s_ref[j].astype(jnp.float32)
@@ -53,25 +58,35 @@
 
     for start in range(0, block_len, chunk):
         def step(j, carry):
-            acc_real, acc_imag = carry
-            t_real = tr_ref[0, 0, pl.ds(j, 1), pl.ds(start, chunk)]
-            t_imag = ti_ref[0, 0, pl.ds(j, 1), pl.ds(start, chunk)]
             s_real = s32_ref[j, :, pl.ds(start, chunk)]
             s_imag = s32_ref[j, :, pl.ds(block_len + start, chunk)]
-            acc_real = acc_real + (t_real * s_real - t_imag * s_imag)
-            acc_imag = acc_imag + (t_real * s_imag + t_imag * s_real)
-            return acc_real, acc_imag
+            out = []
+            for v in range(virtual):
+                t_real = tr_refs[v][0, pl.ds(j, 1), pl.ds(start, chunk)]
+                t_imag = ti_refs[v][0, pl.ds(j, 1), pl.ds(start, chunk)]
+                out.append(carry[2 * v] + (t_real * s_real - t_imag * s_imag))
+                out.append(carry[2 * v + 1] + (t_real * s_imag + t_imag * s_real))
+            return tuple(out)
 
         zero = jnp.zeros((rows, chunk), jnp.float32)
-        acc_real, acc_imag = lax.fori_loop(0, blocks, step, (zero, zero), unroll=4)
-        o_ref[0, 0, :, pl.ds(start, chunk)] = (acc_real * factor).astype(o_ref.dtype)
-        o_ref[0, 0, :, pl.ds(block_len + start, chunk)] = (acc_imag * factor).astype(o_ref.dtype)
+        acc = lax.fori_loop(0, blocks, step, (zero,) * (2 * virtual), unroll=2)
+        for p in range(virtual - 1):
+            for sense in range(2):
+                sign = 1.0 if sense == 0 else -1.0
+                net_real = acc[0] + sign * acc[2 + 2 * p]
+                net_imag = acc[1] + sign * acc[3 + 2 * p]
+                net = 2 * p + sense
+                o_ref[net, 0, :, pl.ds(start, chunk)] = (net_real * half_factor).astype(o_ref.dtype)
+                o_ref[net, 0, :, pl.ds(block_len + start, chunk)] = (net_imag * half_factor).astype(
+                    o_ref.dtype
+                )
 
 
 def mix(spectra_all, t_real, t_imag):
     blocks, rows, doubled = spectra_all.shape
     block_len = doubled // 2
-    nets, owned = t_real.shape[:2]
+    virtual, owned = t_real.shape[:2]
+    nets = 2 * (virtual - 1)
     kernel = functools.partial(
         mix_kernel,
         blocks=blocks,
@@ -79,19 +94,22 @@
         rows=rows,
         chunk=256,
         factor=1.0 / math.sqrt(blocks),
-    )
-    t_spec = pl.BlockSpec((1, 1, blocks, block_len), lambda n, i: (n, i, 0, 0))
+        virtual=virtual,
+    )
+    t_spec = pl.BlockSpec((1, blocks, block_len), lambda i: (i, 0, 0))
+    parts = [t_real[v] for v in range(virtual)] + [t_imag[v] for v in range(virtual)]
     return pl.pallas_call(
         kernel,
-        grid=(nets, owned),
-        in_specs=[pl.BlockSpec((blocks, rows, doubled), lambda n, i: (0, 0, 0)), t_spec, t_spec],
-        out_specs=pl.BlockSpec((1, 1, rows, doubled), lambda n, i: (n, i, 0, 0)),
+        grid=(owned,),
+        in_specs=[pl.BlockSpec((blocks, rows, doubled), lambda i: (0, 0, 0))]
+        + [t_spec] * (2 * virtual),
+        out_specs=pl.BlockSpec((nets, 1, rows, doubled), lambda i: (0, i, 0, 0)),
         out_shape=jax.ShapeDtypeStruct((nets, owned, rows, doubled), jnp.bfloat16),
         scratch_shapes=[pltpu.VMEM((blocks, rows, doubled), jnp.float32)],
         compiler_params=pltpu.CompilerParams(
-            dimension_semantics=("arbitrary", "arbitrary"), vmem_limit_bytes=48 * 1024 * 1024
+            dimension_semantics=("arbitrary",), vmem_limit_bytes=48 * 1024 * 1024
         ),
-    )(spectra_all, t_real, t_imag)
+    )(spectra_all, *parts)
 
 
 def gather_by_permutes(values, axis_name, size, index):
@@ -157,8 +175,6 @@
     all_moments = jnp.transpose(all_moments, (1, 2, 0, 3, 4)).reshape(
         (2, owned_blocks, blocks, block_len)
     )
-    all_first = all_moments[0]
-    all_second = all_moments[1]
 
     cosine, sine_part = tables(block_len)
     local_in = jnp.transpose(inputs, (1, 0, 2)).reshape(owned_blocks * row_count, doubled)
@@ -182,12 +198,17 @@
     cos_minus = to_bf16(jnp.cos(angle_minus))
     sin_minus = to_bf16(jnp.sin(angle_minus))
     up = sign_bits == 1
-    t_real = jnp.stack(
-        [jnp.where(up, cos_plus, cos_minus), jnp.where(up, cos_minus, cos_plus)], 1
-    ).reshape(net_count, owned_blocks, blocks, block_len)
-    t_imag = jnp.stack(
-        [jnp.where(up, sin_plus, sin_minus), jnp.where(up, sin_minus, sin_plus)], 1
-    ).reshape(net_count, owned_blocks, blocks, block_len)
+    cos_half = cos_plus - cos_minus
+    sin_half = sin_plus - sin_minus
+    t_real = jnp.concatenate(
+        [(cos_plus + cos_minus)[None], jnp.where(up, cos_half, -cos_half)], 0
+    )
+    t_imag = jnp.concatenate(
+        [(sin_plus + sin_minus)[None], jnp.where(up, sin_half, -sin_half)], 0
+    )
+    spectra_all, all_directions, all_moments = lax.optimization_barrier(
+        (spectra_all, all_directions, all_moments)
+    )
 
     mixed = mix(spectra_all, t_real, t_imag)
     mixed = mixed.reshape(net_count * owned_blocks * row_count, doubled)
@@ -221,6 +242,8 @@
         jnp.sum(differences[:, None, None, None] * all_directions.astype(f32), axis=0)
         / total_pairs
     )
+    all_first = all_moments[0]
+    all_second = all_moments[1]
     first_bias = 1.0 - beta_first**ADAM_STEP
     second_bias = 1.0 - beta_second**ADAM_STEP
     first_all = beta_first * all_first + (1.0 - beta_first) * estimate_all

time: 127 us -> 123 us (0.969)
  waiting for transfers between devices: 35.2 us -> 25.1 us
  other arithmetic: 21 us -> 27.7 us
  Pallas kernels: 25.7 us -> 20.8 us
  starting transfers between devices: 14.4 us -> 16.1 us
  matrix products: 7.06 us -> 8.43 us
    all_gather x1, waiting for transfers between devices: 7.64 us -> 0.42 us  [body(): spectra_all = lax.all_gather(spectra, 'feat', axis=0, tiled=True)]
    ppermute x6, waiting for transfers between devices: 20 us -> 15 us  [gather_by_permutes(): lax.ppermute(values, axis_name, [(i, (i + s) % size) for i in range(size)])]
    pallas_call x1, Pallas kernels: 25.7 us -> 20.8 us  [mix(): pl.pallas_call(kernel, grid=(owned,), in_specs=[pl.BlockSpec((blocks, row...]
    add x0 -> x1, other arithmetic: none -> 3.83 us  [body(): sin_plus + sin_minus]
    reduce_precision x1 -> x0, other arithmetic: 3.73 us -> none  [to_bf16(): return lax.reduce_precision(values, exponent_bits=8, mantissa_bits=7)]
    select_n x2, other arithmetic: 0.19 us -> 3.24 us  [gather_by_permutes(): return jnp.take(jnp.stack(parts, 0), order, axis=0)]
    gather x2, local copies, waits for them, and re-layouts: 3.86 us -> 6.45 us  [gather_by_permutes(): return jnp.take(jnp.stack(parts, 0), order, axis=0)]
    reshape x0 -> x1, other arithmetic: none -> 2.57 us  [body(): jnp.transpose(all_moments, (1, 2, 0, 3, 4))]
  transfers between devices with their start and end apart: 12 -> 12, of which waited for: 7 -> 11; matrix products, arithmetic and copies ran while one was open for 20% -> 20% of each run, Pallas kernels for 20% -> 0%
where the time goes in v5:
time: 123 us
  other arithmetic  27.7 us (23%)
  waiting for transfers between devices  25.1 us (20%)
  Pallas kernels  20.8 us (17%)
  starting transfers between devices  16.1 us (13%)
  between operations  14.3 us (12%)
  local copies, waits for them, and re-layouts  10.3 us (8%)
  matrix products  8.43 us (7%)
    pallas_call x1, Pallas kernels, mix(): pl.pallas_call(kernel, grid=(owned,), in_specs=[pl.BlockSpec((blocks, row...  20.8 us
    ppermute x6, waiting for transfers between devices, gather_by_permutes(): lax.ppermute(values, axis_name, [(i, (i + s) % size) for i in range(size)])  15 us
    ppermute x6, starting transfers between devices, gather_by_permutes(): lax.ppermute(values, axis_name, [(i, (i + s) % size) for i in range(size)])  9.08 us
    another operation x4, other arithmetic, gather_by_permutes(): return jnp.take(jnp.stack(parts, 0), order, axis=0)  7 us
    gather x2, local copies, waits for them, and re-layouts, gather_by_permutes(): return jnp.take(jnp.stack(parts, 0), order, axis=0)  6.45 us
    ppermute x3, waiting for transfers between devices, merge_stats(): packed = lax.ppermute(jnp.stack([top, total, label], 0), axis_name, perm)  5.75 us
    ppermute x2, waiting for transfers between devices, gather_small(): slots = slots + lax.ppermute(slots, axis_name, perm)  3.89 us
    add x1, other arithmetic, body(): sin_plus + sin_minus  3.83 us
  transfers between devices with their start and end apart: 12, of which 11 were waited for; matrix products, arithmetic and copies ran while one was open for 20% of the time, Pallas kernels for 0%

profile of v5, /device:TPU:0, one launch (start us, length us, event | category | flops | bytes accessed | tf_op | source)
XLA Modules:
  0.0 122.8 jit_solution(17460996155845242892)
XLA Ops:
  7.2 0.5 fusion.38
  7.8 0.6 fusion.41
  8.3 1.3 %copy.15 = bf16[32,4,2048]{2,0,1:T(8,128)(2,1)S(1)} copy(bf16[32,4,2048]{2,1,0:T(4,128)(2,1)} %param.6) | data formatting | bytes 1048576 | tf_op args[0]
  9.7 1.6 %multiply_convert_fusion = (bf16[32,32,1024]{2,1,0:T(8,128)(2,1)S(1)}, bf16[32,32,1024]{2,1,0:T(8,128)(2,1)S(1)}) fusion(f32[32,1024]{1,0:T(8,128)S(1)} %get-tuple-element.42, f32[32,1024]{1,0:T(8,128)S(1)} %get-tuple-element.39, f32[32,1024]{1,0:T(8,128)S(1)} %get-tuple-element.43, f32[32,1024]{1,0:T(8,128)S(1)} %get-tuple-element.38), kind=kLoop, calls=%fused_computation.3 | loop fusion | flops 10485760 | bytes 4718592 | tf_op jit(solution)/shard_map/convert_element_type | solution.py:37
  11.3 0.4 fusion.22
  11.7 0.4 fusion.20
  12.6 0.4 fusion
  13.2 0.4 fusion.1
  13.7 0.8 pad_maximum_fusion.2
  14.6 0.8 fusion.64
  15.4 2.9 %collective-permute-start.3 = (f32[2,4,8,1024]{3,2,1,0:T(8,128)}, f32[2,4,8,1024]{3,2,1,0:T(8,128)}, u32[]{:S(2)}, u32[]{:S(2)}) collective-permute-start(f32[2,4,8,1024]{3,2,1,0:T(8,128)} %get-tuple-element.33), channel_id=1, source_target_pairs={{0,8},{8,16},{16,24},{24,0},{1,9},{9,17},{17,25},{25,1},{2,10},{10... | collective-permute-start | bytes 786440 | tf_op jit(solution)/shard_map/ppermute | solution.py:117
  18.3 1.5 %collective-permute-start.4 = (f32[2,4,8,1024]{3,2,1,0:T(8,128)}, f32[2,4,8,1024]{3,2,1,0:T(8,128)}, u32[]{:S(2)}, u32[]{:S(2)}) collective-permute-start(f32[2,4,8,1024]{3,2,1,0:T(8,128)} %get-tuple-element.33), channel_id=1, source_target_pairs={{0,16},{8,24},{16,0},{24,8},{1,17},{9,25},{17,1},{25,9},{2,18},{10... | collective-permute-start | bytes 786440 | tf_op jit(solution)/shard_map/ppermute | solution.py:117
  19.8 1.4 %collective-permute-start.5 = (f32[2,4,8,1024]{3,2,1,0:T(8,128)}, f32[2,4,8,1024]{3,2,1,0:T(8,128)}, u32[]{:S(2)}, u32[]{:S(2)}) collective-permute-start(f32[2,4,8,1024]{3,2,1,0:T(8,128)} %get-tuple-element.33), channel_id=1, source_target_pairs={{0,24},{8,0},{16,8},{24,16},{1,25},{9,1},{17,9},{25,17},{2,26},{10... | collective-permute-start | bytes 786440 | tf_op jit(solution)/shard_map/ppermute | solution.py:117
  21.3 0.9 add_convert_fusion
  22.2 0.6 collective-permute-start
  22.8 0.5 collective-permute-start.1
  23.3 0.9 fusion.76
  24.3 3.8 %fusion.18 = (f32[4,32,1024]{2,1,0:T(8,128)S(1)}, f32[4,32,1024]{2,1,0:T(8,128)S(1)}, f32[4,32,1024]{2,1,0:T(8,128)S(1)}, f32[4,32,1024]{2,1,0:T(8,128)S(1)}, f3...) fusion(f32[4,32,1024]{2,1,0:T(8,128)S(1)} %copy-done.7), kind=kLoop, calls=%fused_computation.48 | loop fusion | flops 1572864 | bytes 3670016 | tf_op jit(solution)/shard_map/add | solution.py:207
  29.5 2.1 %collective-permute-start.2 = (bf16[2,4,32,1024]{3,2,1,0:T(8,128)(2,1)}, bf16[2,4,32,1024]{3,2,1,0:T(8,128)(2,1)}, u32[]{:S(2)}, u32[]{:S(2)}) collective-permute-start(bf16[2,4,32,1024]{3,2,1,0:T(8,128)(2,1)} %add_convert_fusion), channel_id=1, source_target_pairs={{0,24},{8,0},{16,8},{24,16},{1,25},{9,1},{17,9},{25,17},{2,26},{10... | collective-permute-start | bytes 1572872 | tf_op jit(solution)/shard_map/ppermute | solution.py:117
  31.6 0.8 collective-permute-done.4
  32.4 0.5 collective-permute-done.5
  33.0 2.3 %pad_maximum_fusion.1 = f32[4,2,4,8,1024]{4,3,2,1,0:T(8,128)} fusion(f32[1,2,4,8,1024]{4,3,2,1,0:T(8,128)} %bitcast.20, f32[1,2,4,8,1024]{4,3,2,1,0:T(8,128)} %bitcast.19, f32[1,2,4,8,1024]{4,3,2,1,0:T(8,128)} %bitcast.18, f32[1,2,4,8,1024]{4,3,2,1,0:T(8,128)S(1)} %get-tuple-element.32), kind=kLoop, calls=%fused_computation.14 | loop fusion | flops 786432 | bytes 2097152 | tf_op jit(solution)/shard_map/stack | solution.py:121
  35.2 2.8 %gather_fusion.1 = f32[4,2,4,8,1024]{4,3,2,1,0:T(8,128)} fusion(f32[4,2,4,8,1024]{4,3,2,1,0:T(8,128)} %pad_maximum_fusion.1, s32[1024]{0:T(1024)S(1)} %pad_clamp_fusion), kind=kCustom, calls=%fused_computation.1 | custom fusion | bytes 2097168 | tf_op jit(solution)/shard_map/jit(_take)/gather | solution.py:121
  38.1 2.6 %copy_bitcast_fusion = f32[2,4,32,1024]{3,2,1,0:T(8,128)} fusion(f32[4,2,4,8,1024]{4,3,2,1,0:T(8,128)} %gather_fusion.1, pred[4]{0:T(512)(128)(4,1)S(1)} %compare_and_fusion), kind=kLoop, calls=%fused_computation.15 | loop fusion | flops 262144 | bytes 2097156 | tf_op jit(solution)/shard_map/reshape | solution.py:175
  40.7 3.0 %collective-permute-done = bf16[2,4,32,1024]{3,2,1,0:T(8,128)(2,1)} collective-permute-done((bf16[2,4,32,1024]{3,2,1,0:T(8,128)(2,1)}, bf16[2,4,32,1024]{3,2,1,0:T(8,128)(2,1)}, u32[]{:S(2)}, u32[]{:S(2)}) %collective-permute-start) | collective-permute-done | bytes 524320 | tf_op jit(solution)/shard_map/ppermute | solution.py:117
  43.7 10.3 %collective-permute-done.1 = bf16[2,4,32,1024]{3,2,1,0:T(8,128)(2,1)} collective-permute-done((bf16[2,4,32,1024]{3,2,1,0:T(8,128)(2,1)}, bf16[2,4,32,1024]{3,2,1,0:T(8,128)(2,1)}, u32[]{:S(2)}, u32[]{:S(2)}) %collective-permute-start.1) | collective-permute-done | bytes 524320 | tf_op jit(solution)/shard_map/ppermute | solution.py:117
  54.3 3.0 %pad_maximum_fusion = bf16[4,2,4,32,1024]{4,3,2,1,0:T(8,128)(2,1)} fusion(bf16[1,2,4,32,1024]{4,3,2,1,0:T(8,128)(2,1)} %bitcast.12, bf16[1,2,4,32,1024]{4,3,2,1,0:T(8,128)(2,1)} %bitcast.11, bf16[1,2,4,32,1024]{4,3,2,1,0:T(8,128)(2,1)} %bitcast.10, bf16[1,2,4,32,1024]{4,3,2,1,0:T(8,128)(2,1)S(1)} %copy-done.9), kind=kLoop, calls=%fused_computation.5 | loop fusion | flops 3145728 | bytes 4194304 | tf_op jit(solution)/shard_map/stack | solution.py:121
  57.3 3.6 %gather_fusion = bf16[4,2,4,32,1024]{4,3,2,1,0:T(8,128)(2,1)} fusion(bf16[4,2,4,32,1024]{4,3,2,1,0:T(8,128)(2,1)} %pad_maximum_fusion, s32[1024]{0:T(1024)S(1)} %pad_clamp_fusion), kind=kCustom, calls=%fused_computation | custom fusion | bytes 4194320 | tf_op jit(solution)/shard_map/jit(_take)/gather | solution.py:121
  60.9 3.2 %bitcast_select_fusion = bf16[8,4,32,1024]{3,2,1,0:T(8,128)(2,1)} fusion(bf16[4,2,4,32,1024]{4,3,2,1,0:T(8,128)(2,1)} %gather_fusion, pred[8]{0:T(512)(128)(4,1)S(1)} %broadcast_in_dim.69), kind=kLoop, calls=%fused_computation.6 | loop fusion | flops 1048576 | bytes 4194312 | tf_op jit(solution)/shard_map/jit(_take)/select_n | solution.py:121
  64.6 20.8 %shard_map.93 = bf16[4,4,32,2048]{3,2,1,0:T(8,128)(2,1)S(1)} custom-call(bf16[32,32,2048]{2,1,0:T(8,128)(2,1)} %all-gather.2.cloned.1.call-done.s_ref, f32[4,32,1024]{2,1,0:T(8,128)S(1)} %get-tuple-element.28.refs_0_, f32[4,32,1024]{2,1,0:T(8,128)S(1)} %get-tuple-element.44.refs_1_, f32[4,32,1024]{2,1,0:T(8,128)S(1)} %get-tuple-element.45.refs_2_, ...), custom_call_target="tpu_custom_call" | custom-call | tf_op jit(solution)/shard_map/pallas_call | solution.py:101
  85.4 1.2 %fusion.3 = f32[512,1024]{1,0:T(8,128)S(1)} fusion(bf16[1024,1024]{1,0:T(8,128)(2,1)S(1)} %bitcast.173, bf16[512,2048]{1,0:T(8,128)(2,1)S(1)} %bitcast.163), kind=kOutput, calls=%fused_computation.19 | convolution fusion | flops 1073741824 | bytes 5242880 | tf_op jit(solution)/shard_map/dot_general | solution.py:217
  87.0 1.3 %fusion.7 = f32[512,1024]{1,0:T(8,128)S(1)} fusion(bf16[1024,1024]{1,0:T(8,128)(2,1)S(1)} %bitcast.169, bf16[512,2048]{1,0:T(8,128)(2,1)S(1)} %bitcast.164), kind=kOutput, calls=%fused_computation.23 | convolution fusion | flops 1073741824 | bytes 5242880 | tf_op jit(solution)/shard_map/dot_general | solution.py:217
  88.3 1.3 %fusion.5 = f32[512,1024]{1,0:T(8,128)S(1)} fusion(bf16[1024,1024]{1,0:T(8,128)(2,1)S(1)} %bitcast.174, bf16[512,2048]{1,0:T(8,128)(2,1)S(1)} %bitcast.165), kind=kOutput, calls=%fused_computation.21 | convolution fusion | flops 1073741824 | bytes 5242880 | tf_op jit(solution)/shard_map/dot_general | solution.py:220
  89.5 2.9 %fusion.67 = (f32[512]{0:T(512)S(1)}, f32[512,1024]{1,0:T(8,128)}) fusion(f32[512,1024]{1,0:T(8,128)S(1)} %fusion.5, bf16[1024,1024]{1,0:T(8,128)(2,1)S(1)} %bitcast.170, bf16[512,2048]{1,0:T(8,128)(2,1)S(1)} %bitcast.166, f32[512,1024]{1,0:T(8,128)S(1)} %fusion.7, f32[512,1024]{1,0:T(8,128)S(1)} %fusion.3), kind=kOutput, calls=%fused_computation.145 | convolution fusion | flops 1077411328 | bytes 11536384 | tf_op jit(solution)/shard_map/dot_general | solution.py:220
  92.6 2.4 %exponential_reduce_fusion = (f32[512]{0:T(512)S(1)}, f32[512]{0:T(512)S(1)}) fusion(f32[512,1024]{1,0:T(8,128)} %get-tuple-element.41, f32[512]{0:T(512)S(1)} %sub.121, pred[4,32,1024]{2,1,0:T(8,128)(4,1)S(1)} %broadcast_compare_fusion.1), kind=kLoop, calls=%fused_computation.8 | loop fusion | flops 2096128 | bytes 2234368 | tf_op jit(solution)/shard_map/reduce_sum | solution.py:231
  95.6 0.9 collective-permute-done.6
  96.5 1.2 collective-permute-start.7
  97.8 2.5 %collective-permute-done.7 = f32[3,4,32]{2,1,0:T(4,128)S(1)} collective-permute-done((f32[3,4,32]{2,1,0:T(4,128)S(1)}, f32[3,4,32]{2,1,0:T(4,128)S(1)}, u32[]{:S(2)}, u32[]{:S(2)}) %collective-permute-start.7) | collective-permute-done | bytes 1568 | tf_op jit(solution)/shard_map/ppermute | solution.py:133
  100.3 2.2 %collective-permute-start.8 = (f32[3,4,32]{2,1,0:T(4,128)S(1)}, f32[3,4,32]{2,1,0:T(4,128)S(1)}, u32[]{:S(2)}, u32[]{:S(2)}) collective-permute-start(f32[3,4,32]{2,1,0:T(4,128)S(1)} %pad_maximum_fusion.6), channel_id=1, source_target_pairs={{0,4},{1,5},{2,6},{3,7},{4,0},{5,1},{6,2},{7,3},{8,12},{9,13},{10,... | collective-permute-start | bytes 4616 | tf_op jit(solution)/shard_map/ppermute | solution.py:133
  102.5 2.4 %collective-permute-done.8 = f32[3,4,32]{2,1,0:T(4,128)S(1)} collective-permute-done((f32[3,4,32]{2,1,0:T(4,128)S(1)}, f32[3,4,32]{2,1,0:T(4,128)S(1)}, u32[]{:S(2)}, u32[]{:S(2)}) %collective-permute-start.8) | collective-permute-done | bytes 1568 | tf_op jit(solution)/shard_map/ppermute | solution.py:133
  105.5 1.5 %collective-permute-start.9 = (f32[8]{0:T(128)S(1)}, f32[8]{0:T(128)S(1)}, u32[]{:S(2)}, u32[]{:S(2)}) collective-permute-start(f32[8]{0:T(128)S(1)} %dynamic_update_slice.5), channel_id=1, source_target_pairs={{0,8},{8,0},{16,24},{24,16},{1,9},{9,1},{17,25},{25,17},{2,10},{10... | collective-permute-start | bytes 104 | tf_op jit(solution)/shard_map/ppermute | solution.py:152
  107.0 2.1 %collective-permute-done.9 = f32[8]{0:T(128)S(1)} collective-permute-done((f32[8]{0:T(128)S(1)}, f32[8]{0:T(128)S(1)}, u32[]{:S(2)}, u32[]{:S(2)}) %collective-permute-start.9) | collective-permute-done | bytes 64 | tf_op jit(solution)/shard_map/ppermute | solution.py:152
  109.2 1.7 %collective-permute-start.10 = (f32[8]{0:T(128)S(1)}, f32[8]{0:T(128)S(1)}, u32[]{:S(2)}, u32[]{:S(2)}) collective-permute-start(f32[8]{0:T(128)S(1)} %add_dynamic-update-slice_fusion), channel_id=1, source_target_pairs={{0,16},{8,24},{16,0},{24,8},{1,17},{9,25},{17,1},{25,9},{2,18},{10... | collective-permute-start | bytes 104 | tf_op jit(solution)/shard_map/ppermute | solution.py:152
  111.0 1.8 %collective-permute-done.10 = f32[8]{0:T(128)S(1)} collective-permute-done((f32[8]{0:T(128)S(1)}, f32[8]{0:T(128)S(1)}, u32[]{:S(2)}, u32[]{:S(2)}) %collective-permute-start.10) | collective-permute-done | bytes 64 | tf_op jit(solution)/shard_map/ppermute | solution.py:152
  112.8 0.5 multiply_reduce_fusion
  113.4 1.2 fusion.13
  114.5 0.7 fusion.31
  115.2 0.7 multiply_add_fusion
  (70 shorter events, 4.7 us)
Async XLA Ops:
  7.2 57.4 %all-gather.2.cloned.1.call-start = ((), (), s32[]{:S(2)}) async-start(), calls=%async_computation | async-start | bytes 4718592 | tf_op jit(solution)/shard_map/all_gather | solution.py:192
  11.3 1.4 %copy-start = (bf16[32,32,1024]{2,1,0:T(8,128)(2,1)}, bf16[32,32,1024]{2,1,0:T(8,128)(2,1)S(1)}, u32[]{:S(2)}) copy-start(bf16[32,32,1024]{2,1,0:T(8,128)(2,1)S(1)} %get-tuple-element.31) | copy-start | bytes 6291460
  11.3 2.0 %copy-start.2 = (bf16[32,32,1024]{2,1,0:T(8,128)(2,1)}, bf16[32,32,1024]{2,1,0:T(8,128)(2,1)S(1)}, u32[]{:S(2)}) copy-start(bf16[32,32,1024]{2,1,0:T(8,128)(2,1)S(1)} %get-tuple-element.30) | copy-start | bytes 6291460
  13.2 1.3 %copy-start.11 = (f32[4,8,1024]{2,1,0:T(8,128)S(1)}, f32[4,8,1024]{2,1,0:T(8,128)}, u32[]{:S(2)}) copy-start(f32[4,8,1024]{2,1,0:T(8,128)} %param.11) | copy-start | bytes 393220
  13.2 1.3 %copy-start.13 = (f32[4,8,1024]{2,1,0:T(8,128)S(1)}, f32[4,8,1024]{2,1,0:T(8,128)}, u32[]{:S(2)}) copy-start(f32[4,8,1024]{2,1,0:T(8,128)} %param.10) | copy-start | bytes 393220
  13.2 8.0 %copy-start.4 = (s32[2,4,32,1024]{3,2,1,0:T(8,128)S(1)}, s32[2,4,32,1024]{3,2,1,0:T(8,128)}, u32[]{:S(2)}) copy-start(s32[2,4,32,1024]{3,2,1,0:T(8,128)} %param.9) | copy-start | bytes 3145732
  14.6 9.7 %copy-start.7 = (f32[4,32,1024]{2,1,0:T(8,128)S(1)}, f32[4,32,1024]{2,1,0:T(8,128)}, u32[]{:S(2)}) copy-start(f32[4,32,1024]{2,1,0:T(8,128)} %param.8) | copy-start | bytes 1572868
  15.4 14.1 %collective-permute-start.3 = (f32[2,4,8,1024]{3,2,1,0:T(8,128)}, f32[2,4,8,1024]{3,2,1,0:T(8,128)}, u32[]{:S(2)}, u32[]{:S(2)}) collective-permute-start(f32[2,4,8,1024]{3,2,1,0:T(8,128)} %get-tuple-element.33), channel_id=1, source_target_pairs={{0,8},{8,16},{16,24},{24,0},{1,9},{9,17},{17,25},{25,1},{2,10},{10... | collective-permute-start | bytes 786440 | tf_op jit(solution)/shard_map/ppermute | solution.py:117
  18.3 14.1 %collective-permute-start.4 = (f32[2,4,8,1024]{3,2,1,0:T(8,128)}, f32[2,4,8,1024]{3,2,1,0:T(8,128)}, u32[]{:S(2)}, u32[]{:S(2)}) collective-permute-start(f32[2,4,8,1024]{3,2,1,0:T(8,128)} %get-tuple-element.33), channel_id=1, source_target_pairs={{0,16},{8,24},{16,0},{24,8},{1,17},{9,25},{17,1},{25,9},{2,18},{10... | collective-permute-start | bytes 786440 | tf_op jit(solution)/shard_map/ppermute | solution.py:117
  19.8 13.1 %collective-permute-start.5 = (f32[2,4,8,1024]{3,2,1,0:T(8,128)}, f32[2,4,8,1024]{3,2,1,0:T(8,128)}, u32[]{:S(2)}, u32[]{:S(2)}) collective-permute-start(f32[2,4,8,1024]{3,2,1,0:T(8,128)} %get-tuple-element.33), channel_id=1, source_target_pairs={{0,24},{8,0},{16,8},{24,16},{1,25},{9,1},{17,9},{25,17},{2,26},{10... | collective-permute-start | bytes 786440 | tf_op jit(solution)/shard_map/ppermute | solution.py:117
  22.2 21.5 %collective-permute-start = (bf16[2,4,32,1024]{3,2,1,0:T(8,128)(2,1)}, bf16[2,4,32,1024]{3,2,1,0:T(8,128)(2,1)}, u32[]{:S(2)}, u32[]{:S(2)}) collective-permute-start(bf16[2,4,32,1024]{3,2,1,0:T(8,128)(2,1)} %add_convert_fusion), channel_id=1, source_target_pairs={{0,8},{8,16},{16,24},{24,0},{1,9},{9,17},{17,25},{25,1},{2,10},{10... | collective-permute-start | bytes 1572872 | tf_op jit(solution)/shard_map/ppermute | solution.py:117
  22.8 31.2 %collective-permute-start.1 = (bf16[2,4,32,1024]{3,2,1,0:T(8,128)(2,1)}, bf16[2,4,32,1024]{3,2,1,0:T(8,128)(2,1)}, u32[]{:S(2)}, u32[]{:S(2)}) collective-permute-start(bf16[2,4,32,1024]{3,2,1,0:T(8,128)(2,1)} %add_convert_fusion), channel_id=1, source_target_pairs={{0,16},{8,24},{16,0},{24,8},{1,17},{9,25},{17,1},{25,9},{2,18},{10... | collective-permute-start | bytes 1572872 | tf_op jit(solution)/shard_map/ppermute | solution.py:117
  28.5 0.7 copy-start.15
  29.5 24.8 %collective-permute-start.2 = (bf16[2,4,32,1024]{3,2,1,0:T(8,128)(2,1)}, bf16[2,4,32,1024]{3,2,1,0:T(8,128)(2,1)}, u32[]{:S(2)}, u32[]{:S(2)}) collective-permute-start(bf16[2,4,32,1024]{3,2,1,0:T(8,128)(2,1)} %add_convert_fusion), channel_id=1, source_target_pairs={{0,24},{8,0},{16,8},{24,16},{1,25},{9,1},{17,9},{25,17},{2,26},{10... | collective-permute-start | bytes 1572872 | tf_op jit(solution)/shard_map/ppermute | solution.py:117
  38.1 16.2 %copy-start.9 = (bf16[1,2,4,32,1024]{4,3,2,1,0:T(8,128)(2,1)S(1)}, bf16[1,2,4,32,1024]{4,3,2,1,0:T(8,128)(2,1)}, u32[]{:S(2)}) copy-start(bf16[1,2,4,32,1024]{4,3,2,1,0:T(8,128)(2,1)} %fusion.76) | copy-start | bytes 1572868
  64.6 20.8 %copy-start.3 = (bf16[32,32,1024]{2,1,0:T(8,128)(2,1)S(1)}, bf16[32,32,1024]{2,1,0:T(8,128)(2,1)}, u32[]{:S(2)}) copy-start(bf16[32,32,1024]{2,1,0:T(8,128)(2,1)} %copy-done.2) | copy-start | bytes 6291460
  85.4 1.6 %copy-start.1 = (bf16[32,32,1024]{2,1,0:T(8,128)(2,1)S(1)}, bf16[32,32,1024]{2,1,0:T(8,128)(2,1)}, u32[]{:S(2)}) copy-start(bf16[32,32,1024]{2,1,0:T(8,128)(2,1)} %copy-done) | copy-start | bytes 6291460
  92.4 20.4 %copy-start.5 = (bf16[8,4,32,1024]{3,2,1,0:T(8,128)(2,1)S(1)}, bf16[8,4,32,1024]{3,2,1,0:T(8,128)(2,1)}, u32[]{:S(2)}) copy-start(bf16[8,4,32,1024]{3,2,1,0:T(8,128)(2,1)} %bitcast_select_fusion) | copy-start | bytes 6291460
  92.6 20.7 %copy-start.6 = (f32[2,4,32,1024]{3,2,1,0:T(8,128)S(1)}, f32[2,4,32,1024]{3,2,1,0:T(8,128)}, u32[]{:S(2)}) copy-start(f32[2,4,32,1024]{3,2,1,0:T(8,128)} %copy_bitcast_fusion) | copy-start | bytes 3145732
  95.3 1.2 %collective-permute-start.6 = (f32[3,4,32]{2,1,0:T(4,128)S(1)}, f32[3,4,32]{2,1,0:T(4,128)S(1)}, u32[]{:S(2)}, u32[]{:S(2)}) collective-permute-start(f32[3,4,32]{2,1,0:T(4,128)S(1)} %pad_maximum_fusion.4), channel_id=1, source_target_pairs={{0,1},{1,0},{2,3},{3,2},{4,5},{5,4},{6,7},{7,6},{8,9},{9,8},{10,11... | collective-permute-start | bytes 4616 | tf_op jit(solution)/shard_map/ppermute | solution.py:133
  96.5 3.7 %collective-permute-start.7 = (f32[3,4,32]{2,1,0:T(4,128)S(1)}, f32[3,4,32]{2,1,0:T(4,128)S(1)}, u32[]{:S(2)}, u32[]{:S(2)}) collective-permute-start(f32[3,4,32]{2,1,0:T(4,128)S(1)} %pad_maximum_fusion.5), channel_id=1, source_target_pairs={{0,2},{1,3},{2,0},{3,1},{4,6},{5,7},{6,4},{7,5},{8,10},{9,11},{10,... | collective-permute-start | bytes 4616 | tf_op jit(solution)/shard_map/ppermute | solution.py:133
  100.3 4.6 %collective-permute-start.8 = (f32[3,4,32]{2,1,0:T(4,128)S(1)}, f32[3,4,32]{2,1,0:T(4,128)S(1)}, u32[]{:S(2)}, u32[]{:S(2)}) collective-permute-start(f32[3,4,32]{2,1,0:T(4,128)S(1)} %pad_maximum_fusion.6), channel_id=1, source_target_pairs={{0,4},{1,5},{2,6},{3,7},{4,0},{5,1},{6,2},{7,3},{8,12},{9,13},{10,... | collective-permute-start | bytes 4616 | tf_op jit(solution)/shard_map/ppermute | solution.py:133
  105.5 7.8 %copy-start.8 = (f32[4,32,1024]{2,1,0:T(8,128)S(1)}, f32[4,32,1024]{2,1,0:T(8,128)}, u32[]{:S(2)}) copy-start(f32[4,32,1024]{2,1,0:T(8,128)} %param.8) | copy-start | bytes 1572868
  105.5 3.6 %collective-permute-start.9 = (f32[8]{0:T(128)S(1)}, f32[8]{0:T(128)S(1)}, u32[]{:S(2)}, u32[]{:S(2)}) collective-permute-start(f32[8]{0:T(128)S(1)} %dynamic_update_slice.5), channel_id=1, source_target_pairs={{0,8},{8,0},{16,24},{24,16},{1,9},{9,1},{17,25},{25,17},{2,10},{10... | collective-permute-start | bytes 104 | tf_op jit(solution)/shard_map/ppermute | solution.py:152
  109.2 3.5 %collective-permute-start.10 = (f32[8]{0:T(128)S(1)}, f32[8]{0:T(128)S(1)}, u32[]{:S(2)}, u32[]{:S(2)}) collective-permute-start(f32[8]{0:T(128)S(1)} %add_dynamic-update-slice_fusion), channel_id=1, source_target_pairs={{0,16},{8,24},{16,0},{24,8},{1,17},{9,25},{17,1},{25,9},{2,18},{10... | collective-permute-start | bytes 104 | tf_op jit(solution)/shard_map/ppermute | solution.py:152
  113.3 1.2 copy-start.12
  113.3 1.9 %copy-start.14 = (f32[4,8,1024]{2,1,0:T(8,128)S(1)}, f32[4,8,1024]{2,1,0:T(8,128)}, u32[]{:S(2)}) copy-start(f32[4,8,1024]{2,1,0:T(8,128)} %param.10) | copy-start | bytes 393220
  115.2 0.7 copy-start.10
Sparse Core Ops, SparseCore 0:
  14.7 49.8 all-gather.1

commit v6 on v5

--- a/solution.py
+++ b/solution.py
@@ -69,7 +69,7 @@
             return tuple(out)
 
         zero = jnp.zeros((rows, chunk), jnp.float32)
-        acc = lax.fori_loop(0, blocks, step, (zero,) * (2 * virtual), unroll=2)
+        acc = lax.fori_loop(0, blocks, step, (zero,) * (2 * virtual), unroll=8)
         for p in range(virtual - 1):
             for sense in range(2):
                 sign = 1.0 if sense == 0 else -1.0

time: 123 us -> 121 us (0.984)
  Pallas kernels: 20.8 us -> 18.5 us
    pallas_call x1, Pallas kernels: 20.8 us -> 18.5 us  [mix(): pl.pallas_call(kernel, grid=(owned,), in_specs=[pl.BlockSpec((blocks, row...]
  transfers between devices with their start and end apart: 12 -> 12, of which waited for: 11 -> 11; matrix products, arithmetic and copies ran while one was open for 20% -> 21% of each run, Pallas kernels for 0% -> 0%
where the time goes in v6:
time: 121 us; the launch traced here: 120 us
  other arithmetic  27.7 us (23%)
  waiting for transfers between devices  25.1 us (21%)
  Pallas kernels  18.5 us (15%)
  starting transfers between devices  16.1 us (13%)
  between operations  14.3 us (12%)
  local copies, waits for them, and re-layouts  10.3 us (9%)
  matrix products  8.44 us (7%)
    pallas_call x1, Pallas kernels, mix(): pl.pallas_call(kernel, grid=(owned,), in_specs=[pl.BlockSpec((blocks, row...  18.5 us
    ppermute x6, waiting for transfers between devices, gather_by_permutes(): lax.ppermute(values, axis_name, [(i, (i + s) % size) for i in range(size)])  15 us
    ppermute x6, starting transfers between devices, gather_by_permutes(): lax.ppermute(values, axis_name, [(i, (i + s) % size) for i in range(size)])  9.08 us
    another operation x4, other arithmetic, gather_by_permutes(): return jnp.take(jnp.stack(parts, 0), order, axis=0)  7 us
    gather x2, local copies, waits for them, and re-layouts, gather_by_permutes(): return jnp.take(jnp.stack(parts, 0), order, axis=0)  6.45 us
    ppermute x3, waiting for transfers between devices, merge_stats(): packed = lax.ppermute(jnp.stack([top, total, label], 0), axis_name, perm)  5.76 us
    ppermute x2, waiting for transfers between devices, gather_small(): slots = slots + lax.ppermute(slots, axis_name, perm)  3.9 us
    add x1, other arithmetic, body(): sin_plus + sin_minus  3.83 us
  transfers between devices with their start and end apart: 12, of which 11 were waited for; matrix products, arithmetic and copies ran while one was open for 21% of the time, Pallas kernels for 0%

profile of v6, /device:TPU:0, one launch (start us, length us, event | category | flops | bytes accessed | tf_op | source)
XLA Modules:
  0.0 120.4 jit_solution(10578809475185451725)
XLA Ops:
  7.2 0.5 fusion.38
  7.8 0.6 fusion.41
  8.3 1.3 %copy.15 = bf16[32,4,2048]{2,0,1:T(8,128)(2,1)S(1)} copy(bf16[32,4,2048]{2,1,0:T(4,128)(2,1)} %param.6) | data formatting | bytes 1048576 | tf_op args[0]
  9.7 1.6 %multiply_convert_fusion = (bf16[32,32,1024]{2,1,0:T(8,128)(2,1)S(1)}, bf16[32,32,1024]{2,1,0:T(8,128)(2,1)S(1)}) fusion(f32[32,1024]{1,0:T(8,128)S(1)} %get-tuple-element.42, f32[32,1024]{1,0:T(8,128)S(1)} %get-tuple-element.39, f32[32,1024]{1,0:T(8,128)S(1)} %get-tuple-element.43, f32[32,1024]{1,0:T(8,128)S(1)} %get-tuple-element.38), kind=kLoop, calls=%fused_computation.3 | loop fusion | flops 10485760 | bytes 4718592 | tf_op jit(solution)/shard_map/convert_element_type | solution.py:37
  11.3 0.4 fusion.22
  11.7 0.4 fusion.20
  12.6 0.4 fusion
  13.2 0.4 fusion.1
  13.7 0.8 pad_maximum_fusion.2
  14.6 0.8 fusion.64
  15.4 2.9 %collective-permute-start.3 = (f32[2,4,8,1024]{3,2,1,0:T(8,128)}, f32[2,4,8,1024]{3,2,1,0:T(8,128)}, u32[]{:S(2)}, u32[]{:S(2)}) collective-permute-start(f32[2,4,8,1024]{3,2,1,0:T(8,128)} %get-tuple-element.33), channel_id=1, source_target_pairs={{0,8},{8,16},{16,24},{24,0},{1,9},{9,17},{17,25},{25,1},{2,10},{10... | collective-permute-start | bytes 786440 | tf_op jit(solution)/shard_map/ppermute | solution.py:117
  18.3 1.5 %collective-permute-start.4 = (f32[2,4,8,1024]{3,2,1,0:T(8,128)}, f32[2,4,8,1024]{3,2,1,0:T(8,128)}, u32[]{:S(2)}, u32[]{:S(2)}) collective-permute-start(f32[2,4,8,1024]{3,2,1,0:T(8,128)} %get-tuple-element.33), channel_id=1, source_target_pairs={{0,16},{8,24},{16,0},{24,8},{1,17},{9,25},{17,1},{25,9},{2,18},{10... | collective-permute-start | bytes 786440 | tf_op jit(solution)/shard_map/ppermute | solution.py:117
  19.8 1.4 %collective-permute-start.5 = (f32[2,4,8,1024]{3,2,1,0:T(8,128)}, f32[2,4,8,1024]{3,2,1,0:T(8,128)}, u32[]{:S(2)}, u32[]{:S(2)}) collective-permute-start(f32[2,4,8,1024]{3,2,1,0:T(8,128)} %get-tuple-element.33), channel_id=1, source_target_pairs={{0,24},{8,0},{16,8},{24,16},{1,25},{9,1},{17,9},{25,17},{2,26},{10... | collective-permute-start | bytes 786440 | tf_op jit(solution)/shard_map/ppermute | solution.py:117
  21.3 0.9 add_convert_fusion
  22.2 0.6 collective-permute-start
  22.8 0.5 collective-permute-start.1
  23.3 0.9 fusion.76
  24.3 3.8 %fusion.18 = (f32[4,32,1024]{2,1,0:T(8,128)S(1)}, f32[4,32,1024]{2,1,0:T(8,128)S(1)}, f32[4,32,1024]{2,1,0:T(8,128)S(1)}, f32[4,32,1024]{2,1,0:T(8,128)S(1)}, f3...) fusion(f32[4,32,1024]{2,1,0:T(8,128)S(1)} %copy-done.7), kind=kLoop, calls=%fused_computation.48 | loop fusion | flops 1572864 | bytes 3670016 | tf_op jit(solution)/shard_map/add | solution.py:207
  29.5 2.1 %collective-permute-start.2 = (bf16[2,4,32,1024]{3,2,1,0:T(8,128)(2,1)}, bf16[2,4,32,1024]{3,2,1,0:T(8,128)(2,1)}, u32[]{:S(2)}, u32[]{:S(2)}) collective-permute-start(bf16[2,4,32,1024]{3,2,1,0:T(8,128)(2,1)} %add_convert_fusion), channel_id=1, source_target_pairs={{0,24},{8,0},{16,8},{24,16},{1,25},{9,1},{17,9},{25,17},{2,26},{10... | collective-permute-start | bytes 1572872 | tf_op jit(solution)/shard_map/ppermute | solution.py:117
  31.6 0.8 collective-permute-done.4
  32.4 0.5 collective-permute-done.5
  33.0 2.3 %pad_maximum_fusion.1 = f32[4,2,4,8,1024]{4,3,2,1,0:T(8,128)} fusion(f32[1,2,4,8,1024]{4,3,2,1,0:T(8,128)} %bitcast.20, f32[1,2,4,8,1024]{4,3,2,1,0:T(8,128)} %bitcast.19, f32[1,2,4,8,1024]{4,3,2,1,0:T(8,128)} %bitcast.18, f32[1,2,4,8,1024]{4,3,2,1,0:T(8,128)S(1)} %get-tuple-element.32), kind=kLoop, calls=%fused_computation.14 | loop fusion | flops 786432 | bytes 2097152 | tf_op jit(solution)/shard_map/stack | solution.py:121
  35.2 2.8 %gather_fusion.1 = f32[4,2,4,8,1024]{4,3,2,1,0:T(8,128)} fusion(f32[4,2,4,8,1024]{4,3,2,1,0:T(8,128)} %pad_maximum_fusion.1, s32[1024]{0:T(1024)S(1)} %pad_clamp_fusion), kind=kCustom, calls=%fused_computation.1 | custom fusion | bytes 2097168 | tf_op jit(solution)/shard_map/jit(_take)/gather | solution.py:121
  38.1 2.6 %copy_bitcast_fusion = f32[2,4,32,1024]{3,2,1,0:T(8,128)} fusion(f32[4,2,4,8,1024]{4,3,2,1,0:T(8,128)} %gather_fusion.1, pred[4]{0:T(512)(128)(4,1)S(1)} %compare_and_fusion), kind=kLoop, calls=%fused_computation.15 | loop fusion | flops 262144 | bytes 2097156 | tf_op jit(solution)/shard_map/reshape | solution.py:175
  40.7 3.0 %collective-permute-done = bf16[2,4,32,1024]{3,2,1,0:T(8,128)(2,1)} collective-permute-done((bf16[2,4,32,1024]{3,2,1,0:T(8,128)(2,1)}, bf16[2,4,32,1024]{3,2,1,0:T(8,128)(2,1)}, u32[]{:S(2)}, u32[]{:S(2)}) %collective-permute-start) | collective-permute-done | bytes 524320 | tf_op jit(solution)/shard_map/ppermute | solution.py:117
  43.7 10.3 %collective-permute-done.1 = bf16[2,4,32,1024]{3,2,1,0:T(8,128)(2,1)} collective-permute-done((bf16[2,4,32,1024]{3,2,1,0:T(8,128)(2,1)}, bf16[2,4,32,1024]{3,2,1,0:T(8,128)(2,1)}, u32[]{:S(2)}, u32[]{:S(2)}) %collective-permute-start.1) | collective-permute-done | bytes 524320 | tf_op jit(solution)/shard_map/ppermute | solution.py:117
  54.3 3.0 %pad_maximum_fusion = bf16[4,2,4,32,1024]{4,3,2,1,0:T(8,128)(2,1)} fusion(bf16[1,2,4,32,1024]{4,3,2,1,0:T(8,128)(2,1)} %bitcast.12, bf16[1,2,4,32,1024]{4,3,2,1,0:T(8,128)(2,1)} %bitcast.11, bf16[1,2,4,32,1024]{4,3,2,1,0:T(8,128)(2,1)} %bitcast.10, bf16[1,2,4,32,1024]{4,3,2,1,0:T(8,128)(2,1)S(1)} %copy-done.9), kind=kLoop, calls=%fused_computation.5 | loop fusion | flops 3145728 | bytes 4194304 | tf_op jit(solution)/shard_map/stack | solution.py:121
  57.3 3.6 %gather_fusion = bf16[4,2,4,32,1024]{4,3,2,1,0:T(8,128)(2,1)} fusion(bf16[4,2,4,32,1024]{4,3,2,1,0:T(8,128)(2,1)} %pad_maximum_fusion, s32[1024]{0:T(1024)S(1)} %pad_clamp_fusion), kind=kCustom, calls=%fused_computation | custom fusion | bytes 4194320 | tf_op jit(solution)/shard_map/jit(_take)/gather | solution.py:121
  60.9 3.2 %bitcast_select_fusion = bf16[8,4,32,1024]{3,2,1,0:T(8,128)(2,1)} fusion(bf16[4,2,4,32,1024]{4,3,2,1,0:T(8,128)(2,1)} %gather_fusion, pred[8]{0:T(512)(128)(4,1)S(1)} %broadcast_in_dim.69), kind=kLoop, calls=%fused_computation.6 | loop fusion | flops 1048576 | bytes 4194312 | tf_op jit(solution)/shard_map/jit(_take)/select_n | solution.py:121
  64.6 18.5 %shard_map.93 = bf16[4,4,32,2048]{3,2,1,0:T(8,128)(2,1)S(1)} custom-call(bf16[32,32,2048]{2,1,0:T(8,128)(2,1)} %all-gather.2.cloned.1.call-done.s_ref, f32[4,32,1024]{2,1,0:T(8,128)S(1)} %get-tuple-element.28.refs_0_, f32[4,32,1024]{2,1,0:T(8,128)S(1)} %get-tuple-element.44.refs_1_, f32[4,32,1024]{2,1,0:T(8,128)S(1)} %get-tuple-element.45.refs_2_, ...), custom_call_target="tpu_custom_call" | custom-call | tf_op jit(solution)/shard_map/pallas_call | solution.py:101
  83.1 1.3 %fusion.3 = f32[512,1024]{1,0:T(8,128)S(1)} fusion(bf16[1024,1024]{1,0:T(8,128)(2,1)S(1)} %bitcast.173, bf16[512,2048]{1,0:T(8,128)(2,1)S(1)} %bitcast.163), kind=kOutput, calls=%fused_computation.19 | convolution fusion | flops 1073741824 | bytes 5242880 | tf_op jit(solution)/shard_map/dot_general | solution.py:217
  84.7 1.3 %fusion.7 = f32[512,1024]{1,0:T(8,128)S(1)} fusion(bf16[1024,1024]{1,0:T(8,128)(2,1)S(1)} %bitcast.169, bf16[512,2048]{1,0:T(8,128)(2,1)S(1)} %bitcast.164), kind=kOutput, calls=%fused_computation.23 | convolution fusion | flops 1073741824 | bytes 5242880 | tf_op jit(solution)/shard_map/dot_general | solution.py:217
  85.9 1.3 %fusion.5 = f32[512,1024]{1,0:T(8,128)S(1)} fusion(bf16[1024,1024]{1,0:T(8,128)(2,1)S(1)} %bitcast.174, bf16[512,2048]{1,0:T(8,128)(2,1)S(1)} %bitcast.165), kind=kOutput, calls=%fused_computation.21 | convolution fusion | flops 1073741824 | bytes 5242880 | tf_op jit(solution)/shard_map/dot_general | solution.py:220
  87.2 2.9 %fusion.67 = (f32[512]{0:T(512)S(1)}, f32[512,1024]{1,0:T(8,128)}) fusion(f32[512,1024]{1,0:T(8,128)S(1)} %fusion.5, bf16[1024,1024]{1,0:T(8,128)(2,1)S(1)} %bitcast.170, bf16[512,2048]{1,0:T(8,128)(2,1)S(1)} %bitcast.166, f32[512,1024]{1,0:T(8,128)S(1)} %fusion.7, f32[512,1024]{1,0:T(8,128)S(1)} %fusion.3), kind=kOutput, calls=%fused_computation.145 | convolution fusion | flops 1077411328 | bytes 11536384 | tf_op jit(solution)/shard_map/dot_general | solution.py:220
  90.3 2.4 %exponential_reduce_fusion = (f32[512]{0:T(512)S(1)}, f32[512]{0:T(512)S(1)}) fusion(f32[512,1024]{1,0:T(8,128)} %get-tuple-element.41, f32[512]{0:T(512)S(1)} %sub.121, pred[4,32,1024]{2,1,0:T(8,128)(4,1)S(1)} %broadcast_compare_fusion.1), kind=kLoop, calls=%fused_computation.8 | loop fusion | flops 2096128 | bytes 2234368 | tf_op jit(solution)/shard_map/reduce_sum | solution.py:231
  93.2 0.9 collective-permute-done.6
  94.2 1.2 %collective-permute-start.7 = (f32[3,4,32]{2,1,0:T(4,128)S(1)}, f32[3,4,32]{2,1,0:T(4,128)S(1)}, u32[]{:S(2)}, u32[]{:S(2)}) collective-permute-start(f32[3,4,32]{2,1,0:T(4,128)S(1)} %pad_maximum_fusion.5), channel_id=1, source_target_pairs={{0,2},{1,3},{2,0},{3,1},{4,6},{5,7},{6,4},{7,5},{8,10},{9,11},{10,... | collective-permute-start | bytes 4616 | tf_op jit(solution)/shard_map/ppermute | solution.py:133
  95.4 2.5 %collective-permute-done.7 = f32[3,4,32]{2,1,0:T(4,128)S(1)} collective-permute-done((f32[3,4,32]{2,1,0:T(4,128)S(1)}, f32[3,4,32]{2,1,0:T(4,128)S(1)}, u32[]{:S(2)}, u32[]{:S(2)}) %collective-permute-start.7) | collective-permute-done | bytes 1568 | tf_op jit(solution)/shard_map/ppermute | solution.py:133
  97.9 2.2 %collective-permute-start.8 = (f32[3,4,32]{2,1,0:T(4,128)S(1)}, f32[3,4,32]{2,1,0:T(4,128)S(1)}, u32[]{:S(2)}, u32[]{:S(2)}) collective-permute-start(f32[3,4,32]{2,1,0:T(4,128)S(1)} %pad_maximum_fusion.6), channel_id=1, source_target_pairs={{0,4},{1,5},{2,6},{3,7},{4,0},{5,1},{6,2},{7,3},{8,12},{9,13},{10,... | collective-permute-start | bytes 4616 | tf_op jit(solution)/shard_map/ppermute | solution.py:133
  100.2 2.4 %collective-permute-done.8 = f32[3,4,32]{2,1,0:T(4,128)S(1)} collective-permute-done((f32[3,4,32]{2,1,0:T(4,128)S(1)}, f32[3,4,32]{2,1,0:T(4,128)S(1)}, u32[]{:S(2)}, u32[]{:S(2)}) %collective-permute-start.8) | collective-permute-done | bytes 1568 | tf_op jit(solution)/shard_map/ppermute | solution.py:133
  103.2 1.5 %collective-permute-start.9 = (f32[8]{0:T(128)S(1)}, f32[8]{0:T(128)S(1)}, u32[]{:S(2)}, u32[]{:S(2)}) collective-permute-start(f32[8]{0:T(128)S(1)} %dynamic_update_slice.5), channel_id=1, source_target_pairs={{0,8},{8,0},{16,24},{24,16},{1,9},{9,1},{17,25},{25,17},{2,10},{10... | collective-permute-start | bytes 104 | tf_op jit(solution)/shard_map/ppermute | solution.py:152
  104.7 2.1 %collective-permute-done.9 = f32[8]{0:T(128)S(1)} collective-permute-done((f32[8]{0:T(128)S(1)}, f32[8]{0:T(128)S(1)}, u32[]{:S(2)}, u32[]{:S(2)}) %collective-permute-start.9) | collective-permute-done | bytes 64 | tf_op jit(solution)/shard_map/ppermute | solution.py:152
  106.9 1.7 %collective-permute-start.10 = (f32[8]{0:T(128)S(1)}, f32[8]{0:T(128)S(1)}, u32[]{:S(2)}, u32[]{:S(2)}) collective-permute-start(f32[8]{0:T(128)S(1)} %add_dynamic-update-slice_fusion), channel_id=1, source_target_pairs={{0,16},{8,24},{16,0},{24,8},{1,17},{9,25},{17,1},{25,9},{2,18},{10... | collective-permute-start | bytes 104 | tf_op jit(solution)/shard_map/ppermute | solution.py:152
  108.6 1.8 %collective-permute-done.10 = f32[8]{0:T(128)S(1)} collective-permute-done((f32[8]{0:T(128)S(1)}, f32[8]{0:T(128)S(1)}, u32[]{:S(2)}, u32[]{:S(2)}) %collective-permute-start.10) | collective-permute-done | bytes 64 | tf_op jit(solution)/shard_map/ppermute | solution.py:152
  110.5 0.5 multiply_reduce_fusion
  111.0 1.2 fusion.13
  112.2 0.7 fusion.31
  112.9 0.7 multiply_add_fusion
  (70 shorter events, 4.7 us)
Async XLA Ops:
  7.2 57.4 %all-gather.2.cloned.1.call-start = ((), (), s32[]{:S(2)}) async-start(), calls=%async_computation | async-start | bytes 4718592 | tf_op jit(solution)/shard_map/all_gather | solution.py:192
  11.3 1.4 %copy-start = (bf16[32,32,1024]{2,1,0:T(8,128)(2,1)}, bf16[32,32,1024]{2,1,0:T(8,128)(2,1)S(1)}, u32[]{:S(2)}) copy-start(bf16[32,32,1024]{2,1,0:T(8,128)(2,1)S(1)} %get-tuple-element.31) | copy-start | bytes 6291460
  11.3 2.0 %copy-start.2 = (bf16[32,32,1024]{2,1,0:T(8,128)(2,1)}, bf16[32,32,1024]{2,1,0:T(8,128)(2,1)S(1)}, u32[]{:S(2)}) copy-start(bf16[32,32,1024]{2,1,0:T(8,128)(2,1)S(1)} %get-tuple-element.30) | copy-start | bytes 6291460
  13.2 1.3 %copy-start.11 = (f32[4,8,1024]{2,1,0:T(8,128)S(1)}, f32[4,8,1024]{2,1,0:T(8,128)}, u32[]{:S(2)}) copy-start(f32[4,8,1024]{2,1,0:T(8,128)} %param.11) | copy-start | bytes 393220
  13.2 1.3 %copy-start.13 = (f32[4,8,1024]{2,1,0:T(8,128)S(1)}, f32[4,8,1024]{2,1,0:T(8,128)}, u32[]{:S(2)}) copy-start(f32[4,8,1024]{2,1,0:T(8,128)} %param.10) | copy-start | bytes 393220
  13.2 8.0 %copy-start.4 = (s32[2,4,32,1024]{3,2,1,0:T(8,128)S(1)}, s32[2,4,32,1024]{3,2,1,0:T(8,128)}, u32[]{:S(2)}) copy-start(s32[2,4,32,1024]{3,2,1,0:T(8,128)} %param.9) | copy-start | bytes 3145732
  14.6 9.7 %copy-start.7 = (f32[4,32,1024]{2,1,0:T(8,128)S(1)}, f32[4,32,1024]{2,1,0:T(8,128)}, u32[]{:S(2)}) copy-start(f32[4,32,1024]{2,1,0:T(8,128)} %param.8) | copy-start | bytes 1572868
  15.4 14.1 %collective-permute-start.3 = (f32[2,4,8,1024]{3,2,1,0:T(8,128)}, f32[2,4,8,1024]{3,2,1,0:T(8,128)}, u32[]{:S(2)}, u32[]{:S(2)}) collective-permute-start(f32[2,4,8,1024]{3,2,1,0:T(8,128)} %get-tuple-element.33), channel_id=1, source_target_pairs={{0,8},{8,16},{16,24},{24,0},{1,9},{9,17},{17,25},{25,1},{2,10},{10... | collective-permute-start | bytes 786440 | tf_op jit(solution)/shard_map/ppermute | solution.py:117
  18.3 14.1 %collective-permute-start.4 = (f32[2,4,8,1024]{3,2,1,0:T(8,128)}, f32[2,4,8,1024]{3,2,1,0:T(8,128)}, u32[]{:S(2)}, u32[]{:S(2)}) collective-permute-start(f32[2,4,8,1024]{3,2,1,0:T(8,128)} %get-tuple-element.33), channel_id=1, source_target_pairs={{0,16},{8,24},{16,0},{24,8},{1,17},{9,25},{17,1},{25,9},{2,18},{10... | collective-permute-start | bytes 786440 | tf_op jit(solution)/shard_map/ppermute | solution.py:117
  19.8 13.1 %collective-permute-start.5 = (f32[2,4,8,1024]{3,2,1,0:T(8,128)}, f32[2,4,8,1024]{3,2,1,0:T(8,128)}, u32[]{:S(2)}, u32[]{:S(2)}) collective-permute-start(f32[2,4,8,1024]{3,2,1,0:T(8,128)} %get-tuple-element.33), channel_id=1, source_target_pairs={{0,24},{8,0},{16,8},{24,16},{1,25},{9,1},{17,9},{25,17},{2,26},{10... | collective-permute-start | bytes 786440 | tf_op jit(solution)/shard_map/ppermute | solution.py:117
  22.2 21.5 %collective-permute-start = (bf16[2,4,32,1024]{3,2,1,0:T(8,128)(2,1)}, bf16[2,4,32,1024]{3,2,1,0:T(8,128)(2,1)}, u32[]{:S(2)}, u32[]{:S(2)}) collective-permute-start(bf16[2,4,32,1024]{3,2,1,0:T(8,128)(2,1)} %add_convert_fusion), channel_id=1, source_target_pairs={{0,8},{8,16},{16,24},{24,0},{1,9},{9,17},{17,25},{25,1},{2,10},{10... | collective-permute-start | bytes 1572872 | tf_op jit(solution)/shard_map/ppermute | solution.py:117
  22.8 31.2 %collective-permute-start.1 = (bf16[2,4,32,1024]{3,2,1,0:T(8,128)(2,1)}, bf16[2,4,32,1024]{3,2,1,0:T(8,128)(2,1)}, u32[]{:S(2)}, u32[]{:S(2)}) collective-permute-start(bf16[2,4,32,1024]{3,2,1,0:T(8,128)(2,1)} %add_convert_fusion), channel_id=1, source_target_pairs={{0,16},{8,24},{16,0},{24,8},{1,17},{9,25},{17,1},{25,9},{2,18},{10... | collective-permute-start | bytes 1572872 | tf_op jit(solution)/shard_map/ppermute | solution.py:117
  28.5 0.7 copy-start.15
  29.5 24.8 %collective-permute-start.2 = (bf16[2,4,32,1024]{3,2,1,0:T(8,128)(2,1)}, bf16[2,4,32,1024]{3,2,1,0:T(8,128)(2,1)}, u32[]{:S(2)}, u32[]{:S(2)}) collective-permute-start(bf16[2,4,32,1024]{3,2,1,0:T(8,128)(2,1)} %add_convert_fusion), channel_id=1, source_target_pairs={{0,24},{8,0},{16,8},{24,16},{1,25},{9,1},{17,9},{25,17},{2,26},{10... | collective-permute-start | bytes 1572872 | tf_op jit(solution)/shard_map/ppermute | solution.py:117
  38.1 16.2 %copy-start.9 = (bf16[1,2,4,32,1024]{4,3,2,1,0:T(8,128)(2,1)S(1)}, bf16[1,2,4,32,1024]{4,3,2,1,0:T(8,128)(2,1)}, u32[]{:S(2)}) copy-start(bf16[1,2,4,32,1024]{4,3,2,1,0:T(8,128)(2,1)} %fusion.76) | copy-start | bytes 1572868
  64.6 18.5 %copy-start.3 = (bf16[32,32,1024]{2,1,0:T(8,128)(2,1)S(1)}, bf16[32,32,1024]{2,1,0:T(8,128)(2,1)}, u32[]{:S(2)}) copy-start(bf16[32,32,1024]{2,1,0:T(8,128)(2,1)} %copy-done.2) | copy-start | bytes 6291460
  83.1 1.6 %copy-start.1 = (bf16[32,32,1024]{2,1,0:T(8,128)(2,1)S(1)}, bf16[32,32,1024]{2,1,0:T(8,128)(2,1)}, u32[]{:S(2)}) copy-start(bf16[32,32,1024]{2,1,0:T(8,128)(2,1)} %copy-done) | copy-start | bytes 6291460
  90.1 20.4 %copy-start.5 = (bf16[8,4,32,1024]{3,2,1,0:T(8,128)(2,1)S(1)}, bf16[8,4,32,1024]{3,2,1,0:T(8,128)(2,1)}, u32[]{:S(2)}) copy-start(bf16[8,4,32,1024]{3,2,1,0:T(8,128)(2,1)} %bitcast_select_fusion) | copy-start | bytes 6291460
  90.3 20.7 %copy-start.6 = (f32[2,4,32,1024]{3,2,1,0:T(8,128)S(1)}, f32[2,4,32,1024]{3,2,1,0:T(8,128)}, u32[]{:S(2)}) copy-start(f32[2,4,32,1024]{3,2,1,0:T(8,128)} %copy_bitcast_fusion) | copy-start | bytes 3145732
  92.9 1.2 %collective-permute-start.6 = (f32[3,4,32]{2,1,0:T(4,128)S(1)}, f32[3,4,32]{2,1,0:T(4,128)S(1)}, u32[]{:S(2)}, u32[]{:S(2)}) collective-permute-start(f32[3,4,32]{2,1,0:T(4,128)S(1)} %pad_maximum_fusion.4), channel_id=1, source_target_pairs={{0,1},{1,0},{2,3},{3,2},{4,5},{5,4},{6,7},{7,6},{8,9},{9,8},{10,11... | collective-permute-start | bytes 4616 | tf_op jit(solution)/shard_map/ppermute | solution.py:133
  94.2 3.7 %collective-permute-start.7 = (f32[3,4,32]{2,1,0:T(4,128)S(1)}, f32[3,4,32]{2,1,0:T(4,128)S(1)}, u32[]{:S(2)}, u32[]{:S(2)}) collective-permute-start(f32[3,4,32]{2,1,0:T(4,128)S(1)} %pad_maximum_fusion.5), channel_id=1, source_target_pairs={{0,2},{1,3},{2,0},{3,1},{4,6},{5,7},{6,4},{7,5},{8,10},{9,11},{10,... | collective-permute-start | bytes 4616 | tf_op jit(solution)/shard_map/ppermute | solution.py:133
  97.9 4.6 %collective-permute-start.8 = (f32[3,4,32]{2,1,0:T(4,128)S(1)}, f32[3,4,32]{2,1,0:T(4,128)S(1)}, u32[]{:S(2)}, u32[]{:S(2)}) collective-permute-start(f32[3,4,32]{2,1,0:T(4,128)S(1)} %pad_maximum_fusion.6), channel_id=1, source_target_pairs={{0,4},{1,5},{2,6},{3,7},{4,0},{5,1},{6,2},{7,3},{8,12},{9,13},{10,... | collective-permute-start | bytes 4616 | tf_op jit(solution)/shard_map/ppermute | solution.py:133
  103.2 7.8 %copy-start.8 = (f32[4,32,1024]{2,1,0:T(8,128)S(1)}, f32[4,32,1024]{2,1,0:T(8,128)}, u32[]{:S(2)}) copy-start(f32[4,32,1024]{2,1,0:T(8,128)} %param.8) | copy-start | bytes 1572868
  103.2 3.6 %collective-permute-start.9 = (f32[8]{0:T(128)S(1)}, f32[8]{0:T(128)S(1)}, u32[]{:S(2)}, u32[]{:S(2)}) collective-permute-start(f32[8]{0:T(128)S(1)} %dynamic_update_slice.5), channel_id=1, source_target_pairs={{0,8},{8,0},{16,24},{24,16},{1,9},{9,1},{17,25},{25,17},{2,10},{10... | collective-permute-start | bytes 104 | tf_op jit(solution)/shard_map/ppermute | solution.py:152
  106.9 3.5 %collective-permute-start.10 = (f32[8]{0:T(128)S(1)}, f32[8]{0:T(128)S(1)}, u32[]{:S(2)}, u32[]{:S(2)}) collective-permute-start(f32[8]{0:T(128)S(1)} %add_dynamic-update-slice_fusion), channel_id=1, source_target_pairs={{0,16},{8,24},{16,0},{24,8},{1,17},{9,25},{17,1},{25,9},{2,18},{10... | collective-permute-start | bytes 104 | tf_op jit(solution)/shard_map/ppermute | solution.py:152
  111.0 1.2 copy-start.12
  111.0 1.9 %copy-start.14 = (f32[4,8,1024]{2,1,0:T(8,128)S(1)}, f32[4,8,1024]{2,1,0:T(8,128)}, u32[]{:S(2)}) copy-start(f32[4,8,1024]{2,1,0:T(8,128)} %param.10) | copy-start | bytes 393220
  112.9 0.7 copy-start.10
Sparse Core Ops, SparseCore 0:
  14.7 49.8 all-gather.1

commit v7 on v6

--- a/solution.py
+++ b/solution.py
@@ -112,6 +112,38 @@
     )(spectra_all, *parts)
 
 
+def estimate_sum(differences, parts, size, index):
+    count = parts[0].shape[0]
+    diffs = differences.reshape(size, count)
+
+    def partial(shift):
+        source = (index - shift) % size
+        weights = lax.dynamic_index_in_dim(diffs, source, 0, keepdims=False)
+        return jnp.sum(weights[:, None, None, None] * parts[shift].astype(jnp.float32), axis=0)
+
+    if size != 4:
+        stacked = jnp.stack(parts, 0)
+        ordered = jnp.take(stacked, (index - jnp.arange(size)) % size, axis=0)
+        flat = ordered.reshape((size * count,) + parts[0].shape[1:])
+        return jnp.sum(differences[:, None, None, None] * flat.astype(jnp.float32), axis=0)
+    sums = [partial(shift) for shift in range(size)]
+    even = (sums[0] + sums[3]) + (sums[1] + sums[2])
+    odd = (sums[0] + sums[1]) + (sums[2] + sums[3])
+    return jnp.where(index % 2 == 0, even, odd)
+
+
+def permuted_parts(values, axis_name, size):
+    return [values] + [
+        lax.ppermute(values, axis_name, [(i, (i + s) % size) for i in range(size)])
+        for s in range(1, size)
+    ]
+
+
+def in_source_order(parts, size, index):
+    order = (index - jnp.arange(size)) % size
+    return jnp.take(jnp.stack(parts, 0), order, axis=0)
+
+
 def gather_by_permutes(values, axis_name, size, index):
     parts = [values] + [
         lax.ppermute(values, axis_name, [(i, (i + s) % size) for i in range(size)])
@@ -140,15 +172,16 @@
     return top, total, label
 
 
-def gather_small(values, axis_name, size, index):
-    if size & (size - 1):
-        return lax.all_gather(values, axis_name, axis=0, tiled=True)
+def gather_small(values, axis_name, size, index, stride=1):
     count = values.shape[0]
     slots = jnp.zeros((size * count,), values.dtype)
     slots = lax.dynamic_update_slice_in_dim(slots, values, index * count, 0)
+    if size & (size - 1):
+        owner = (lax.axis_index(axis_name) % stride) == 0
+        return lax.psum(jnp.where(owner, slots, 0.0), axis_name)
     step = 1
     while step < size:
-        perm = [(i, i ^ step) for i in range(size)]
+        perm = [(i, i ^ (step * stride)) for i in range(size * stride)]
         slots = slots + lax.ppermute(slots, axis_name, perm)
         step *= 2
     return slots
@@ -168,16 +201,30 @@
     feat_index = lax.axis_index("feat")
 
     directions = (2 * sign_bits - 1).astype(jnp.bfloat16)
-    all_directions = gather_by_permutes(directions, "grp", group_count, group_index)
-    all_directions = all_directions.reshape((total_pairs,) + directions.shape[1:])
+    direction_parts = permuted_parts(directions, "grp", group_count)
     moments = jnp.stack([moment_first, moment_second], 0)
-    all_moments = gather_by_permutes(moments, "grp", group_count, group_index)
-    all_moments = jnp.transpose(all_moments, (1, 2, 0, 3, 4)).reshape(
+    moments = jnp.transpose(moments, (2, 0, 1, 3))
+    all_moments = lax.all_gather(moments, "grp", axis=0, tiled=True)
+    all_moments = jnp.transpose(all_moments, (1, 2, 0, 3)).reshape(
         (2, owned_blocks, blocks, block_len)
     )
 
+    row_parts = 2 if group_count % 2 == 0 and row_count % 32 == 0 else 1
+    rows_here = row_count // row_parts
+    row_part = group_index % row_parts
+    first_row = row_part * rows_here
+    set_pairs = pairs_here * row_parts
+    if row_parts == 2:
+        neighbour = jnp.where(group_index % 2 == 0, direction_parts[-1], direction_parts[1])
+        first_half = jnp.where(row_part == 0, directions, neighbour)
+        second_half = jnp.where(row_part == 0, neighbour, directions)
+        set_directions = jnp.concatenate([first_half, second_half], 0)
+    else:
+        set_directions = directions
+
     cosine, sine_part = tables(block_len)
-    local_in = jnp.transpose(inputs, (1, 0, 2)).reshape(owned_blocks * row_count, doubled)
+    own_in = lax.dynamic_slice_in_dim(inputs, first_row, rows_here, 0)
+    local_in = jnp.transpose(own_in, (1, 0, 2)).reshape(owned_blocks * rows_here, doubled)
     in_real = local_in[:, :block_len]
     in_imag = local_in[:, block_len:]
     f32 = jnp.float32
@@ -188,7 +235,7 @@
         in_real, sine_part, preferred_element_type=f32
     )
     spectra = jnp.concatenate([spec_real, spec_imag], 1).astype(jnp.bfloat16)
-    spectra = spectra.reshape(owned_blocks, row_count, doubled)
+    spectra = spectra.reshape(owned_blocks, rows_here, doubled)
     spectra_all = lax.all_gather(spectra, "feat", axis=0, tiled=True)
 
     angle_plus = phases + jnp.float32(perturb_size)
@@ -197,21 +244,16 @@
     sin_plus = to_bf16(jnp.sin(angle_plus))
     cos_minus = to_bf16(jnp.cos(angle_minus))
     sin_minus = to_bf16(jnp.sin(angle_minus))
-    up = sign_bits == 1
+    signs = set_directions.astype(f32)
     cos_half = cos_plus - cos_minus
     sin_half = sin_plus - sin_minus
-    t_real = jnp.concatenate(
-        [(cos_plus + cos_minus)[None], jnp.where(up, cos_half, -cos_half)], 0
-    )
-    t_imag = jnp.concatenate(
-        [(sin_plus + sin_minus)[None], jnp.where(up, sin_half, -sin_half)], 0
-    )
-    spectra_all, all_directions, all_moments = lax.optimization_barrier(
-        (spectra_all, all_directions, all_moments)
-    )
+    t_real = jnp.concatenate([(cos_plus + cos_minus)[None], signs * cos_half[None]], 0)
+    t_imag = jnp.concatenate([(sin_plus + sin_minus)[None], signs * sin_half[None]], 0)
+    spectra_all, set_directions = lax.optimization_barrier((spectra_all, set_directions))
 
     mixed = mix(spectra_all, t_real, t_imag)
-    mixed = mixed.reshape(net_count * owned_blocks * row_count, doubled)
+    set_nets = 2 * set_pairs
+    mixed = mixed.reshape(set_nets * owned_blocks * rows_here, doubled)
     mix_real = mixed[:, :block_len]
     mix_imag = mixed[:, block_len:]
     field_real = jnp.dot(mix_real, cosine, preferred_element_type=f32) - jnp.dot(
@@ -221,25 +263,32 @@
         mix_imag, cosine, preferred_element_type=f32
     )
     intensity = field_real**2 + field_imag**2
-    logits = logit_scale * intensity.reshape(net_count, owned_blocks, row_count, block_len)
+    logits = logit_scale * intensity.reshape(set_nets, owned_blocks, rows_here, block_len)
     first_class = feat_index * (owned_blocks * block_len)
     classes = first_class + jnp.arange(owned_blocks * block_len, dtype=jnp.int32).reshape(
         owned_blocks, 1, block_len
     )
-    matches = classes == labels[None, :, None]
+    own_labels = lax.dynamic_slice_in_dim(labels, first_row, rows_here, 0)
+    matches = classes == own_labels[None, :, None]
     local_top = jnp.max(logits, axis=(1, 3))
     local_total = jnp.sum(jnp.exp(logits - local_top[:, None, :, None]), axis=(1, 3))
     local_label = jnp.sum(jnp.where(matches[None], logits, 0.0), axis=(1, 3))
     row_top, row_total, row_label = merge_stats(
         local_top, local_total, local_label, "feat", feat_count
     )
-    losses = jnp.mean(row_top + jnp.log(row_total) - row_label, axis=1)
-    losses = losses.reshape(pairs_here, 2)
-    own_differences = (losses[:, 0] - losses[:, 1]) / (2.0 * perturb_size)
-    differences = gather_small(own_differences, "grp", group_count, group_index)
+    row_sums = jnp.sum(row_top + jnp.log(row_total) - row_label, axis=1)
+    if row_parts == 2:
+        row_sums = row_sums + lax.ppermute(
+            row_sums, "grp", [(i, i ^ 1) for i in range(group_count)]
+        )
+    losses = (row_sums / row_count).reshape(set_pairs, 2)
+    set_differences = (losses[:, 0] - losses[:, 1]) / (2.0 * perturb_size)
+    differences = gather_small(
+        set_differences, "grp", group_count // row_parts, group_index // row_parts, row_parts
+    )
 
     estimate_all = (
-        jnp.sum(differences[:, None, None, None] * all_directions.astype(f32), axis=0)
+        estimate_sum(differences, direction_parts, group_count, group_index)
         / total_pairs
     )
     all_first = all_moments[0]

time: 121 us -> 115 us (0.950)
  waiting for transfers between devices: 25.1 us -> 31.6 us
  other arithmetic: 27.7 us -> 22 us
  starting transfers between devices: 16.1 us -> 12.4 us
  Pallas kernels: 18.5 us -> 15.3 us
  between operations: 14.3 us -> 15.8 us
  local copies, waits for them, and re-layouts: 10.3 us -> 8.83 us
    another operation x4 -> x0, other arithmetic: 7 us -> none  [gather_by_permutes(): return jnp.take(jnp.stack(parts, 0), order, axis=0)]
    gather x2 -> x0, local copies, waits for them, and re-layouts: 6.45 us -> none  [gather_by_permutes(): return jnp.take(jnp.stack(parts, 0), order, axis=0)]
    ppermute x6 -> x4, waiting for transfers between devices: 15 us -> 20.8 us  [the longest x3 18.7 us: permuted_parts(): lax.ppermute(values, axis_name, [(i, (i + s) % size) for i in range(size)])]
    reduce_sum x2 -> x5, other arithmetic: 0.65 us -> 5.94 us  [the longest x4 5.81 us: partial(): jnp.sum(weights[:, None, None, None] * parts[shift].astype(jnp.float32),...]
    all_gather x0 -> x1, waiting for transfers between devices: none -> 4.08 us  [body(): all_moments = lax.all_gather(moments, 'grp', axis=0, tiled=True)]
    add x1 -> x0, other arithmetic: 3.83 us -> none  [body(): sin_plus + sin_minus]
    sub x0 -> x1, other arithmetic: none -> 3.82 us  [body(): sin_half = sin_plus - sin_minus]
    unnamed x33 -> x39, local copies, waits for them, and re-layouts: 2.74 us -> 6.31 us
  transfers between devices with their start and end apart: 12 -> 10, of which waited for: 11 -> 8; matrix products, arithmetic and copies ran while one was open for 21% -> 21% of each run, Pallas kernels for 0% -> 13%
where the time goes in v7:
time: 115 us
  waiting for transfers between devices  31.6 us (27%)
  other arithmetic  22 us (19%)
  between operations  15.8 us (14%)
  Pallas kernels  15.3 us (13%)
  starting transfers between devices  12.4 us (11%)
  local copies, waits for them, and re-layouts  8.83 us (8%)
  matrix products  8.58 us (7%)
    ppermute x3, waiting for transfers between devices, permuted_parts(): lax.ppermute(values, axis_name, [(i, (i + s) % size) for i in range(size)])  18.7 us
    pallas_call x1, Pallas kernels, mix(): pl.pallas_call(kernel, grid=(owned,), in_specs=[pl.BlockSpec((blocks, row...  15.3 us
    unnamed x39, local copies, waits for them, and re-layouts  6.31 us
    reduce_sum x4, other arithmetic, partial(): jnp.sum(weights[:, None, None, None] * parts[shift].astype(jnp.float32),...  5.81 us
    ppermute x3, starting transfers between devices, permuted_parts(): lax.ppermute(values, axis_name, [(i, (i + s) % size) for i in range(size)])  4.99 us
    ppermute x3, waiting for transfers between devices, merge_stats(): packed = lax.ppermute(jnp.stack([top, total, label], 0), axis_name, perm)  4.45 us
    ppermute x3, starting transfers between devices, merge_stats(): packed = lax.ppermute(jnp.stack([top, total, label], 0), axis_name, perm)  4.44 us
    all_gather x1, waiting for transfers between devices, body(): all_moments = lax.all_gather(moments, 'grp', axis=0, tiled=True)  4.08 us
  transfers between devices with their start and end apart: 10, of which 8 were waited for; matrix products, arithmetic and copies ran while one was open for 21% of the time, Pallas kernels for 13%

profile of v7, /device:TPU:0, one launch (start us, length us, event | category | flops | bytes accessed | tf_op | source)
XLA Modules:
  0.0 114.5 jit_solution(16119113246168873763)
XLA Ops:
  8.1 0.5 fusion.42
  8.6 0.4 copy-done
  9.3 0.6 fusion.45
  9.9 1.5 %multiply_convert_fusion.1 = (bf16[32,32,1024]{2,1,0:T(8,128)(2,1)S(1)}, bf16[32,32,1024]{2,1,0:T(8,128)(2,1)S(1)}) fusion(f32[32,1024]{1,0:T(8,128)S(1)} %get-tuple-element.44, f32[32,1024]{1,0:T(8,128)S(1)} %get-tuple-element.41, f32[32,1024]{1,0:T(8,128)S(1)} %get-tuple-element.45, f32[32,1024]{1,0:T(8,128)S(1)} %get-tuple-element.40), kind=kLoop, calls=%fused_computation.1 | loop fusion | flops 10485760 | bytes 4718592 | tf_op jit(solution)/shard_map/convert_element_type | solution.py:36
  11.5 0.5 fusion.40
  12.0 0.5 fusion.36
  12.4 0.3 copy-done.6
  12.8 0.5 fusion
  13.4 0.5 fusion.1
  13.9 0.7 pad_maximum_fusion.1
  14.7 0.9 add_convert_fusion
  15.7 3.9 %collective-permute-start = (bf16[2,4,32,1024]{3,2,1,0:T(8,128)(2,1)}, bf16[2,4,32,1024]{3,2,1,0:T(8,128)(2,1)}, u32[]{:S(2)}, u32[]{:S(2)}) collective-permute-start(bf16[2,4,32,1024]{3,2,1,0:T(8,128)(2,1)} %add_convert_fusion), channel_id=1, source_target_pairs={{0,24},{8,0},{16,8},{24,16},{1,25},{9,1},{17,9},{25,17},{2,26},{10... | collective-permute-start | bytes 1572872 | tf_op jit(solution)/shard_map/ppermute | solution.py:137
  19.6 1.1 collective-permute-start.7
  20.9 3.8 %fusion.21 = (f32[4,32,1024]{2,1,0:T(8,128)S(1)}, f32[4,32,1024]{2,1,0:T(8,128)S(1)}, f32[4,32,1024]{2,1,0:T(8,128)S(1)}, f32[4,32,1024]{2,1,0:T(8,128)S(1)}) fusion(f32[4,32,1024]{2,1,0:T(8,128)S(1)} %copy-done.13), kind=kLoop, calls=%fused_computation.54 | loop fusion | flops 1310720 | bytes 2621440 | tf_op jit(solution)/shard_map/sub | solution.py:249
  24.7 7.5 %collective-permute-done = bf16[2,4,32,1024]{3,2,1,0:T(8,128)(2,1)} collective-permute-done((bf16[2,4,32,1024]{3,2,1,0:T(8,128)(2,1)}, bf16[2,4,32,1024]{3,2,1,0:T(8,128)(2,1)}, u32[]{:S(2)}, u32[]{:S(2)}) %collective-permute-start) | collective-permute-done | bytes 524320 | tf_op jit(solution)/shard_map/ppermute | solution.py:137
  32.2 11.1 %collective-permute-done.1 = bf16[2,4,32,1024]{3,2,1,0:T(8,128)(2,1)} collective-permute-done((bf16[2,4,32,1024]{3,2,1,0:T(8,128)(2,1)}, bf16[2,4,32,1024]{3,2,1,0:T(8,128)(2,1)}, u32[]{:S(2)}, u32[]{:S(2)}) %collective-permute-start.1) | collective-permute-done | bytes 524320 | tf_op jit(solution)/shard_map/ppermute | solution.py:137
  43.4 1.2 %broadcast_select_fusion.1 = (bf16[2,4,32,1024]{3,2,1,0:T(8,128)(2,1)S(1)}, bf16[2,4,32,1024]{3,2,1,0:T(8,128)(2,1)S(1)}) fusion(pred[]{:T(512)S(6)} %eq.34, bf16[2,4,32,1024]{3,2,1,0:T(8,128)(2,1)} %collective-permute-done, bf16[2,4,32,1024]{3,2,1,0:T(8,128)(2,1)} %collective-permute-done.1, s32[2,4,32,1024]{3,2,1,0:T(8,128)S(1)} %copy-done.10), kind=kLoop, calls=%fused_computation.50 | loop fusion | flops 1572864 | bytes 3145729 | tf_op jit(solution)/shard_map/jit(_where)/select_n | solution.py:219
  44.6 0.5 convert_multiply_fusion
  45.2 1.6 %slice_bitcast_fusion = (f32[4,32,1024]{2,1,0:T(8,128)S(1)}, f32[4,32,1024]{2,1,0:T(8,128)S(1)}, f32[4,32,1024]{2,1,0:T(8,128)S(1)}, f32[4,32,1024]{2,1,0:T(8,12...) fusion(f32[4,4,32,1024]{3,2,1,0:T(8,128)S(1)} %get-tuple-element.24, ...), kind=kLoop, calls=%fused_computation.36 | loop fusion | bytes 8388608 | tf_op jit(solution)/shard_map/squeeze | solution.py:100
  46.7 1.0 copy-done.1
  47.8 1.0 copy-done.2
  48.8 1.0 copy-done.3
  49.9 1.0 copy-done.4
  50.9 1.0 copy-done.5
  52.0 15.3 %shard_map.93 = bf16[8,4,16,2048]{3,2,1,0:T(8,128)(2,1)} custom-call(bf16[32,16,2048]{2,1,0:T(8,128)(2,1)} %all-gather.3.cloned.1.call-done.s_ref, f32[4,32,1024]{2,1,0:T(8,128)S(1)} %get-tuple-element.28.refs_0_, f32[4,32,1024]{2,1,0:T(8,128)S(1)} %copy-done.2, f32[4,32,1024]{2,1,0:T(8,128)S(1)} %copy-done.3, f32[4,32,1024]{2,1,0:T(8,128)S(1)} %copy-done.4, ...), custom_call_target="tpu_custom_call" | custom-call | tf_op jit(solution)/shard_map/pallas_call | solution.py:101
  67.3 2.6 %fusion.3 = f32[512,1024]{1,0:T(8,128)S(1)} fusion(bf16[1024,1024]{1,0:T(8,128)(2,1)S(1)} %bitcast.169, bf16[512,2048]{1,0:T(8,128)(2,1)} %bitcast.171), kind=kOutput, calls=%fused_computation.18 | convolution fusion | flops 1073741824 | bytes 5242880 | tf_op jit(solution)/shard_map/dot_general | solution.py:259
  69.9 1.3 %fusion.7 = f32[512,1024]{1,0:T(8,128)S(1)} fusion(bf16[1024,1024]{1,0:T(8,128)(2,1)S(1)} %bitcast.165, bf16[512,2048]{1,0:T(8,128)(2,1)S(1)} %bitcast.172), kind=kOutput, calls=%fused_computation.22 | convolution fusion | flops 1073741824 | bytes 5242880 | tf_op jit(solution)/shard_map/dot_general | solution.py:259
  71.2 1.3 %fusion.5 = f32[512,1024]{1,0:T(8,128)S(1)} fusion(bf16[1024,1024]{1,0:T(8,128)(2,1)S(1)} %bitcast.170, bf16[512,2048]{1,0:T(8,128)(2,1)S(1)} %bitcast.173), kind=kOutput, calls=%fused_computation.20 | convolution fusion | flops 1073741824 | bytes 5242880 | tf_op jit(solution)/shard_map/dot_general | solution.py:262
  72.5 1.5 %fusion.69 = (f32[512]{0:T(512)S(1)}, f32[512,1024]{1,0:T(8,128)S(1)}) fusion(f32[512,1024]{1,0:T(8,128)S(1)} %fusion.5, bf16[1024,1024]{1,0:T(8,128)(2,1)S(1)} %bitcast.166, bf16[512,2048]{1,0:T(8,128)(2,1)S(1)} %bitcast.174, f32[512,1024]{1,0:T(8,128)S(1)} %fusion.7, f32[512,1024]{1,0:T(8,128)S(1)} %fusion.3), kind=kOutput, calls=%fused_computation.146 | convolution fusion | flops 1077411328 | bytes 11536384 | tf_op jit(solution)/shard_map/dot_general | solution.py:262
  74.2 0.6 exponential_reduce_fusion
  75.3 0.7 maximum_bitcast_fusion
  76.1 0.3 collective-permute-done.2
  76.4 1.6 %collective-permute-start.3 = (f32[3,8,16]{2,1,0:T(8,128)S(1)}, f32[3,8,16]{2,1,0:T(8,128)S(1)}, u32[]{:S(2)}, u32[]{:S(2)}) collective-permute-start(f32[3,8,16]{2,1,0:T(8,128)S(1)} %pad_maximum_fusion.3), channel_id=1, source_target_pairs={{0,2},{1,3},{2,0},{3,1},{4,6},{5,7},{6,4},{7,5},{8,10},{9,11},{10,... | collective-permute-start | bytes 4616 | tf_op jit(solution)/shard_map/ppermute | solution.py:165
  78.0 2.1 %collective-permute-done.3 = f32[3,8,16]{2,1,0:T(8,128)S(1)} collective-permute-done((f32[3,8,16]{2,1,0:T(8,128)S(1)}, f32[3,8,16]{2,1,0:T(8,128)S(1)}, u32[]{:S(2)}, u32[]{:S(2)}) %collective-permute-start.3) | collective-permute-done | bytes 1568 | tf_op jit(solution)/shard_map/ppermute | solution.py:165
  80.2 2.6 %collective-permute-start.4 = (f32[3,8,16]{2,1,0:T(8,128)S(1)}, f32[3,8,16]{2,1,0:T(8,128)S(1)}, u32[]{:S(2)}, u32[]{:S(2)}) collective-permute-start(f32[3,8,16]{2,1,0:T(8,128)S(1)} %pad_maximum_fusion.4), channel_id=1, source_target_pairs={{0,4},{1,5},{2,6},{3,7},{4,0},{5,1},{6,2},{7,3},{8,12},{9,13},{10,... | collective-permute-start | bytes 4616 | tf_op jit(solution)/shard_map/ppermute | solution.py:165
  82.8 2.0 %collective-permute-done.4 = f32[3,8,16]{2,1,0:T(8,128)S(1)} collective-permute-done((f32[3,8,16]{2,1,0:T(8,128)S(1)}, f32[3,8,16]{2,1,0:T(8,128)S(1)}, u32[]{:S(2)}, u32[]{:S(2)}) %collective-permute-start.4) | collective-permute-done | bytes 1568 | tf_op jit(solution)/shard_map/ppermute | solution.py:165
  85.0 1.5 %collective-permute-start.5 = (f32[8]{0:T(128)S(1)}, f32[8]{0:T(128)S(1)}, u32[]{:S(2)}, u32[]{:S(2)}) collective-permute-start(f32[8]{0:T(128)S(1)} %fusion.48), channel_id=1, source_target_pairs={{0,8},{8,0},{16,24},{24,16},{1,9},{9,1},{17,25},{25,17},{2,10},{10... | collective-permute-start | bytes 104 | tf_op jit(solution)/shard_map/ppermute | solution.py:281
  86.4 2.1 %collective-permute-done.5 = f32[8]{0:T(128)S(1)} collective-permute-done((f32[8]{0:T(128)S(1)}, f32[8]{0:T(128)S(1)}, u32[]{:S(2)}, u32[]{:S(2)}) %collective-permute-start.5) | collective-permute-done | bytes 64 | tf_op jit(solution)/shard_map/ppermute | solution.py:281
  88.8 0.2 dynamic_update_slice.5
  89.1 1.4 %collective-permute-start.6 = (f32[8]{0:T(128)S(1)}, f32[8]{0:T(128)S(1)}, u32[]{:S(2)}, u32[]{:S(2)}) collective-permute-start(f32[8]{0:T(128)S(1)} %dynamic_update_slice.5), channel_id=1, source_target_pairs={{0,16},{8,24},{16,0},{24,8},{1,17},{9,25},{17,1},{25,9},{2,18},{10... | collective-permute-start | bytes 104 | tf_op jit(solution)/shard_map/ppermute | solution.py:185
  90.5 2.2 %collective-permute-done.6 = f32[8]{0:T(128)S(1)} collective-permute-done((f32[8]{0:T(128)S(1)}, f32[8]{0:T(128)S(1)}, u32[]{:S(2)}, u32[]{:S(2)}) %collective-permute-start.6) | collective-permute-done | bytes 64 | tf_op jit(solution)/shard_map/ppermute | solution.py:185
  92.9 1.3 %multiply_reduce_fusion.1 = f32[4,32,1024]{2,1,0:T(8,128)S(1)} fusion(bf16[2,4,32,1024]{3,2,1,0:T(8,128)(2,1)} %collective-permute-done.1, f32[2]{0:T(128)S(1)} %get-tuple-element.36), kind=kLoop, calls=%fused_computation.13 | loop fusion | flops 655360 | bytes 1048584 | tf_op jit(solution)/shard_map/reduce_sum | solution.py:122
  94.2 2.3 %multiply_reduce_fusion.2 = f32[4,32,1024]{2,1,0:T(8,128)} fusion(bf16[2,4,32,1024]{3,2,1,0:T(8,128)(2,1)} %collective-permute-done, f32[2]{0:T(128)S(1)} %get-tuple-element.38), kind=kLoop, calls=%fused_computation.14 | loop fusion | flops 655360 | bytes 1048584 | tf_op jit(solution)/shard_map/reduce_sum | solution.py:122
  96.4 2.1 %multiply_reduce_fusion = f32[4,32,1024]{2,1,0:T(8,128)} fusion(bf16[2,4,32,1024]{3,2,1,0:T(8,128)(2,1)} %collective-permute-done.7, f32[2]{0:T(128)S(1)} %get-tuple-element.37), kind=kLoop, calls=%fused_computation.12 | loop fusion | flops 655360 | bytes 1048584 | tf_op jit(solution)/shard_map/reduce_sum | solution.py:122
  98.7 4.1 %all-gather.5.cloned.1.call-done = f32[32,2,4,1024]{3,0,2,1:T(8,128)} async-done(((f32[8,2,4,1024]{3,0,2,1:T(8,128)}), f32[32,2,4,1024]{3,0,2,1:T(8,128)}) %all-gather.5.cloned.1.call-update) | async-done | bytes 1048592 | tf_op jit(solution)/shard_map/all_gather | solution.py:207
  102.8 2.8 %fusion.15 = (f32[4,32,1024]{2,1,0:T(8,128)}, f32[4,32,1024]{2,1,0:T(8,128)S(1)}) fusion(f32[4,32,1024]{2,1,0:T(8,128)S(1)} %copy-done.14, f32[2,4,32,1024]{3,2,1,0:T(8,128)} %bitcast.179, f32[4,32,1024]{2,1,0:T(8,128)} %multiply_reduce_fusion, f32[4,32,1024]{2,1,0:T(8,128)} %multiply_reduce_fusion.2, f32[4,32,1024]{2,1,0:T(8,128)S(1)} %multiply_reduce_fusion.3, ...), kind=kLoop, calls=%fused_computation.31 | loop fusion | flops 2621440 | bytes 4718593 | tf_op jit(solution)/shard_map/sub | solution.py:300
  105.7 0.7 fusion.29
  106.4 0.7 multiply_add_fusion
  (68 shorter events, 2.4 us)
Async XLA Ops:
  8.0 1.0 copy-start
  8.0 38.7 %all-gather.3.cloned.1.call-start = ((), (), s32[]{:S(2)}) async-start(), calls=%async_computation | async-start | bytes 2359296 | tf_op jit(solution)/shard_map/all_gather | solution.py:239
  11.5 1.3 %copy-start.6 = (bf16[32,32,1024]{2,1,0:T(8,128)(2,1)}, bf16[32,32,1024]{2,1,0:T(8,128)(2,1)S(1)}, u32[]{:S(2)}) copy-start(bf16[32,32,1024]{2,1,0:T(8,128)(2,1)S(1)} %get-tuple-element.30) | copy-start | bytes 6291460
  11.5 1.9 %copy-start.8 = (bf16[32,32,1024]{2,1,0:T(8,128)(2,1)}, bf16[32,32,1024]{2,1,0:T(8,128)(2,1)S(1)}, u32[]{:S(2)}) copy-start(bf16[32,32,1024]{2,1,0:T(8,128)(2,1)S(1)} %get-tuple-element.31) | copy-start | bytes 6291460
  13.4 1.3 %copy-start.10 = (s32[2,4,32,1024]{3,2,1,0:T(8,128)S(1)}, s32[2,4,32,1024]{3,2,1,0:T(8,128)}, u32[]{:S(2)}) copy-start(s32[2,4,32,1024]{3,2,1,0:T(8,128)} %param.9) | copy-start | bytes 3145732
  13.4 7.2 %copy-start.18 = (s32[32]{0:T(128)S(1)}, s32[32]{0:T(128)}, u32[]{:S(2)}) copy-start(s32[32]{0:T(128)} %param.7) | copy-start | bytes 388
  13.4 7.4 %copy-start.13 = (f32[4,32,1024]{2,1,0:T(8,128)S(1)}, f32[4,32,1024]{2,1,0:T(8,128)}, u32[]{:S(2)}) copy-start(f32[4,32,1024]{2,1,0:T(8,128)} %param.8) | copy-start | bytes 1572868
  14.7 88.2 %all-gather.5.cloned.1.call-start = ((), (), s32[]{:S(2)}) async-start(), calls=%async_computation.1 | async-start | bytes 1310720 | tf_op jit(solution)/shard_map/all_gather | solution.py:207
  15.7 16.6 %collective-permute-start = (bf16[2,4,32,1024]{3,2,1,0:T(8,128)(2,1)}, bf16[2,4,32,1024]{3,2,1,0:T(8,128)(2,1)}, u32[]{:S(2)}, u32[]{:S(2)}) collective-permute-start(bf16[2,4,32,1024]{3,2,1,0:T(8,128)(2,1)} %add_convert_fusion), channel_id=1, source_target_pairs={{0,24},{8,0},{16,8},{24,16},{1,25},{9,1},{17,9},{25,17},{2,26},{10... | collective-permute-start | bytes 1572872 | tf_op jit(solution)/shard_map/ppermute | solution.py:137
  19.6 23.8 %collective-permute-start.1 = (bf16[2,4,32,1024]{3,2,1,0:T(8,128)(2,1)}, bf16[2,4,32,1024]{3,2,1,0:T(8,128)(2,1)}, u32[]{:S(2)}, u32[]{:S(2)}) collective-permute-start(bf16[2,4,32,1024]{3,2,1,0:T(8,128)(2,1)} %add_convert_fusion), channel_id=1, source_target_pairs={{0,8},{8,16},{16,24},{24,0},{1,9},{9,17},{17,25},{25,1},{2,10},{10... | collective-permute-start | bytes 1572872 | tf_op jit(solution)/shard_map/ppermute | solution.py:137
  19.6 76.9 %collective-permute-start.7 = (bf16[2,4,32,1024]{3,2,1,0:T(8,128)(2,1)}, bf16[2,4,32,1024]{3,2,1,0:T(8,128)(2,1)}, u32[]{:S(2)}, u32[]{:S(2)}) collective-permute-start(bf16[2,4,32,1024]{3,2,1,0:T(8,128)(2,1)} %add_convert_fusion), channel_id=1, source_target_pairs={{0,16},{8,24},{16,0},{24,8},{1,17},{9,25},{17,1},{25,9},{2,18},{10... | collective-permute-start | bytes 1572872 | tf_op jit(solution)/shard_map/ppermute | solution.py:137
  46.7 1.0 copy-start.1
  47.8 1.0 copy-start.2
  48.8 1.0 copy-start.3
  49.9 1.0 copy-start.4
  50.9 1.0 copy-start.5
  51.9 15.3 %copy-start.9 = (bf16[32,32,1024]{2,1,0:T(8,128)(2,1)S(1)}, bf16[32,32,1024]{2,1,0:T(8,128)(2,1)}, u32[]{:S(2)}) copy-start(bf16[32,32,1024]{2,1,0:T(8,128)(2,1)} %copy-done.8) | copy-start | bytes 6291460
  67.3 2.6 %copy-start.7 = (bf16[32,32,1024]{2,1,0:T(8,128)(2,1)S(1)}, bf16[32,32,1024]{2,1,0:T(8,128)(2,1)}, u32[]{:S(2)}) copy-start(bf16[32,32,1024]{2,1,0:T(8,128)(2,1)} %copy-done.6) | copy-start | bytes 6291460
  67.3 2.6 %copy-start.12 = (bf16[8,4,16,2048]{3,2,1,0:T(8,128)(2,1)S(1)}, bf16[8,4,16,2048]{3,2,1,0:T(8,128)(2,1)}, u32[]{:S(2)}) copy-start(bf16[8,4,16,2048]{3,2,1,0:T(8,128)(2,1)} %shard_map.93) | copy-start | bytes 6291460
  74.0 1.3 %copy-start.16 = (f32[4,8,1024]{2,1,0:T(8,128)S(1)}, f32[4,8,1024]{2,1,0:T(8,128)}, u32[]{:S(2)}) copy-start(f32[4,8,1024]{2,1,0:T(8,128)} %param.11) | copy-start | bytes 393220
  74.0 1.3 %copy-start.17 = (f32[4,8,1024]{2,1,0:T(8,128)S(1)}, f32[4,8,1024]{2,1,0:T(8,128)}, u32[]{:S(2)}) copy-start(f32[4,8,1024]{2,1,0:T(8,128)} %param.10) | copy-start | bytes 393220
  75.1 1.2 %collective-permute-start.2 = (f32[3,8,16]{2,1,0:T(8,128)S(1)}, f32[3,8,16]{2,1,0:T(8,128)S(1)}, u32[]{:S(2)}, u32[]{:S(2)}) collective-permute-start(f32[3,8,16]{2,1,0:T(8,128)S(1)} %pad_maximum_fusion.2), channel_id=1, source_target_pairs={{0,1},{1,0},{2,3},{3,2},{4,5},{5,4},{6,7},{7,6},{8,9},{9,8},{10,11... | collective-permute-start | bytes 4616 | tf_op jit(solution)/shard_map/ppermute | solution.py:165
  75.3 23.2 %copy-start.11 = (s32[2,4,32,1024]{3,2,1,0:T(8,128)S(1)}, s32[2,4,32,1024]{3,2,1,0:T(8,128)}, u32[]{:S(2)}) copy-start(s32[2,4,32,1024]{3,2,1,0:T(8,128)} %param.9) | copy-start | bytes 3145732
  76.4 3.8 %collective-permute-start.3 = (f32[3,8,16]{2,1,0:T(8,128)S(1)}, f32[3,8,16]{2,1,0:T(8,128)S(1)}, u32[]{:S(2)}, u32[]{:S(2)}) collective-permute-start(f32[3,8,16]{2,1,0:T(8,128)S(1)} %pad_maximum_fusion.3), channel_id=1, source_target_pairs={{0,2},{1,3},{2,0},{3,1},{4,6},{5,7},{6,4},{7,5},{8,10},{9,11},{10,... | collective-permute-start | bytes 4616 | tf_op jit(solution)/shard_map/ppermute | solution.py:165
  80.2 4.7 %collective-permute-start.4 = (f32[3,8,16]{2,1,0:T(8,128)S(1)}, f32[3,8,16]{2,1,0:T(8,128)S(1)}, u32[]{:S(2)}, u32[]{:S(2)}) collective-permute-start(f32[3,8,16]{2,1,0:T(8,128)S(1)} %pad_maximum_fusion.4), channel_id=1, source_target_pairs={{0,4},{1,5},{2,6},{3,7},{4,0},{5,1},{6,2},{7,3},{8,12},{9,13},{10,... | collective-permute-start | bytes 4616 | tf_op jit(solution)/shard_map/ppermute | solution.py:165
  85.0 3.6 %collective-permute-start.5 = (f32[8]{0:T(128)S(1)}, f32[8]{0:T(128)S(1)}, u32[]{:S(2)}, u32[]{:S(2)}) collective-permute-start(f32[8]{0:T(128)S(1)} %fusion.48), channel_id=1, source_target_pairs={{0,8},{8,0},{16,24},{24,16},{1,9},{9,1},{17,25},{25,17},{2,10},{10... | collective-permute-start | bytes 104 | tf_op jit(solution)/shard_map/ppermute | solution.py:281
  89.1 3.6 %collective-permute-start.6 = (f32[8]{0:T(128)S(1)}, f32[8]{0:T(128)S(1)}, u32[]{:S(2)}, u32[]{:S(2)}) collective-permute-start(f32[8]{0:T(128)S(1)} %dynamic_update_slice.5), channel_id=1, source_target_pairs={{0,16},{8,24},{16,0},{24,8},{1,17},{9,25},{17,1},{25,9},{2,18},{10... | collective-permute-start | bytes 104 | tf_op jit(solution)/shard_map/ppermute | solution.py:185
  94.2 8.6 %copy-start.14 = (f32[4,32,1024]{2,1,0:T(8,128)S(1)}, f32[4,32,1024]{2,1,0:T(8,128)}, u32[]{:S(2)}) copy-start(f32[4,32,1024]{2,1,0:T(8,128)} %param.8) | copy-start | bytes 1572868
  106.4 0.7 copy-start.15
Sparse Core Ops, SparseCore 0:
  14.8 31.8 all-gather.2
Sparse Core Ops, SparseCore 1:
  76.1 26.6 all-gather.4

commit v8 on v7

--- a/solution.py
+++ b/solution.py
@@ -203,11 +203,7 @@
     directions = (2 * sign_bits - 1).astype(jnp.bfloat16)
     direction_parts = permuted_parts(directions, "grp", group_count)
     moments = jnp.stack([moment_first, moment_second], 0)
-    moments = jnp.transpose(moments, (2, 0, 1, 3))
-    all_moments = lax.all_gather(moments, "grp", axis=0, tiled=True)
-    all_moments = jnp.transpose(all_moments, (1, 2, 0, 3)).reshape(
-        (2, owned_blocks, blocks, block_len)
-    )
+    moment_parts = permuted_parts(moments, "grp", group_count)
 
     row_parts = 2 if group_count % 2 == 0 and row_count % 32 == 0 else 1
     rows_here = row_count // row_parts
@@ -291,15 +287,22 @@
         estimate_sum(differences, direction_parts, group_count, group_index)
         / total_pairs
     )
-    all_first = all_moments[0]
-    all_second = all_moments[1]
     first_bias = 1.0 - beta_first**ADAM_STEP
     second_bias = 1.0 - beta_second**ADAM_STEP
-    first_all = beta_first * all_first + (1.0 - beta_first) * estimate_all
-    second_all = beta_second * all_second + (1.0 - beta_second) * estimate_all * estimate_all
-    phases_next = phases - learn_rate * (first_all / first_bias) / (
-        jnp.sqrt(second_all / second_bias) + adam_eps
-    )
+    phases_next = phases
+    for shift in range(group_count):
+        column = ((group_index - shift) % group_count) * own_columns
+        part_estimate = lax.dynamic_slice_in_dim(estimate_all, column, own_columns, 1)
+        part_phases = lax.dynamic_slice_in_dim(phases, column, own_columns, 1)
+        part_first = beta_first * moment_parts[shift][0] + (1.0 - beta_first) * part_estimate
+        part_second = (
+            beta_second * moment_parts[shift][1]
+            + (1.0 - beta_second) * part_estimate * part_estimate
+        )
+        part_next = part_phases - learn_rate * (part_first / first_bias) / (
+            jnp.sqrt(part_second / second_bias) + adam_eps
+        )
+        phases_next = lax.dynamic_update_slice_in_dim(phases_next, part_next, column, 1)
     first_column = group_index * own_columns
     estimate = lax.dynamic_slice_in_dim(estimate_all, first_column, own_columns, 1)
     first_new = beta_first * moment_first + (1.0 - beta_first) * estimate

time: 115 us -> 111 us (0.965)
  waiting for transfers between devices: 31.6 us -> 23.4 us
  starting transfers between devices: 12.4 us -> 17.5 us
  between operations: 15.8 us -> 14.5 us
    ppermute x3 -> x6, starting transfers between devices: 4.99 us -> 11.3 us  [permuted_parts(): lax.ppermute(values, axis_name, [(i, (i + s) % size) for i in range(size)])]
    ppermute x3 -> x6, waiting for transfers between devices: 18.7 us -> 12.8 us  [permuted_parts(): lax.ppermute(values, axis_name, [(i, (i + s) % size) for i in range(size)])]
    all_gather x1 -> x0, waiting for transfers between devices: 4.08 us -> none  [body(): all_moments = lax.all_gather(moments, 'grp', axis=0, tiled=True)]
    dynamic_update_slice x0 -> x3, other arithmetic: none -> 3.22 us  [body(): lax.dynamic_update_slice_in_dim(phases_next, part_next, column, 1)]
    sub x1 -> x0, other arithmetic: 2.8 us -> none  [body(): phases - learn_rate * (first_all / first_bias) / (jnp.sqrt(second_all / s...]
    reduce_sum x4, other arithmetic: 5.81 us -> 4.09 us  [partial(): jnp.sum(weights[:, None, None, None] * parts[shift].astype(jnp.float32),...]
    unnamed x39 -> x43, local copies, waits for them, and re-layouts: 6.31 us -> 7.13 us
  transfers between devices with their start and end apart: 10 -> 12, of which waited for: 8 -> 7; matrix products, arithmetic and copies ran while one was open for 21% -> 23% of each run, Pallas kernels for 13% -> 14%
where the time goes in v8:
time: 111 us; the launch traced here: 110 us
  waiting for transfers between devices  23.4 us (21%)
  other arithmetic  20.9 us (19%)
  starting transfers between devices  17.5 us (16%)
  Pallas kernels  15.4 us (14%)
  between operations  14.5 us (13%)
  local copies, waits for them, and re-layouts  9.62 us (9%)
  matrix products  8.57 us (8%)
    pallas_call x1, Pallas kernels, mix(): pl.pallas_call(kernel, grid=(owned,), in_specs=[pl.BlockSpec((blocks, row...  15.4 us
    ppermute x6, waiting for transfers between devices, permuted_parts(): lax.ppermute(values, axis_name, [(i, (i + s) % size) for i in range(size)])  12.8 us
    ppermute x6, starting transfers between devices, permuted_parts(): lax.ppermute(values, axis_name, [(i, (i + s) % size) for i in range(size)])  11.3 us
    unnamed x43, local copies, waits for them, and re-layouts  7.13 us
    ppermute x3, waiting for transfers between devices, merge_stats(): packed = lax.ppermute(jnp.stack([top, total, label], 0), axis_name, perm)  5.24 us
    ppermute x3, starting transfers between devices, merge_stats(): packed = lax.ppermute(jnp.stack([top, total, label], 0), axis_name, perm)  4.37 us
    reduce_sum x4, other arithmetic, partial(): jnp.sum(weights[:, None, None, None] * parts[shift].astype(jnp.float32),...  4.09 us
    sub x1, other arithmetic, body(): sin_half = sin_plus - sin_minus  3.82 us
  transfers between devices with their start and end apart: 12, of which 7 were waited for; matrix products, arithmetic and copies ran while one was open for 23% of the time, Pallas kernels for 14%

profile of v8, /device:TPU:0, one launch (start us, length us, event | category | flops | bytes accessed | tf_op | source)
XLA Modules:
  0.0 109.9 jit_solution(10791937156925419186)
XLA Ops:
  7.2 0.5 fusion.72
  8.5 0.6 fusion.75
  9.1 1.5 %multiply_convert_fusion.1 = (bf16[32,32,1024]{2,1,0:T(8,128)(2,1)S(1)}, bf16[32,32,1024]{2,1,0:T(8,128)(2,1)S(1)}) fusion(f32[32,1024]{1,0:T(8,128)S(1)} %get-tuple-element.43, f32[32,1024]{1,0:T(8,128)S(1)} %get-tuple-element.40, f32[32,1024]{1,0:T(8,128)S(1)} %get-tuple-element.44, f32[32,1024]{1,0:T(8,128)S(1)} %get-tuple-element.39), kind=kLoop, calls=%fused_computation.1 | loop fusion | flops 10485760 | bytes 4718592 | tf_op jit(solution)/shard_map/convert_element_type | solution.py:36
  10.6 0.5 fusion.70
  12.0 0.5 fusion
  12.6 0.5 fusion.1
  13.1 0.7 pad_maximum_fusion.1
  13.8 0.9 add_convert_fusion
  14.8 3.9 %collective-permute-start = (bf16[2,4,32,1024]{3,2,1,0:T(8,128)(2,1)}, bf16[2,4,32,1024]{3,2,1,0:T(8,128)(2,1)}, u32[]{:S(2)}, u32[]{:S(2)}) collective-permute-start(bf16[2,4,32,1024]{3,2,1,0:T(8,128)(2,1)} %add_convert_fusion), channel_id=1, source_target_pairs={{0,24},{8,0},{16,8},{24,16},{1,25},{9,1},{17,9},{25,17},{2,26},{10... | collective-permute-start | bytes 1572872 | tf_op jit(solution)/shard_map/ppermute | solution.py:137
  18.7 1.1 collective-permute-start.7
  19.8 0.7 pad_maximum_fusion.2
  20.5 2.4 %collective-permute-start.8 = (f32[2,4,8,1024]{3,2,1,0:T(8,128)}, f32[2,4,8,1024]{3,2,1,0:T(8,128)}, u32[]{:S(2)}, u32[]{:S(2)}) collective-permute-start(f32[2,4,8,1024]{3,2,1,0:T(8,128)} %pad_maximum_fusion.2), channel_id=1, source_target_pairs={{0,8},{8,16},{16,24},{24,0},{1,9},{9,17},{17,25},{25,1},{2,10},{10... | collective-permute-start | bytes 786440 | tf_op jit(solution)/shard_map/ppermute | solution.py:137
  22.9 0.5 collective-permute-start.9
  23.6 3.8 %fusion.11 = (f32[4,32,1024]{2,1,0:T(8,128)S(1)}, f32[4,32,1024]{2,1,0:T(8,128)S(1)}, f32[4,32,1024]{2,1,0:T(8,128)S(1)}, f32[4,32,1024]{2,1,0:T(8,128)S(1)}) fusion(f32[4,32,1024]{2,1,0:T(8,128)S(1)} %copy-done.13), kind=kLoop, calls=%fused_computation.42 | loop fusion | flops 1310720 | bytes 2621440 | tf_op jit(solution)/shard_map/sub | solution.py:245
  27.5 3.9 %collective-permute-done = bf16[2,4,32,1024]{3,2,1,0:T(8,128)(2,1)} collective-permute-done((bf16[2,4,32,1024]{3,2,1,0:T(8,128)(2,1)}, bf16[2,4,32,1024]{3,2,1,0:T(8,128)(2,1)}, u32[]{:S(2)}, u32[]{:S(2)}) %collective-permute-start) | collective-permute-done | bytes 524320 | tf_op jit(solution)/shard_map/ppermute | solution.py:137
  31.4 3.4 %collective-permute-start.10 = (f32[2,4,8,1024]{3,2,1,0:T(8,128)}, f32[2,4,8,1024]{3,2,1,0:T(8,128)}, u32[]{:S(2)}, u32[]{:S(2)}) collective-permute-start(f32[2,4,8,1024]{3,2,1,0:T(8,128)} %pad_maximum_fusion.2), channel_id=1, source_target_pairs={{0,24},{8,0},{16,8},{24,16},{1,25},{9,1},{17,9},{25,17},{2,26},{10... | collective-permute-start | bytes 786440 | tf_op jit(solution)/shard_map/ppermute | solution.py:137
  34.7 8.9 %collective-permute-done.1 = bf16[2,4,32,1024]{3,2,1,0:T(8,128)(2,1)} collective-permute-done((bf16[2,4,32,1024]{3,2,1,0:T(8,128)(2,1)}, bf16[2,4,32,1024]{3,2,1,0:T(8,128)(2,1)}, u32[]{:S(2)}, u32[]{:S(2)}) %collective-permute-start.1) | collective-permute-done | bytes 524320 | tf_op jit(solution)/shard_map/ppermute | solution.py:137
  43.6 1.2 %broadcast_select_fusion.1 = (bf16[2,4,32,1024]{3,2,1,0:T(8,128)(2,1)S(1)}, bf16[2,4,32,1024]{3,2,1,0:T(8,128)(2,1)S(1)}) fusion(pred[]{:T(512)S(6)} %eq.38, bf16[2,4,32,1024]{3,2,1,0:T(8,128)(2,1)} %collective-permute-done, bf16[2,4,32,1024]{3,2,1,0:T(8,128)(2,1)} %collective-permute-done.1, s32[2,4,32,1024]{3,2,1,0:T(8,128)S(1)} %copy-done.10), kind=kLoop, calls=%fused_computation.38 | loop fusion | flops 1572864 | bytes 3145729 | tf_op jit(solution)/shard_map/jit(_where)/select_n | solution.py:215
  44.9 0.5 convert_multiply_fusion
  45.4 1.5 %slice_bitcast_fusion = (f32[4,32,1024]{2,1,0:T(8,128)S(1)}, f32[4,32,1024]{2,1,0:T(8,128)S(1)}, f32[4,32,1024]{2,1,0:T(8,128)S(1)}, f32[4,32,1024]{2,1,0:T(8,12...) fusion(f32[4,4,32,1024]{3,2,1,0:T(8,128)S(1)} %get-tuple-element.22, ...), kind=kLoop, calls=%fused_computation.24 | loop fusion | bytes 8388608 | tf_op jit(solution)/shard_map/squeeze | solution.py:100
  46.9 1.0 copy-done.1
  48.0 1.0 copy-done.2
  49.0 1.0 copy-done.3
  50.1 1.0 copy-done.4
  51.1 1.0 copy-done.5
  52.2 15.4 %shard_map.93 = bf16[8,4,16,2048]{3,2,1,0:T(8,128)(2,1)} custom-call(bf16[32,16,2048]{2,1,0:T(8,128)(2,1)} %all-gather.2.cloned.1.call-done.s_ref, f32[4,32,1024]{2,1,0:T(8,128)S(1)} %get-tuple-element.28.refs_0_, f32[4,32,1024]{2,1,0:T(8,128)S(1)} %copy-done.2, f32[4,32,1024]{2,1,0:T(8,128)S(1)} %copy-done.3, f32[4,32,1024]{2,1,0:T(8,128)S(1)} %copy-done.4, ...), custom_call_target="tpu_custom_call" | custom-call | tf_op jit(solution)/shard_map/pallas_call | solution.py:101
  67.5 2.6 %fusion.3 = f32[512,1024]{1,0:T(8,128)S(1)} fusion(bf16[1024,1024]{1,0:T(8,128)(2,1)S(1)} %bitcast.180, bf16[512,2048]{1,0:T(8,128)(2,1)} %bitcast.182), kind=kOutput, calls=%fused_computation.18 | convolution fusion | flops 1073741824 | bytes 5242880 | tf_op jit(solution)/shard_map/dot_general | solution.py:255
  70.2 1.3 %fusion.7 = f32[512,1024]{1,0:T(8,128)S(1)} fusion(bf16[1024,1024]{1,0:T(8,128)(2,1)S(1)} %bitcast.176, bf16[512,2048]{1,0:T(8,128)(2,1)S(1)} %bitcast.183), kind=kOutput, calls=%fused_computation.22 | convolution fusion | flops 1073741824 | bytes 5242880 | tf_op jit(solution)/shard_map/dot_general | solution.py:255
  71.4 1.3 %fusion.5 = f32[512,1024]{1,0:T(8,128)S(1)} fusion(bf16[1024,1024]{1,0:T(8,128)(2,1)S(1)} %bitcast.181, bf16[512,2048]{1,0:T(8,128)(2,1)S(1)} %bitcast.184), kind=kOutput, calls=%fused_computation.20 | convolution fusion | flops 1073741824 | bytes 5242880 | tf_op jit(solution)/shard_map/dot_general | solution.py:258
  72.7 1.5 %fusion.99 = (f32[512]{0:T(512)S(1)}, f32[512,1024]{1,0:T(8,128)S(1)}) fusion(f32[512,1024]{1,0:T(8,128)S(1)} %fusion.5, bf16[1024,1024]{1,0:T(8,128)(2,1)S(1)} %bitcast.177, bf16[512,2048]{1,0:T(8,128)(2,1)S(1)} %bitcast.185, f32[512,1024]{1,0:T(8,128)S(1)} %fusion.7, f32[512,1024]{1,0:T(8,128)S(1)} %fusion.3), kind=kOutput, calls=%fused_computation.183 | convolution fusion | flops 1077411328 | bytes 11536384 | tf_op jit(solution)/shard_map/dot_general | solution.py:258
  74.4 0.6 exponential_reduce_fusion
  75.4 1.1 %collective-permute-done.2 = f32[3,8,16]{2,1,0:T(8,128)S(1)} collective-permute-done((f32[3,8,16]{2,1,0:T(8,128)S(1)}, f32[3,8,16]{2,1,0:T(8,128)S(1)}, u32[]{:S(2)}, u32[]{:S(2)}) %collective-permute-start.2) | collective-permute-done | bytes 1568 | tf_op jit(solution)/shard_map/ppermute | solution.py:165
  76.6 1.6 %collective-permute-start.3 = (f32[3,8,16]{2,1,0:T(8,128)S(1)}, f32[3,8,16]{2,1,0:T(8,128)S(1)}, u32[]{:S(2)}, u32[]{:S(2)}) collective-permute-start(f32[3,8,16]{2,1,0:T(8,128)S(1)} %pad_maximum_fusion.4), channel_id=1, source_target_pairs={{0,2},{1,3},{2,0},{3,1},{4,6},{5,7},{6,4},{7,5},{8,10},{9,11},{10,... | collective-permute-start | bytes 4616 | tf_op jit(solution)/shard_map/ppermute | solution.py:165
  78.2 2.1 %collective-permute-done.3 = f32[3,8,16]{2,1,0:T(8,128)S(1)} collective-permute-done((f32[3,8,16]{2,1,0:T(8,128)S(1)}, f32[3,8,16]{2,1,0:T(8,128)S(1)}, u32[]{:S(2)}, u32[]{:S(2)}) %collective-permute-start.3) | collective-permute-done | bytes 1568 | tf_op jit(solution)/shard_map/ppermute | solution.py:165
  80.4 2.7 %collective-permute-start.4 = (f32[3,8,16]{2,1,0:T(8,128)S(1)}, f32[3,8,16]{2,1,0:T(8,128)S(1)}, u32[]{:S(2)}, u32[]{:S(2)}) collective-permute-start(f32[3,8,16]{2,1,0:T(8,128)S(1)} %pad_maximum_fusion.5), channel_id=1, source_target_pairs={{0,4},{1,5},{2,6},{3,7},{4,0},{5,1},{6,2},{7,3},{8,12},{9,13},{10,... | collective-permute-start | bytes 4616 | tf_op jit(solution)/shard_map/ppermute | solution.py:165
  83.0 2.0 %collective-permute-done.4 = f32[3,8,16]{2,1,0:T(8,128)S(1)} collective-permute-done((f32[3,8,16]{2,1,0:T(8,128)S(1)}, f32[3,8,16]{2,1,0:T(8,128)S(1)}, u32[]{:S(2)}, u32[]{:S(2)}) %collective-permute-start.4) | collective-permute-done | bytes 1568 | tf_op jit(solution)/shard_map/ppermute | solution.py:165
  85.2 1.5 %collective-permute-start.5 = (f32[8]{0:T(128)S(1)}, f32[8]{0:T(128)S(1)}, u32[]{:S(2)}, u32[]{:S(2)}) collective-permute-start(f32[8]{0:T(128)S(1)} %fusion.78), channel_id=1, source_target_pairs={{0,8},{8,0},{16,24},{24,16},{1,9},{9,1},{17,25},{25,17},{2,10},{10... | collective-permute-start | bytes 104 | tf_op jit(solution)/shard_map/ppermute | solution.py:277
  86.7 2.1 %collective-permute-done.5 = f32[8]{0:T(128)S(1)} collective-permute-done((f32[8]{0:T(128)S(1)}, f32[8]{0:T(128)S(1)}, u32[]{:S(2)}, u32[]{:S(2)}) %collective-permute-start.5) | collective-permute-done | bytes 64 | tf_op jit(solution)/shard_map/ppermute | solution.py:277
  89.6 3.2 %collective-permute-done.6 = f32[8]{0:T(128)S(1)} collective-permute-done((f32[8]{0:T(128)S(1)}, f32[8]{0:T(128)S(1)}, u32[]{:S(2)}, u32[]{:S(2)}) %collective-permute-start.6) | collective-permute-done | bytes 64 | tf_op jit(solution)/shard_map/ppermute | solution.py:185
  93.1 1.3 %multiply_reduce_fusion.1 = f32[4,32,1024]{2,1,0:T(8,128)S(1)} fusion(bf16[2,4,32,1024]{3,2,1,0:T(8,128)(2,1)} %collective-permute-done.1, f32[2]{0:T(128)S(1)} %get-tuple-element.35), kind=kLoop, calls=%fused_computation.13 | loop fusion | flops 655360 | bytes 1048584 | tf_op jit(solution)/shard_map/reduce_sum | solution.py:122
  94.4 1.3 %multiply_reduce_fusion.2 = f32[4,32,1024]{2,1,0:T(8,128)S(1)} fusion(bf16[2,4,32,1024]{3,2,1,0:T(8,128)(2,1)} %collective-permute-done, f32[2]{0:T(128)S(1)} %get-tuple-element.37), kind=kLoop, calls=%fused_computation.14 | loop fusion | flops 655360 | bytes 1048584 | tf_op jit(solution)/shard_map/reduce_sum | solution.py:122
  95.9 1.3 %multiply_reduce_fusion = f32[4,32,1024]{2,1,0:T(8,128)S(1)} fusion(bf16[2,4,32,1024]{3,2,1,0:T(8,128)(2,1)} %collective-permute-done.7, f32[2]{0:T(128)S(1)} %get-tuple-element.36), kind=kLoop, calls=%fused_computation.12 | loop fusion | flops 655360 | bytes 1048584 | tf_op jit(solution)/shard_map/reduce_sum | solution.py:122
  97.5 0.8 fusion.19
  98.3 1.1 fusion.33
  99.4 1.1 fusion.40
  100.5 0.7 multiply_add_fusion
  101.2 1.1 fusion.47
  102.2 0.8 copy-done.15
  (77 shorter events, 4.2 us)
Async XLA Ops:
  7.2 1.0 copy-start
  7.2 39.8 %all-gather.2.cloned.1.call-start = ((), (), s32[]{:S(2)}) async-start(), calls=%async_computation | async-start | bytes 2359296 | tf_op jit(solution)/shard_map/all_gather | solution.py:235
  10.6 1.3 %copy-start.6 = (bf16[32,32,1024]{2,1,0:T(8,128)(2,1)}, bf16[32,32,1024]{2,1,0:T(8,128)(2,1)S(1)}, u32[]{:S(2)}) copy-start(bf16[32,32,1024]{2,1,0:T(8,128)(2,1)S(1)} %get-tuple-element.29) | copy-start | bytes 6291460
  10.6 1.9 %copy-start.8 = (bf16[32,32,1024]{2,1,0:T(8,128)(2,1)}, bf16[32,32,1024]{2,1,0:T(8,128)(2,1)S(1)}, u32[]{:S(2)}) copy-start(bf16[32,32,1024]{2,1,0:T(8,128)(2,1)S(1)} %get-tuple-element.30) | copy-start | bytes 6291460
  12.6 1.3 %copy-start.10 = (s32[2,4,32,1024]{3,2,1,0:T(8,128)S(1)}, s32[2,4,32,1024]{3,2,1,0:T(8,128)}, u32[]{:S(2)}) copy-start(s32[2,4,32,1024]{3,2,1,0:T(8,128)} %param.9) | copy-start | bytes 3145732
  12.6 7.2 %copy-start.17 = (f32[4,8,1024]{2,1,0:T(8,128)S(1)}, f32[4,8,1024]{2,1,0:T(8,128)}, u32[]{:S(2)}) copy-start(f32[4,8,1024]{2,1,0:T(8,128)} %param.10) | copy-start | bytes 393220
  12.6 7.2 %copy-start.19 = (f32[4,8,1024]{2,1,0:T(8,128)S(1)}, f32[4,8,1024]{2,1,0:T(8,128)}, u32[]{:S(2)}) copy-start(f32[4,8,1024]{2,1,0:T(8,128)} %param.11) | copy-start | bytes 393220
  13.1 10.4 %copy-start.20 = (s32[32]{0:T(128)S(1)}, s32[32]{0:T(128)}, u32[]{:S(2)}) copy-start(s32[32]{0:T(128)} %param.7) | copy-start | bytes 388
  13.1 10.5 %copy-start.13 = (f32[4,32,1024]{2,1,0:T(8,128)S(1)}, f32[4,32,1024]{2,1,0:T(8,128)}, u32[]{:S(2)}) copy-start(f32[4,32,1024]{2,1,0:T(8,128)} %param.8) | copy-start | bytes 1572868
  14.8 16.6 %collective-permute-start = (bf16[2,4,32,1024]{3,2,1,0:T(8,128)(2,1)}, bf16[2,4,32,1024]{3,2,1,0:T(8,128)(2,1)}, u32[]{:S(2)}, u32[]{:S(2)}) collective-permute-start(bf16[2,4,32,1024]{3,2,1,0:T(8,128)(2,1)} %add_convert_fusion), channel_id=1, source_target_pairs={{0,24},{8,0},{16,8},{24,16},{1,25},{9,1},{17,9},{25,17},{2,26},{10... | collective-permute-start | bytes 1572872 | tf_op jit(solution)/shard_map/ppermute | solution.py:137
  18.7 25.0 %collective-permute-start.1 = (bf16[2,4,32,1024]{3,2,1,0:T(8,128)(2,1)}, bf16[2,4,32,1024]{3,2,1,0:T(8,128)(2,1)}, u32[]{:S(2)}, u32[]{:S(2)}) collective-permute-start(bf16[2,4,32,1024]{3,2,1,0:T(8,128)(2,1)} %add_convert_fusion), channel_id=1, source_target_pairs={{0,8},{8,16},{16,24},{24,0},{1,9},{9,17},{17,25},{25,1},{2,10},{10... | collective-permute-start | bytes 1572872 | tf_op jit(solution)/shard_map/ppermute | solution.py:137
  18.7 77.2 %collective-permute-start.7 = (bf16[2,4,32,1024]{3,2,1,0:T(8,128)(2,1)}, bf16[2,4,32,1024]{3,2,1,0:T(8,128)(2,1)}, u32[]{:S(2)}, u32[]{:S(2)}) collective-permute-start(bf16[2,4,32,1024]{3,2,1,0:T(8,128)(2,1)} %add_convert_fusion), channel_id=1, source_target_pairs={{0,16},{8,24},{16,0},{24,8},{1,17},{9,25},{17,1},{25,9},{2,18},{10... | collective-permute-start | bytes 1572872 | tf_op jit(solution)/shard_map/ppermute | solution.py:137
  20.5 77.7 %collective-permute-start.8 = (f32[2,4,8,1024]{3,2,1,0:T(8,128)}, f32[2,4,8,1024]{3,2,1,0:T(8,128)}, u32[]{:S(2)}, u32[]{:S(2)}) collective-permute-start(f32[2,4,8,1024]{3,2,1,0:T(8,128)} %pad_maximum_fusion.2), channel_id=1, source_target_pairs={{0,8},{8,16},{16,24},{24,0},{1,9},{9,17},{17,25},{25,1},{2,10},{10... | collective-permute-start | bytes 786440 | tf_op jit(solution)/shard_map/ppermute | solution.py:137
  22.9 76.5 %collective-permute-start.9 = (f32[2,4,8,1024]{3,2,1,0:T(8,128)}, f32[2,4,8,1024]{3,2,1,0:T(8,128)}, u32[]{:S(2)}, u32[]{:S(2)}) collective-permute-start(f32[2,4,8,1024]{3,2,1,0:T(8,128)} %pad_maximum_fusion.2), channel_id=1, source_target_pairs={{0,16},{8,24},{16,0},{24,8},{1,17},{9,25},{17,1},{25,9},{2,18},{10... | collective-permute-start | bytes 786440 | tf_op jit(solution)/shard_map/ppermute | solution.py:137
  31.4 69.8 %collective-permute-start.10 = (f32[2,4,8,1024]{3,2,1,0:T(8,128)}, f32[2,4,8,1024]{3,2,1,0:T(8,128)}, u32[]{:S(2)}, u32[]{:S(2)}) collective-permute-start(f32[2,4,8,1024]{3,2,1,0:T(8,128)} %pad_maximum_fusion.2), channel_id=1, source_target_pairs={{0,24},{8,0},{16,8},{24,16},{1,25},{9,1},{17,9},{25,17},{2,26},{10... | collective-permute-start | bytes 786440 | tf_op jit(solution)/shard_map/ppermute | solution.py:137
  46.9 1.0 copy-start.1
  48.0 1.0 copy-start.2
  49.0 1.0 copy-start.3
  50.1 1.0 copy-start.4
  51.1 1.0 copy-start.5
  52.2 15.4 %copy-start.9 = (bf16[32,32,1024]{2,1,0:T(8,128)(2,1)S(1)}, bf16[32,32,1024]{2,1,0:T(8,128)(2,1)}, u32[]{:S(2)}) copy-start(bf16[32,32,1024]{2,1,0:T(8,128)(2,1)} %copy-done.8) | copy-start | bytes 6291460
  67.5 2.6 %copy-start.7 = (bf16[32,32,1024]{2,1,0:T(8,128)(2,1)S(1)}, bf16[32,32,1024]{2,1,0:T(8,128)(2,1)}, u32[]{:S(2)}) copy-start(bf16[32,32,1024]{2,1,0:T(8,128)(2,1)} %copy-done.6) | copy-start | bytes 6291460
  67.5 2.6 %copy-start.12 = (bf16[8,4,16,2048]{3,2,1,0:T(8,128)(2,1)S(1)}, bf16[8,4,16,2048]{3,2,1,0:T(8,128)(2,1)}, u32[]{:S(2)}) copy-start(bf16[8,4,16,2048]{3,2,1,0:T(8,128)(2,1)} %shard_map.93) | copy-start | bytes 6291460
  75.1 20.6 %copy-start.11 = (s32[2,4,32,1024]{3,2,1,0:T(8,128)S(1)}, s32[2,4,32,1024]{3,2,1,0:T(8,128)}, u32[]{:S(2)}) copy-start(s32[2,4,32,1024]{3,2,1,0:T(8,128)} %param.9) | copy-start | bytes 3145732
  75.3 1.2 %collective-permute-start.2 = (f32[3,8,16]{2,1,0:T(8,128)S(1)}, f32[3,8,16]{2,1,0:T(8,128)S(1)}, u32[]{:S(2)}, u32[]{:S(2)}) collective-permute-start(f32[3,8,16]{2,1,0:T(8,128)S(1)} %pad_maximum_fusion.3), channel_id=1, source_target_pairs={{0,1},{1,0},{2,3},{3,2},{4,5},{5,4},{6,7},{7,6},{8,9},{9,8},{10,11... | collective-permute-start | bytes 4616 | tf_op jit(solution)/shard_map/ppermute | solution.py:165
  76.6 3.8 %collective-permute-start.3 = (f32[3,8,16]{2,1,0:T(8,128)S(1)}, f32[3,8,16]{2,1,0:T(8,128)S(1)}, u32[]{:S(2)}, u32[]{:S(2)}) collective-permute-start(f32[3,8,16]{2,1,0:T(8,128)S(1)} %pad_maximum_fusion.4), channel_id=1, source_target_pairs={{0,2},{1,3},{2,0},{3,1},{4,6},{5,7},{6,4},{7,5},{8,10},{9,11},{10,... | collective-permute-start | bytes 4616 | tf_op jit(solution)/shard_map/ppermute | solution.py:165
  80.4 4.7 %collective-permute-start.4 = (f32[3,8,16]{2,1,0:T(8,128)S(1)}, f32[3,8,16]{2,1,0:T(8,128)S(1)}, u32[]{:S(2)}, u32[]{:S(2)}) collective-permute-start(f32[3,8,16]{2,1,0:T(8,128)S(1)} %pad_maximum_fusion.5), channel_id=1, source_target_pairs={{0,4},{1,5},{2,6},{3,7},{4,0},{5,1},{6,2},{7,3},{8,12},{9,13},{10,... | collective-permute-start | bytes 4616 | tf_op jit(solution)/shard_map/ppermute | solution.py:165
  85.2 3.6 %collective-permute-start.5 = (f32[8]{0:T(128)S(1)}, f32[8]{0:T(128)S(1)}, u32[]{:S(2)}, u32[]{:S(2)}) collective-permute-start(f32[8]{0:T(128)S(1)} %fusion.78), channel_id=1, source_target_pairs={{0,8},{8,0},{16,24},{24,16},{1,9},{9,1},{17,25},{25,17},{2,10},{10... | collective-permute-start | bytes 104 | tf_op jit(solution)/shard_map/ppermute | solution.py:277
  89.3 3.6 %collective-permute-start.6 = (f32[8]{0:T(128)S(1)}, f32[8]{0:T(128)S(1)}, u32[]{:S(2)}, u32[]{:S(2)}) collective-permute-start(f32[8]{0:T(128)S(1)} %dynamic_update_slice.17), channel_id=1, source_target_pairs={{0,16},{8,24},{16,0},{24,8},{1,17},{9,25},{17,1},{25,9},{2,18},{10... | collective-permute-start | bytes 104 | tf_op jit(solution)/shard_map/ppermute | solution.py:185
  95.9 1.6 %copy-start.16 = (f32[4,32,1024]{2,1,0:T(8,128)S(1)}, f32[4,32,1024]{2,1,0:T(8,128)}, u32[]{:S(2)}) copy-start(f32[4,32,1024]{2,1,0:T(8,128)} %param.8) | copy-start | bytes 1572868
  97.2 1.0 copy-start.14
  98.2 4.0 %copy-start.18 = (f32[4,8,1024]{2,1,0:T(8,128)}, f32[4,8,1024]{2,1,0:T(8,128)S(1)}, u32[]{:S(2)}) copy-start(f32[4,8,1024]{2,1,0:T(8,128)S(1)} %get-tuple-element.9) | copy-start | bytes 393220
  102.2 0.8 copy-start.15
Sparse Core Ops, SparseCore 0:
  14.0 31.7 all-gather.1
